TPU v7x, 512 devices: a whole 4x8x8 slice. The times are simulated.
512 devices in a mesh: dp: 16 (over z, core), expert: 32 (over x, y).
Axes of the slice: x: 4, y: 8, z: 8, core: 2. Of those that a mesh axis runs over, the one named last changes fastest.
Arguments:
- tokens: bfloat16 [65536, 1024], P(('dp', 'expert')), may hold values from -6 to 6
- expert_ids: int32 [65536, 8], P(('dp', 'expert')), may hold values from 0 to 63, all different within a row; in each aligned block of 128 rows (0 to 127, 128 to 255, ...) at most 17 rows name the same one
- gate_values: float32 [65536, 8], P(('dp', 'expert')), may hold values from 0.05 to 0.5
- w_gate: bfloat16 [64, 1024, 384], P('expert', 'dp'), may hold values from -0.1875 to 0.1875
- w_up: bfloat16 [64, 1024, 384], P('expert', 'dp'), may hold values from -0.1875 to 0.1875
- w_down: bfloat16 [64, 384, 1024], P('expert', 'dp'), may hold values from -0.3125 to 0.3125
- partner: int32 [512], replicated, may hold values from 0 to 511, as said below
Outputs:
- contrast_loss: float32 [], replicated
- token_grad: bfloat16 [65536, 1024], P(('dp', 'expert'))
- gate_grad: float32 [65536, 8], P(('dp', 'expert'))
Inputs may be any that keep to these rules, and one draw needn't show every extreme that they name: `expert_ids`: each row names 8 different experts. Among the 128 rows of one sequence no expert is named more than 17 times, and in every draw some sequence names some expert exactly 17 times. partner[i] differs from i.
All inputs are finite; a program needn't handle non-finite values.
Results may differ from a plain program's by a relative error of at most 0.014.
Values may be sent and summed in bfloat16 or wider, within the bound.
No kernel may reach another device: no remote copies, remote signals or barrier semaphores. Data moves between devices by JAX's collectives and lax.ppermute only.
A program may use at most 64 MiB of HBM per device.

v0:
```python
import jax
import jax.numpy as jnp
from jax import lax
from jax.sharding import PartitionSpec as P

score_scale = 20.0
highest = lax.Precision.HIGHEST


def silu_parts(pre_act):
    sigmoid_val = jax.nn.sigmoid(pre_act)
    return (pre_act * sigmoid_val, sigmoid_val * (1.0 + pre_act * (1.0 - sigmoid_val)))


def expert_forward(slot_piece, gate_full, up_full, down_full):
    pre_gate = jnp.einsum(
        "encd,edf->encf", slot_piece, gate_full, preferred_element_type=jnp.float32
    )
    pre_up = jnp.einsum("encd,edf->encf", slot_piece, up_full, preferred_element_type=jnp.float32)
    activated, derivative = silu_parts(pre_gate)
    hidden = (activated * pre_up).astype(jnp.bfloat16)
    expert_out = jnp.einsum(
        "encf,efd->encd", hidden, down_full, preferred_element_type=jnp.float32
    ).astype(jnp.bfloat16)
    return (expert_out, pre_gate, pre_up)


def on_device(tokens, expert_ids, gate_values, w_gate, w_up, w_down, partner):
    tok_rows, model_width = tokens.shape
    route_count = expert_ids.shape[1]
    local_experts = w_gate.shape[0]
    experts = lax.axis_size("expert") * local_experts
    capacity = tok_rows * route_count // experts + max(1, tok_rows * route_count // (16 * experts))
    slot_total = experts * capacity
    gate_full, up_full, down_full = (
        lax.all_gather(w_gate, "dp", axis=1, tiled=True),
        lax.all_gather(w_up, "dp", axis=1, tiled=True),
        lax.all_gather(w_down, "dp", axis=1, tiled=True),
    )
    expert_iota = jnp.arange(experts, dtype=jnp.int32)
    matches = expert_ids[:, :, None] == expert_iota
    chosen = jnp.sum(matches.astype(jnp.int32), axis=1, dtype=jnp.int32)
    chosen_gate = jnp.sum(jnp.where(matches, gate_values[:, :, None], 0.0), axis=1)
    before = jnp.cumsum(chosen, axis=0, dtype=jnp.int32) - chosen
    slot_rank = jnp.take_along_axis(before, expert_ids, axis=1)
    slot_row = (expert_ids * capacity + slot_rank).reshape(-1)
    slot_iota = jnp.arange(capacity, dtype=jnp.int32)
    onehot = (chosen.T[:, None, :] == 1) & (before.T[:, None, :] == slot_iota[None, :, None])
    placer = onehot.astype(jnp.bfloat16)
    slot_gate = jnp.sum(jnp.where(onehot, chosen_gate.T[:, None, :], 0.0), axis=2)
    outgoing = jnp.einsum("ect,td->ecd", placer, tokens, preferred_element_type=jnp.float32).astype(
        jnp.bfloat16
    )
    outgoing = outgoing.reshape(experts, 1, capacity, model_width)
    placer_flat = placer.reshape(slot_total, tok_rows)
    out_here, pre_gate, pre_up = expert_forward(
        lax.all_to_all(outgoing, "expert", split_axis=0, concat_axis=1, tiled=True),
        gate_full,
        up_full,
        down_full,
    )
    returned_out = lax.all_to_all(
        out_here, "expert", split_axis=1, concat_axis=0, tiled=True
    ).reshape(slot_total, model_width)
    weighted_sum = jnp.dot(
        slot_gate.reshape(slot_total), returned_out.astype(jnp.float32), precision=highest
    )
    pooled = jnp.mean(tokens.astype(jnp.float32), axis=0) + weighted_sum / tok_rows
    inv_rms = lax.rsqrt(jnp.mean(pooled * pooled) + 1e-06)
    embedding = (pooled * inv_rms).astype(jnp.bfloat16)[None, :]
    gathered = lax.all_gather(embedding, ("dp", "expert"), axis=0, tiled=True)
    batch_size = gathered.shape[0]
    own_index = lax.axis_index(("dp", "expert"))
    batch_iota = jnp.arange(batch_size, dtype=jnp.int32)
    scores = (
        score_scale
        / model_width
        * jnp.dot(gathered, embedding[0], preferred_element_type=jnp.float32)
    )
    others = batch_iota != own_index
    log_total = jnp.log(jnp.sum(jnp.where(others, jnp.exp(scores), 0.0)))
    own_partner = lax.dynamic_index_in_dim(partner, own_index, keepdims=False)
    partner_hit = (batch_iota == own_partner).astype(jnp.float32)
    weight = jnp.where(others, jnp.exp(scores - log_total), 0.0) - partner_hit
    all_embed = gathered.astype(jnp.float32)
    row_term = jnp.dot(weight, all_embed, precision=highest)
    all_totals = lax.all_gather(log_total[None], ("dp", "expert"), axis=0, tiled=True)
    column_weight = jnp.where(others, jnp.exp(scores - all_totals), 0.0) - (
        partner == own_index
    ).astype(jnp.float32)
    embed_grad = (
        score_scale
        / model_width
        * (row_term + jnp.dot(column_weight, all_embed, precision=highest))
    )
    partner_rows = jnp.take(gathered, partner, axis=0)
    partner_score = (
        score_scale
        / model_width
        * jnp.einsum("bd,bd->b", gathered, partner_rows, preferred_element_type=jnp.float32)
    )
    contrast_loss = jnp.mean(all_totals - partner_score)
    seq_grad = (
        inv_rms * embed_grad - inv_rms**3 * jnp.sum(pooled * embed_grad) / model_width * pooled
    )
    slot_dots = jnp.dot(returned_out.astype(jnp.float32), seq_grad, precision=highest)
    gate_grad = jnp.take(slot_dots, slot_row, axis=0).reshape(tok_rows, route_count)
    out_grad = (
        (slot_gate[:, :, None] * seq_grad)
        .astype(jnp.bfloat16)
        .reshape(experts, 1, capacity, model_width)
    )
    arrived = lax.all_to_all(out_grad, "expert", split_axis=0, concat_axis=1, tiled=True)
    hidden_grad = jnp.einsum(
        "encd,efd->encf", arrived, down_full, preferred_element_type=jnp.float32
    )
    activated, derivative = silu_parts(pre_gate)
    gate_side = (hidden_grad * pre_up * derivative).astype(jnp.bfloat16)
    up_side = (hidden_grad * activated).astype(jnp.bfloat16)
    route_here = jnp.einsum(
        "encf,edf->encd", gate_side, gate_full, preferred_element_type=jnp.float32
    )
    route_here = (
        route_here
        + jnp.einsum("encf,edf->encd", up_side, up_full, preferred_element_type=jnp.float32)
    ).astype(jnp.bfloat16)
    returned = lax.all_to_all(
        route_here, "expert", split_axis=1, concat_axis=0, tiled=True
    ).reshape(slot_total, model_width)
    route_sum = jnp.einsum("st,sd->td", placer_flat, returned, preferred_element_type=jnp.float32)
    token_grad = (seq_grad + route_sum).astype(jnp.bfloat16)
    return (contrast_loss, token_grad, gate_grad)


def solution(mesh):
    placed = (
        P(("dp", "expert"), None),
        P(("dp", "expert"), None),
        P(("dp", "expert"), None),
        P("expert", "dp", None),
        P("expert", "dp", None),
        P("expert", "dp", None),
        P(),
    )
    return jax.shard_map(
        on_device,
        mesh=mesh,
        in_specs=placed,
        out_specs=(P(), P(("dp", "expert"), None), P(("dp", "expert"), None)),
        check_vma=False,
    )
```

profile of v0, /device:TPU:1, one launch (start us, length us, event | category | flops | bytes accessed | tf_op | source)
XLA Modules:
  0.0 603.2 jit_solution(16274606224665401877)
XLA Ops:
  7.2 0.7 all-gather.6.cloned.1.call-update
  7.9 0.7 all-gather.8.cloned.1.call-update
  8.6 0.7 convert_reduce_fusion.1
  9.9 1.7 convert_bitcast_fusion
  11.6 3.0 copy.118
  14.7 10.5 %all-to-all-start = ((bf16[64,1,17,1024]{3,2,1,0:T(8,128)(2,1)}), bf16[64,1,17,1024]{3,2,1,0:T(8,128)(2,1)S(1)}, u32[]{:S(2)}, u32[]{:S(2)}) async-start(bf16[64,1,17,1024]{3,2,1,0:T(8,128)(2,1)} %copy.118), calls=%async_computation | async-start | bytes 6291456 | tf_op jit(solution)/shard_map/all_to_all | solution.py:57
  25.2 0.7 all-gather.10.cloned.1.call-update
  25.9 32.5 %all-gather.6.cloned.1.call-done = bf16[2,1024,384]{2,1,0:T(8,128)(2,1)} async-done(((bf16[2,64,384]{2,1,0:T(8,128)(2,1)}), bf16[2,1024,384]{2,1,0:T(8,128)(2,1)}) %all-gather.6.cloned.1.call-update) | async-done | bytes 1572880 | tf_op jit(solution)/shard_map/all_gather | solution.py:36
  58.4 38.2 %all-to-all-done = bf16[64,1,17,1024]{3,2,1,0:T(8,128)(2,1)S(1)} async-done(((bf16[64,1,17,1024]{3,2,1,0:T(8,128)(2,1)}), bf16[64,1,17,1024]{3,2,1,0:T(8,128)(2,1)S(1)}, u32[]{:S(2)}, u32[]{:S(2)}) %all-to-all-start) | async-done | bytes 2228256 | tf_op jit(solution)/shard_map/all_to_all | solution.py:57
  96.7 4.3 fusion.5
  101.2 4.2 fusion.3
  105.5 38.8 %all-gather.10.cloned.1.call-done = bf16[2,384,1024]{2,1,0:T(8,128)(2,1)} async-done(((bf16[2,24,1024]{2,1,0:T(8,128)(2,1)}), bf16[2,384,1024]{2,1,0:T(8,128)(2,1)}) %all-gather.10.cloned.1.call-update) | async-done | bytes 1572880 | tf_op jit(solution)/shard_map/all_gather | solution.py:38
  144.2 3.7 convolution_convert_fusion
  148.0 3.7 copy.121
  151.7 9.3 %all-to-all-start.1 = ((bf16[2,32,17,1024]{3,0,2,1:T(2,128)(2,1)}), bf16[2,32,17,1024]{3,0,2,1:T(2,128)(2,1)S(1)}, u32[]{:S(2)}, u32[]{:S(2)}) async-start(bf16[2,32,17,1024]{3,0,2,1:T(2,128)(2,1)} %copy.121), calls=%async_computation.1 | async-start | bytes 4456448 | tf_op jit(solution)/shard_map/all_to_all | solution.py:62
  161.9 50.5 %all-to-all-done.1 = bf16[2,32,17,1024]{3,0,2,1:T(2,128)(2,1)S(1)} async-done(((bf16[2,32,17,1024]{3,0,2,1:T(2,128)(2,1)}), bf16[2,32,17,1024]{3,0,2,1:T(2,128)(2,1)S(1)}, u32[]{:S(2)}, u32[]{:S(2)}) %all-to-all-start.1) | async-done | bytes 2228256 | tf_op jit(solution)/shard_map/all_to_all | solution.py:62
  212.4 2.7 copy.122
  215.1 3.0 reshape.128
  218.1 1.0 fusion.28
  219.1 0.6 multiply_reduce_fusion.1
  221.0 0.6 dynamic_slice.4
  222.8 1.3 reshape.169
  224.0 105.4 %all-gather.12.cloned.1.call-done = bf16[524288]{0:T(1024)(128)(2,1)} async-done(((bf16[1024]{0:T(1024)(128)(2,1)}), bf16[524288]{0:T(1024)(128)(2,1)}) %all-gather.12.cloned.1.call-update) | async-done | bytes 1048592 | tf_op jit(solution)/shard_map/all_gather | solution.py:71
  329.5 1.5 reshape.154
  331.0 1.1 fusion.29
  332.0 0.6 select_reduce_fusion.2
  333.9 1.4 dynamic-update-slice
  335.3 97.8 %all-reduce = f32[512]{0:T(512)} all-reduce(f32[512]{0:T(512)} %dynamic-update-slice), channel_id=1, replica_groups=mesh['dp'=16,'expert'=32] {'dp','expert'}, use_global_device_ids=true, to_apply=%add | all-reduce | flops 512 | bytes 4096
  433.1 2.9 gather_fusion
  436.0 1.8 fusion.7
  437.8 1.4 convert_subtract_fusion
  440.2 0.6 multiply_reduce_fusion
  441.5 0.7 multiply_subtract_fusion
  442.2 1.2 multiply_convert_fusion
  443.3 75.5 %all_to_all.66 = bf16[64,1,17,1024]{3,2,1,0:T(8,128)(2,1)S(1)} all-to-all(bf16[64,1,17,1024]{3,2,1,0:T(8,128)(2,1)S(1)} %multiply_convert_fusion), channel_id=1, replica_groups=mesh['dp'=16,'expert'=32] {'expert'}, dimensions={0} | all-to-all | bytes 4456448 | tf_op jit(solution)/shard_map/all_to_all | solution.py:113
  518.9 1.7 fusion
  521.3 1.5 fusion.11
  522.8 1.4 add_convert_fusion
  524.2 3.7 copy.125
  527.9 8.7 %all-to-all-start.3 = ((bf16[2,32,17,1024]{3,0,2,1:T(2,128)(2,1)}), bf16[2,32,17,1024]{3,0,2,1:T(2,128)(2,1)}, u32[]{:S(2)}, u32[]{:S(2)}) async-start(bf16[2,32,17,1024]{3,0,2,1:T(2,128)(2,1)} %copy.125), calls=%async_computation.3 | async-start | bytes 4456448 | tf_op jit(solution)/shard_map/all_to_all | solution.py:127
  536.6 0.8 and.41
  537.6 7.1 %gather_fusion.2 = s32[1024]{0:T(1024)S(1)} fusion(s32[128,64]{1,0:T(8,128)S(1)} %sub.31, s32[1024]{0:T(1024)S(1)} %reshape.148), kind=kCustom, calls=%fused_computation.2 | custom fusion | bytes 16384 | tf_op jit(solution)/shard_map/jit(take_along_axis)/gather | solution.py:45
  545.0 1.8 convolution_reduce_fusion
  546.9 6.2 %gather_fusion.1 = f32[1024]{0:T(1024)S(1)} fusion(f32[1088]{0:T(1024)S(1)} %convolution_reduce_fusion, s32[1024]{0:T(1024)S(1)} %broadcast_clamp_fusion), kind=kCustom, calls=%fused_computation.1 | custom fusion | bytes 12288 | tf_op jit(solution)/shard_map/jit(_take)/gather | solution.py:107
  554.5 33.3 %all-to-all-done.3 = bf16[2,32,17,1024]{3,0,2,1:T(2,128)(2,1)} async-done(((bf16[2,32,17,1024]{3,0,2,1:T(2,128)(2,1)}), bf16[2,32,17,1024]{3,0,2,1:T(2,128)(2,1)}, u32[]{:S(2)}, u32[]{:S(2)}) %all-to-all-start.3) | async-done | bytes 2228256 | tf_op jit(solution)/shard_map/all_to_all | solution.py:127
  587.8 2.5 copy.126
  590.4 2.3 reshape.129
  592.7 2.9 fusion.18
  (62 shorter events, 7.0 us)
Async XLA Ops:
  7.2 51.3 %all-gather.6.cloned.1.call-start = ((), (), s32[]{:S(2)}) async-start(), calls=%async_computation.4 | async-start | bytes 1671168 | tf_op jit(solution)/shard_map/all_gather | solution.py:36
  7.9 93.3 %all-gather.8.cloned.1.call-start = ((), (), s32[]{:S(2)}) async-start(), calls=%async_computation.5 | async-start | bytes 1671168 | tf_op jit(solution)/shard_map/all_gather | solution.py:37
  14.7 82.0 %all-to-all-start = ((bf16[64,1,17,1024]{3,2,1,0:T(8,128)(2,1)}), bf16[64,1,17,1024]{3,2,1,0:T(8,128)(2,1)S(1)}, u32[]{:S(2)}, u32[]{:S(2)}) async-start(bf16[64,1,17,1024]{3,2,1,0:T(8,128)(2,1)} %copy.118), calls=%async_computation | async-start | bytes 6291456 | tf_op jit(solution)/shard_map/all_to_all | solution.py:57
  25.2 119.0 %all-gather.10.cloned.1.call-start = ((), (), s32[]{:S(2)}) async-start(), calls=%async_computation.6 | async-start | bytes 1671168 | tf_op jit(solution)/shard_map/all_gather | solution.py:38
  151.7 9.6 %copy-start.3 = (s32[128,8]{0,1:T(8,128)S(1)}, s32[128,8]{0,1:T(8,128)}, u32[]{:S(2)}) copy-start(s32[128,8]{0,1:T(8,128)} %param.8) | copy-start | bytes 12292
  151.7 9.6 %copy-start.7 = (f32[128,8]{0,1:T(8,128)S(1)}, f32[128,8]{0,1:T(8,128)}, u32[]{:S(2)}) copy-start(f32[128,8]{0,1:T(8,128)} %param.9) | copy-start | bytes 12292
  151.7 10.1 %copy-start = (bf16[128,1024]{1,0:T(8,128)(2,1)S(1)}, bf16[128,1024]{1,0:T(8,128)(2,1)}, u32[]{:S(2)}) copy-start(bf16[128,1024]{1,0:T(8,128)(2,1)} %param.7) | copy-start | bytes 786436
  151.7 60.7 %all-to-all-start.1 = ((bf16[2,32,17,1024]{3,0,2,1:T(2,128)(2,1)}), bf16[2,32,17,1024]{3,0,2,1:T(2,128)(2,1)S(1)}, u32[]{:S(2)}, u32[]{:S(2)}) async-start(bf16[2,32,17,1024]{3,0,2,1:T(2,128)(2,1)} %copy.121), calls=%async_computation.1 | async-start | bytes 4456448 | tf_op jit(solution)/shard_map/all_to_all | solution.py:62
  161.1 168.4 %all-gather.12.cloned.1.call-start = ((), (), s32[]{:S(2)}) async-start(), calls=%async_computation.7 | async-start | bytes 1050624 | tf_op jit(solution)/shard_map/all_gather | solution.py:71
  161.7 53.4 %copy-start.2 = (f32[64,17]{1,0:T(8,128)}, f32[64,17]{1,0:T(8,128)S(1)}, u32[]{:S(2)}) copy-start(f32[64,17]{1,0:T(8,128)S(1)} %select_reduce_fusion) | copy-start | bytes 13060
  218.1 2.9 copy-start.5
  436.0 1.8 copy-start.6
  440.2 1.3 copy-start.4
  443.3 75.5 %copy-start.10 = (bf16[2,384,1024]{2,1,0:T(8,128)(2,1)S(1)}, bf16[2,384,1024]{2,1,0:T(8,128)(2,1)}, u32[]{:S(2)}) copy-start(bf16[2,384,1024]{2,1,0:T(8,128)(2,1)} %all-gather.10.cloned.1.call-done) | copy-start | bytes 4718596
  518.9 1.8 copy-start.8
  518.9 1.9 copy-start.11
  518.9 2.4 copy-start.12
  521.3 1.5 copy-start.9
  527.9 59.9 %all-to-all-start.3 = ((bf16[2,32,17,1024]{3,0,2,1:T(2,128)(2,1)}), bf16[2,32,17,1024]{3,0,2,1:T(2,128)(2,1)}, u32[]{:S(2)}, u32[]{:S(2)}) async-start(bf16[2,32,17,1024]{3,0,2,1:T(2,128)(2,1)} %copy.125), calls=%async_computation.3 | async-start | bytes 4456448 | tf_op jit(solution)/shard_map/all_to_all | solution.py:127
  590.4 2.3 copy-start.1
Sparse Core Ops, SparseCore 0:
  10.1 48.2 all-gather.5
  60.6 40.5 all-gather.7
  103.4 40.8 all-gather.9
  221.1 108.3 all-gather.11
where the time goes:
time: 605 us; the launch traced here: 603 us
  waiting for transfers between devices  301 us (50%)
  blocking collectives  173 us (29%)
  local copies, waits for them, and re-layouts  44.9 us (7%)
  starting transfers between devices  28.9 us (5%)
  matrix products  26.4 us (4%)
  between operations  18 us (3%)
  other arithmetic  10.6 us (2%)
    all_gather x1, waiting for transfers between devices, on_device(): gathered = lax.all_gather(embedding, ('dp', 'expert'), axis=0, tiled=True)  105 us
    unnamed x1, blocking collectives  97.8 us
    all_to_all x1, blocking collectives, on_device(): lax.all_to_all(out_grad, 'expert', split_axis=0, concat_axis=1, tiled=True)  75.5 us
    all_to_all x1, waiting for transfers between devices, on_device(): lax.all_to_all(out_here, 'expert', split_axis=1, concat_axis=0, tiled=True)  50.5 us
    all_gather x1, waiting for transfers between devices, on_device(): lax.all_gather(w_down, 'dp', axis=1, tiled=True)  38.8 us
    all_to_all x1, waiting for transfers between devices, on_device(): lax.all_to_all(outgoing, 'expert', split_axis=0, concat_axis=1, tiled=True)  38.2 us
    all_to_all x1, waiting for transfers between devices, on_device(): lax.all_to_all(route_here, 'expert', split_axis=1, concat_axis=0, tiled=T...  33.3 us
    all_gather x1, waiting for transfers between devices, on_device(): lax.all_gather(w_gate, 'dp', axis=1, tiled=True)  32.5 us
  transfers between devices with their start and end apart: 7, of which 7 were waited for; matrix products, arithmetic and copies ran while one was open for 6% of the time, Pallas kernels for 0%

commit v1 on v0

v1 whole, which is shorter than its diff:
```python
import jax
import jax.numpy as jnp
from jax import lax
from jax.sharding import PartitionSpec as P

score_scale = 20.0
highest = lax.Precision.HIGHEST
f32 = jnp.float32
bf16 = jnp.bfloat16


def silu_parts(pre_act):
    sigmoid_val = jax.nn.sigmoid(pre_act)
    return (pre_act * sigmoid_val, sigmoid_val * (1.0 + pre_act * (1.0 - sigmoid_val)))


def split3(x):
    hi = lax.reduce_precision(x, exponent_bits=8, mantissa_bits=7)
    rest = x - hi
    mid = lax.reduce_precision(rest, exponent_bits=8, mantissa_bits=7)
    lo = rest - mid
    return jnp.concatenate([hi, mid, lo], axis=-1).astype(bf16)


def join3(packed, n):
    hi = packed[..., :n].astype(f32)
    mid = packed[..., n : 2 * n].astype(f32)
    lo = packed[..., 2 * n : 3 * n].astype(f32)
    return hi + (mid + lo)


def pack_row(values, width):
    pieces = split3(values)
    pad = width - pieces.shape[-1]
    pieces = jnp.pad(pieces, [(0, 0)] * (pieces.ndim - 1) + [(0, pad)])
    return pieces[..., None, :]


def on_device(tokens, expert_ids, gate_values, w_gate, w_up, w_down, partner):
    tok_rows, model_width = tokens.shape
    route_count = expert_ids.shape[1]
    local_experts = w_gate.shape[0]
    group = lax.axis_size("expert")
    experts = group * local_experts
    capacity = tok_rows * route_count // experts + max(1, tok_rows * route_count // (16 * experts))
    slot_total = experts * capacity
    me = lax.axis_index("expert")
    row_block = lax.axis_index("dp")

    gate_full, up_full, down_full = (
        lax.all_gather(w_gate, "dp", axis=1, tiled=True),
        lax.all_gather(w_up, "dp", axis=1, tiled=True),
        lax.all_gather(w_down, "dp", axis=1, tiled=True),
    )

    expert_iota = jnp.arange(experts, dtype=jnp.int32)
    matches = expert_ids[:, :, None] == expert_iota
    chosen = jnp.sum(matches.astype(jnp.int32), axis=1, dtype=jnp.int32)
    chosen_gate = jnp.sum(jnp.where(matches, gate_values[:, :, None], 0.0), axis=1)
    before = jnp.cumsum(chosen, axis=0, dtype=jnp.int32) - chosen
    slot_rank = jnp.take_along_axis(before, expert_ids, axis=1)
    slot_row = (expert_ids * capacity + slot_rank).reshape(-1)
    slot_iota = jnp.arange(capacity, dtype=jnp.int32)
    onehot = (chosen.T[:, None, :] == 1) & (before.T[:, None, :] == slot_iota[None, :, None])
    placer = onehot.astype(bf16)
    slot_gate = jnp.sum(jnp.where(onehot, chosen_gate.T[:, None, :], 0.0), axis=2)
    outgoing = jnp.einsum("ect,td->ecd", placer, tokens, preferred_element_type=f32).astype(bf16)
    outgoing = jnp.concatenate([outgoing, pack_row(slot_gate, model_width)], axis=1)
    outgoing = outgoing.reshape(experts, 1, capacity + 1, model_width)
    placer_flat = placer.reshape(slot_total, tok_rows)

    arrived = lax.all_to_all(outgoing, "expert", split_axis=0, concat_axis=1, tiled=True)
    rows_in = arrived[:, :, :capacity, :]
    gates = join3(arrived[:, :, capacity, :], capacity)
    pre_gate = jnp.einsum("escd,edf->escf", rows_in, gate_full, preferred_element_type=f32)
    pre_up = jnp.einsum("escd,edf->escf", rows_in, up_full, preferred_element_type=f32)
    activated, derivative = silu_parts(pre_gate)
    hidden = (activated * pre_up).astype(bf16)
    expert_out = jnp.einsum("escf,efd->escd", hidden, down_full, preferred_element_type=f32).astype(
        bf16
    )
    out_f32 = expert_out.astype(f32)
    partial = jnp.sum(gates[..., None] * out_f32, axis=(0, 2))

    token_mean = jnp.mean(tokens.astype(f32), axis=0)
    own_row = (jnp.arange(group, dtype=jnp.int32) == me)[:, None]
    share = partial / tok_rows + jnp.where(own_row, token_mean[None, :], 0.0)
    pooled = lax.psum(share, "expert")
    inv_rms = lax.rsqrt(jnp.mean(pooled * pooled, axis=1) + 1e-06)
    embedding = (pooled * inv_rms[:, None]).astype(bf16)
    gathered = lax.all_gather(embedding, "dp", axis=0, tiled=True)
    batch_size = gathered.shape[0]

    scores = (
        score_scale
        / model_width
        * lax.dot_general(
            gathered, gathered, (((1,), (1,)), ((), ())), preferred_element_type=f32
        )
    )
    batch_iota = jnp.arange(batch_size, dtype=jnp.int32)
    others = batch_iota[:, None] != batch_iota[None, :]
    log_total = jnp.log(jnp.sum(jnp.where(others, jnp.exp(scores), 0.0), axis=1))
    partner_score = jnp.take_along_axis(scores, partner[:, None], axis=1)[:, 0]
    contrast_loss = jnp.mean(log_total - partner_score)

    first = row_block * group
    rows = first + jnp.arange(group, dtype=jnp.int32)
    row_scores = lax.dynamic_slice_in_dim(scores, first, group, axis=0)
    row_totals = lax.dynamic_slice_in_dim(log_total, first, group, axis=0)
    row_partner = lax.dynamic_slice_in_dim(partner, first, group, axis=0)
    row_others = rows[:, None] != batch_iota[None, :]
    row_weight = jnp.where(row_others, jnp.exp(row_scores - row_totals[:, None]), 0.0) - (
        batch_iota[None, :] == row_partner[:, None]
    ).astype(f32)
    col_scores = lax.dynamic_slice_in_dim(scores, first, group, axis=1).T
    col_weight = jnp.where(row_others, jnp.exp(col_scores - log_total[None, :]), 0.0) - (
        rows[:, None] == partner[None, :]
    ).astype(f32)
    embed_grad = (
        score_scale
        / model_width
        * jnp.dot(row_weight + col_weight, gathered.astype(f32), precision=highest)
    )
    seq_grad = (
        inv_rms[:, None] * embed_grad
        - (inv_rms**3 * jnp.sum(pooled * embed_grad, axis=1) / model_width)[:, None] * pooled
    )

    slot_dots = jnp.sum(out_f32 * seq_grad[None, :, None, :], axis=3)
    out_grad = (gates[..., None] * seq_grad[None, :, None, :]).astype(bf16)
    hidden_grad = jnp.einsum("escd,efd->escf", out_grad, down_full, preferred_element_type=f32)
    gate_side = (hidden_grad * pre_up * derivative).astype(bf16)
    up_side = (hidden_grad * activated).astype(bf16)
    route_here = jnp.einsum("escf,edf->escd", gate_side, gate_full, preferred_element_type=f32)
    route_here = (
        route_here
        + jnp.einsum("escf,edf->escd", up_side, up_full, preferred_element_type=f32)
    ).astype(bf16)
    route_here = jnp.concatenate([route_here, pack_row(slot_dots, model_width)], axis=2)
    returned = lax.all_to_all(route_here, "expert", split_axis=1, concat_axis=0, tiled=True)
    returned = returned.reshape(experts, capacity + 1, model_width)

    route_rows = returned[:, :capacity, :].reshape(slot_total, model_width)
    slot_grads = join3(returned[:, capacity, :], capacity).reshape(slot_total)
    gate_grad = jnp.take(slot_grads, slot_row, axis=0).reshape(tok_rows, route_count)
    route_sum = jnp.einsum("st,sd->td", placer_flat, route_rows, preferred_element_type=f32)
    own_grad = lax.dynamic_index_in_dim(seq_grad, me, axis=0, keepdims=False)
    token_grad = (own_grad[None, :] + route_sum).astype(bf16)
    return (contrast_loss, token_grad, gate_grad)


def solution(mesh):
    placed = (
        P(("dp", "expert"), None),
        P(("dp", "expert"), None),
        P(("dp", "expert"), None),
        P("expert", "dp", None),
        P("expert", "dp", None),
        P("expert", "dp", None),
        P(),
    )
    return jax.shard_map(
        on_device,
        mesh=mesh,
        in_specs=placed,
        out_specs=(P(), P(("dp", "expert"), None), P(("dp", "expert"), None)),
        check_vma=False,
    )
```

time: 605 us -> 458 us (0.76)
  blocking collectives: 173 us -> 0 us
  waiting for transfers between devices: 301 us -> 342 us
  starting transfers between devices: 28.9 us -> 20.5 us
    psum x0 -> x1, waiting for transfers between devices: none -> 146 us  [on_device(): pooled = lax.psum(share, 'expert')]
    unnamed x1 -> x0, blocking collectives: 97.8 us -> none
    all_to_all x1 -> x0, blocking collectives: 75.5 us -> none  [on_device(): lax.all_to_all(out_grad, 'expert', split_axis=0, concat_axis=1, tiled=True)]
    all_gather x1, waiting for transfers between devices: 105 us -> 43.7 us  [on_device(): gathered = lax.all_gather(embedding, 'dp', axis=0, tiled=True)]
    all_to_all x1 -> x0, waiting for transfers between devices: 50.5 us -> none  [on_device(): lax.all_to_all(out_here, 'expert', split_axis=1, concat_axis=0, tiled=True)]
    all_gather x1, waiting for transfers between devices: 32.5 us -> 0.01 us  [on_device(): lax.all_gather(w_gate, 'dp', axis=1, tiled=True)]
    all_to_all x1, waiting for transfers between devices: 38.2 us -> 70.6 us  [on_device(): lax.all_to_all(outgoing, 'expert', split_axis=0, concat_axis=1, tiled=True)]
    all_to_all x1, waiting for transfers between devices: 33.3 us -> 45 us  [on_device(): lax.all_to_all(route_here, 'expert', split_axis=1, concat_axis=0, tiled=T...]
  transfers between devices with their start and end apart: 7 -> 7, of which waited for: 7 -> 5; matrix products, arithmetic and copies ran while one was open for 6% -> 6% of each run, Pallas kernels for 0% -> 0%
where the time goes in v1:
time: 458 us; the launch traced here: 456 us
  waiting for transfers between devices  342 us (75%)
  local copies, waits for them, and re-layouts  44 us (10%)
  matrix products  24.7 us (5%)
  starting transfers between devices  20.5 us (4%)
  between operations  15.9 us (3%)
  other arithmetic  9.16 us (2%)
    psum x1, waiting for transfers between devices, on_device(): pooled = lax.psum(share, 'expert')  146 us
    all_to_all x1, waiting for transfers between devices, on_device(): lax.all_to_all(outgoing, 'expert', split_axis=0, concat_axis=1, tiled=True)  70.6 us
    all_to_all x1, waiting for transfers between devices, on_device(): lax.all_to_all(route_here, 'expert', split_axis=1, concat_axis=0, tiled=T...  45 us
    all_gather x1, waiting for transfers between devices, on_device(): gathered = lax.all_gather(embedding, 'dp', axis=0, tiled=True)  43.7 us
    all_gather x1, waiting for transfers between devices, on_device(): lax.all_gather(w_down, 'dp', axis=1, tiled=True)  34.4 us
    all_to_all x1, starting transfers between devices, on_device(): lax.all_to_all(outgoing, 'expert', split_axis=0, concat_axis=1, tiled=True)  10.5 us
    all_to_all x1, starting transfers between devices, on_device(): lax.all_to_all(route_here, 'expert', split_axis=1, concat_axis=0, tiled=T...  9.6 us
  transfers between devices with their start and end apart: 7, of which 5 were waited for; matrix products, arithmetic and copies ran while one was open for 6% of the time, Pallas kernels for 0%

profile of v1, /device:TPU:1, one launch (start us, length us, event | category | flops | bytes accessed | tf_op | source)
XLA Modules:
  0.0 455.9 jit_solution(546418799210746381)
XLA Ops:
  7.2 0.7 all-gather.5.cloned.1.call-update
  8.0 0.7 all-gather.7.cloned.1.call-update
  8.7 0.7 convert_reduce_fusion.1
  9.5 0.7 select_reduce_fusion.2
  10.2 0.2 reduce_window_sum.11
  10.5 0.2 select_reduce_fusion.1
  10.9 0.7 convolution_convert_fusion.1
  11.7 0.2 maximum_bitcast_fusion
  11.9 3.0 copy.126
  14.9 10.5 %all-to-all-start = ((bf16[64,1,18,1024]{3,2,1,0:T(8,128)(2,1)}), bf16[64,1,18,1024]{3,2,1,0:T(8,128)(2,1)S(1)}, u32[]{:S(2)}, u32[]{:S(2)}) async-start(bf16[64,1,18,1024]{3,2,1,0:T(8,128)(2,1)} %copy.126), calls=%async_computation | async-start | bytes 6291456 | tf_op jit(solution)/shard_map/all_to_all | solution.py:72
  25.5 0.7 all-gather.9.cloned.1.call-update
  26.3 70.6 %all-to-all-done = bf16[64,1,18,1024]{3,2,1,0:T(8,128)(2,1)S(1)} async-done(((bf16[64,1,18,1024]{3,2,1,0:T(8,128)(2,1)}), bf16[64,1,18,1024]{3,2,1,0:T(8,128)(2,1)S(1)}, u32[]{:S(2)}, u32[]{:S(2)}) %all-to-all-start) | async-done | bytes 2359328 | tf_op jit(solution)/shard_map/all_to_all | solution.py:72
  96.9 1.7 copy-done
  98.6 3.2 copy.146
  102.0 3.9 fusion.13
  105.9 3.9 fusion.9
  109.8 34.4 %all-gather.9.cloned.1.call-done = bf16[2,384,1024]{2,1,0:T(8,128)(2,1)} async-done(((bf16[2,24,1024]{2,1,0:T(8,128)(2,1)}), bf16[2,384,1024]{2,1,0:T(8,128)(2,1)}) %all-gather.9.cloned.1.call-update) | async-done | bytes 1572880 | tf_op jit(solution)/shard_map/all_gather | solution.py:53
  144.2 3.8 fusion
  148.0 0.7 select_add_fusion
  148.8 0.2 all-gather.11.cloned.1.call-start
  149.0 145.7 %all-reduce.4.cloned.1.call-done = f32[32,1024]{1,0:T(8,128)} async-done(((f32[32,1024]{1,0:T(8,128)}), f32[32,1024]{1,0:T(8,128)}) %all-reduce.4.cloned.1.call-update) | async-done | bytes 131088 | tf_op jit(solution)/shard_map/psum | solution.py:88
  294.8 1.0 multiply_reduce_fusion.1
  295.8 1.6 multiply_convert_fusion.8
  297.5 0.6 dynamic_slice.18
  298.0 0.5 iota_add_fusion
  298.6 43.7 %all-gather.11.cloned.1.call-done = bf16[512,1024]{1,0:T(8,128)(2,1)} async-done(((bf16[32,1024]{1,0:T(8,128)(2,1)}), bf16[512,1024]{1,0:T(8,128)(2,1)}) %all-gather.11.cloned.1.call-update) | async-done | bytes 1048592 | tf_op jit(solution)/shard_map/all_gather | solution.py:91
  342.3 3.1 select_reduce_fusion
  345.4 0.8 constant_dynamic-slice_fusion.1
  346.2 4.5 gather_fusion.1
  350.8 1.3 fusion.81
  352.1 0.6 dynamic_slice.17
  352.7 1.7 copy.144
  354.4 2.1 multiply_reduce_fusion
  356.6 0.5 fusion.1
  357.3 2.9 fusion.2
  360.3 1.5 fusion.11
  361.8 1.4 add_convert_fusion
  363.3 0.2 pad_maximum_fusion
  363.5 3.8 copy.133
  367.3 9.6 %all-to-all-start.1 = ((bf16[2,32,18,1024]{3,0,2,1:T(2,128)(2,1)}), bf16[2,32,18,1024]{3,0,2,1:T(2,128)(2,1)S(1)}, u32[]{:S(2)}, u32[]{:S(2)}) async-start(bf16[2,32,18,1024]{3,0,2,1:T(2,128)(2,1)} %copy.133), calls=%async_computation.1 | async-start | bytes 4718592 | tf_op jit(solution)/shard_map/all_to_all | solution.py:141
  377.2 7.1 %gather_fusion.2 = s32[1024]{0:T(1024)S(1)} fusion(s32[128,64]{1,0:T(8,128)S(1)} %sub.51, s32[1024]{0:T(1024)S(1)} %reshape.148), kind=kCustom, calls=%fused_computation.2 | custom fusion | bytes 16384 | tf_op jit(solution)/shard_map/jit(take_along_axis)/gather | solution.py:61
  385.3 0.8 constant_dynamic-slice_fusion
  386.1 45.0 %all-to-all-done.1 = bf16[2,32,18,1024]{3,0,2,1:T(2,128)(2,1)S(1)} async-done(((bf16[2,32,18,1024]{3,0,2,1:T(2,128)(2,1)}), bf16[2,32,18,1024]{3,0,2,1:T(2,128)(2,1)S(1)}, u32[]{:S(2)}, u32[]{:S(2)}) %all-to-all-start.1) | async-done | bytes 2359328 | tf_op jit(solution)/shard_map/all_to_all | solution.py:141
  431.1 3.7 copy.134
  434.8 5.0 %reshape.128 = bf16[64,18,1024]{2,0,1:T(8,128)(2,1)S(1)} reshape(bf16[32,2,1,18,1024]{4,1,0,3,2:T(2,128)(2,1)} %copy.134) | data formatting | bytes 4718592 | tf_op jit(solution)/shard_map/reshape | solution.py:142
  439.8 1.3 fusion.23
  441.3 6.2 %gather_fusion = f32[1024]{0:T(1024)S(1)} fusion(f32[1088]{0:T(1024)S(1)} %reshape.130, s32[1024]{0:T(1024)S(1)} %broadcast_clamp_fusion), kind=kCustom, calls=%fused_computation | custom fusion | bytes 12288 | tf_op jit(solution)/shard_map/jit(_take)/gather | solution.py:146
  447.6 0.6 and_select_fusion
  (65 shorter events, 2.1 us)
Async XLA Ops:
  7.2 3.8 copy-start.6
  7.2 94.8 %all-gather.5.cloned.1.call-start = ((), (), s32[]{:S(2)}) async-start(), calls=%async_computation.2 | async-start | bytes 1671168 | tf_op jit(solution)/shard_map/all_gather | solution.py:51
  7.9 98.0 %all-gather.7.cloned.1.call-start = ((), (), s32[]{:S(2)}) async-start(), calls=%async_computation.3 | async-start | bytes 1671168 | tf_op jit(solution)/shard_map/all_gather | solution.py:52
  14.9 82.0 %all-to-all-start = ((bf16[64,1,18,1024]{3,2,1,0:T(8,128)(2,1)}), bf16[64,1,18,1024]{3,2,1,0:T(8,128)(2,1)S(1)}, u32[]{:S(2)}, u32[]{:S(2)}) async-start(bf16[64,1,18,1024]{3,2,1,0:T(8,128)(2,1)} %copy.126), calls=%async_computation | async-start | bytes 6291456 | tf_op jit(solution)/shard_map/all_to_all | solution.py:72
  25.4 118.8 %all-gather.9.cloned.1.call-start = ((), (), s32[]{:S(2)}) async-start(), calls=%async_computation.4 | async-start | bytes 1671168 | tf_op jit(solution)/shard_map/all_gather | solution.py:53
  26.2 268.6 %all-reduce.4.cloned.1.call-start = ((), (), s32[]{:S(2)}) async-start(), calls=%async_computation.5 | async-start | bytes 262144 | tf_op jit(solution)/shard_map/psum | solution.py:88
  96.9 1.7 copy-start
  109.8 187.6 %copy-start.9 = (s32[512]{0:T(512)S(1)}, s32[512]{0:T(512)}, u32[]{:S(2)}) copy-start(s32[512]{0:T(512)} %param.13) | copy-start | bytes 6148
  148.8 193.5 %all-gather.11.cloned.1.call-start = ((), (), s32[]{:S(2)}) async-start(), calls=%async_computation.6 | async-start | bytes 1114112 | tf_op jit(solution)/shard_map/all_gather | solution.py:91
  345.4 9.0 %copy-start.1 = (f32[32,1024]{1,0:T(8,128)S(1)}, f32[32,1024]{1,0:T(8,128)}, u32[]{:S(2)}) copy-start(f32[32,1024]{1,0:T(8,128)} %all-reduce.4.cloned.1.call-done) | copy-start | bytes 393220
  356.5 3.7 copy-start.7
  357.3 3.0 copy-start.2
  357.3 3.0 copy-start.3
  357.3 3.0 copy-start.4
  360.3 1.6 copy-start.5
  367.3 9.6 %copy-start.8 = (s32[128,8]{0,1:T(8,128)S(1)}, s32[128,8]{0,1:T(8,128)}, u32[]{:S(2)}) copy-start(s32[128,8]{0,1:T(8,128)} %param.8) | copy-start | bytes 12292
  367.3 63.7 %all-to-all-start.1 = ((bf16[2,32,18,1024]{3,0,2,1:T(2,128)(2,1)}), bf16[2,32,18,1024]{3,0,2,1:T(2,128)(2,1)S(1)}, u32[]{:S(2)}, u32[]{:S(2)}) async-start(bf16[2,32,18,1024]{3,0,2,1:T(2,128)(2,1)} %copy.133), calls=%async_computation.1 | async-start | bytes 4718592 | tf_op jit(solution)/shard_map/all_to_all | solution.py:141
Sparse Core Ops, SparseCore 0:
  10.1 48.2 all-gather.4
  60.6 40.5 all-gather.6
  103.4 40.8 all-gather.8
  148.9 145.8 all-reduce.3
  297.6 44.7 all-gather.10

commit v2 on v1

--- a/solution.py
+++ b/solution.py
@@ -47,11 +47,19 @@
     me = lax.axis_index("expert")
     row_block = lax.axis_index("dp")
 
-    gate_full, up_full, down_full = (
-        lax.all_gather(w_gate, "dp", axis=1, tiled=True),
-        lax.all_gather(w_up, "dp", axis=1, tiled=True),
-        lax.all_gather(w_down, "dp", axis=1, tiled=True),
-    )
+    ff_width = w_gate.shape[2]
+    stacked = jnp.stack([w_gate, w_up, w_down.reshape(w_gate.shape)])
+    every = lax.all_gather(stacked, "dp", axis=0, tiled=False)
+    parts = every.shape[0]
+
+    def joined(k, slab, inner):
+        return jnp.swapaxes(every[:, k].reshape((parts, local_experts) + slab), 0, 1).reshape(
+            (local_experts, parts * slab[0]) + inner
+        )
+
+    gate_full = joined(0, w_gate.shape[1:], (ff_width,))
+    up_full = joined(1, w_gate.shape[1:], (ff_width,))
+    down_full = joined(2, w_down.shape[1:], (model_width,))
 
     expert_iota = jnp.arange(experts, dtype=jnp.int32)
     matches = expert_ids[:, :, None] == expert_iota
@@ -83,9 +91,10 @@
     partial = jnp.sum(gates[..., None] * out_f32, axis=(0, 2))
 
     token_mean = jnp.mean(tokens.astype(f32), axis=0)
-    own_row = (jnp.arange(group, dtype=jnp.int32) == me)[:, None]
-    share = partial / tok_rows + jnp.where(own_row, token_mean[None, :], 0.0)
-    pooled = lax.psum(share, "expert")
+    shares = lax.all_to_all(partial / tok_rows, "expert", split_axis=0, concat_axis=0, tiled=True)
+    own_pooled = token_mean + jnp.sum(shares, axis=0)
+    copies = jnp.broadcast_to(own_pooled[None, :], (group, model_width))
+    pooled = lax.all_to_all(copies, "expert", split_axis=0, concat_axis=0, tiled=True)
     inv_rms = lax.rsqrt(jnp.mean(pooled * pooled, axis=1) + 1e-06)
     embedding = (pooled * inv_rms[:, None]).astype(bf16)
     gathered = lax.all_gather(embedding, "dp", axis=0, tiled=True)

time: 458 us -> 307 us (0.67)
  waiting for transfers between devices: 342 us -> 98.7 us
  blocking collectives: 0 us -> 92.6 us
  local copies, waits for them, and re-layouts: 44 us -> 52.2 us
  matrix products: 24.7 us -> 19.8 us
    psum x1 -> x0, waiting for transfers between devices: 146 us -> none  [on_device(): pooled = lax.psum(share, 'expert')]
    all_to_all x0 -> x2, blocking collectives: none -> 92.6 us  [the longest x1 79.9 us: on_device(): lax.all_to_all(outgoing, 'expert', split_axis=0, concat_axis=1, tiled=True)]
    all_to_all x1, waiting for transfers between devices: 70.6 us -> 9.05 us  [on_device(): lax.all_to_all(partial / tok_rows, 'expert', split_axis=0, concat_axis=0,...]
    all_gather x3 -> x1, waiting for transfers between devices: 34.4 us -> 0.01 us  [on_device(): every = lax.all_gather(stacked, 'dp', axis=0, tiled=False)]
    another operation x0 -> x3, local copies, waits for them, and re-layouts: none -> 7.04 us  [the longest x2 5.98 us: joined(): every[:, k].reshape((parts, local_experts) + slab)]
    slice x0 -> x1, local copies, waits for them, and re-layouts: none -> 4.81 us  [joined(): every[:, k].reshape((parts, local_experts) + slab)]
  transfers between devices with their start and end apart: 7 -> 4, of which waited for: 5 -> 3; matrix products, arithmetic and copies ran while one was open for 6% -> 5% of each run, Pallas kernels for 0% -> 0%
where the time goes in v2:
time: 307 us; the launch traced here: 305 us
  waiting for transfers between devices  98.7 us (32%)
  blocking collectives  92.6 us (30%)
  local copies, waits for them, and re-layouts  52.2 us (17%)
  matrix products  19.8 us (6%)
  starting transfers between devices  18.3 us (6%)
  between operations  16.3 us (5%)
  other arithmetic  7.22 us (2%)
    all_to_all x1, blocking collectives, on_device(): lax.all_to_all(outgoing, 'expert', split_axis=0, concat_axis=1, tiled=True)  79.9 us
    all_to_all x1, waiting for transfers between devices, on_device(): lax.all_to_all(route_here, 'expert', split_axis=1, concat_axis=0, tiled=T...  45.7 us
    all_gather x1, waiting for transfers between devices, on_device(): gathered = lax.all_gather(embedding, 'dp', axis=0, tiled=True)  43.9 us
    all_to_all x1, blocking collectives, on_device(): lax.all_to_all(copies, 'expert', split_axis=0, concat_axis=0, tiled=True)  12.7 us
    all_to_all x1, starting transfers between devices, on_device(): lax.all_to_all(route_here, 'expert', split_axis=1, concat_axis=0, tiled=T...  9.61 us
    all_to_all x1, waiting for transfers between devices, on_device(): lax.all_to_all(partial / tok_rows, 'expert', split_axis=0, concat_axis=0,...  9.05 us
    all_to_all x1, starting transfers between devices, on_device(): lax.all_to_all(partial / tok_rows, 'expert', split_axis=0, concat_axis=0,...  8.59 us
    gather x5, local copies, waits for them, and re-layouts, on_device(): slot_rank = jnp.take_along_axis(before, expert_ids, axis=1)  7.39 us
  transfers between devices with their start and end apart: 4, of which 3 were waited for; matrix products, arithmetic and copies ran while one was open for 5% of the time, Pallas kernels for 0%

profile of v2, /device:TPU:1, one launch (start us, length us, event | category | flops | bytes accessed | tf_op | source)
XLA Modules:
  0.0 305.1 jit_solution(2950248311429738672)
XLA Ops:
  7.2 1.1 stack_reshape.3
  8.3 1.7 pad_maximum_fusion.1
  10.0 0.7 convert_reduce_fusion.1
  10.8 0.2 reduce_window_sum.11
  11.1 0.8 select_reduce_fusion.2
  11.9 0.2 select_reduce_fusion.1
  12.3 0.7 convolution_convert_fusion.1
  13.0 0.2 maximum_bitcast_fusion
  13.2 1.4 copy.144
  14.6 79.9 %all_to_all.48 = bf16[64,1,18,1024]{3,2,1,0:T(8,128)(2,1)S(1)} all-to-all(bf16[64,1,18,1024]{3,2,1,0:T(8,128)(2,1)S(1)} %copy.144), channel_id=1, replica_groups=mesh['dp'=16,'expert'=32] {'expert'}, dimensions={0} | all-to-all | bytes 4718592 | tf_op jit(solution)/shard_map/all_to_all | solution.py:80
  94.5 1.3 copy.175
  96.0 4.8 %fusion.77 = (bf16[16,1,2,64,384]{4,3,2,1,0:T(8,128)(2,1)S(1)}, bf16[16,1,2,64,384]{4,3,2,1,0:T(8,128)(2,1)}, bf16[16,1,2,64,384]{4,3,2,1,0:T(8,128)(2,1)}) fusion(bf16[16,3,2,64,384]{4,3,2,1,0:T(8,128)(2,1)} %bitcast.118), kind=kLoop, calls=%fused_computation.134 | loop fusion | bytes 9437184 | tf_op jit(solution)/shard_map/slice | solution.py:56
  100.8 1.4 copy.167
  102.2 4.3 %reshape.194 = bf16[16,2,24,1024]{3,2,1,0:T(8,128)(2,1)} reshape(bf16[16,1,2,64,384]{4,3,2,1,0:T(8,128)(2,1)} %get-tuple-element.19) | data formatting | bytes 3145728 | tf_op jit(solution)/shard_map/reshape;squeeze | solution.py:56
  106.5 1.7 copy.165
  108.2 0.2 copy-done
  108.4 0.2 copy.168
  108.6 2.2 copy-done.1
  110.8 1.3 fusion.79
  112.1 1.3 fusion.80
  113.5 2.8 fusion
  116.3 0.7 div.31
  117.0 8.6 %all-to-all-start.1 = ((f32[32,1,1024]{2,1,0:T(1,128)}), f32[32,1,1024]{2,1,0:T(1,128)S(1)}, u32[]{:S(2)}, u32[]{:S(2)}) async-start(f32[32,1,1024]{2,1,0:T(1,128)} %div.31), calls=%async_computation.1 | async-start | bytes 262144 | tf_op jit(solution)/shard_map/all_to_all | solution.py:94
  125.7 9.1 %all-to-all-done.1 = f32[32,1,1024]{2,1,0:T(1,128)S(1)} async-done(((f32[32,1,1024]{2,1,0:T(1,128)}), f32[32,1,1024]{2,1,0:T(1,128)S(1)}, u32[]{:S(2)}, u32[]{:S(2)}) %all-to-all-start.1) | async-done | bytes 131104 | tf_op jit(solution)/shard_map/all_to_all | solution.py:94
  135.0 12.7 %all_to_all.49 = f32[32,1,1024]{2,1,0:T(1,128)S(1)} all-to-all(f32[32,1,1024]{2,1,0:T(1,128)S(1)} %broadcast_in_dim.56), channel_id=1, replica_groups=mesh['dp'=16,'expert'=32] {'expert'}, dimensions={0} | all-to-all | bytes 262144 | tf_op jit(solution)/shard_map/all_to_all | solution.py:97
  147.8 0.7 fusion.42
  148.7 43.9 %all-gather.4.cloned.1.call-done = bf16[512,1024]{1,0:T(8,128)(2,1)} async-done(((bf16[32,1024]{1,0:T(8,128)(2,1)}), bf16[512,1024]{1,0:T(8,128)(2,1)}) %all-gather.4.cloned.1.call-update) | async-done | bytes 1048592 | tf_op jit(solution)/shard_map/all_gather | solution.py:100
  192.6 2.4 select_reduce_fusion
  195.0 0.1 constant_dynamic-slice_fusion.1
  195.2 4.5 %gather_fusion.1 = f32[512]{0:T(512)S(1)} fusion(f32[512,512]{0,1:T(8,128)S(1)} %get-tuple-element.34, s32[512]{0:T(512)S(1)} %bitcast.108), kind=kCustom, calls=%fused_computation.1 | custom fusion | bytes 8192 | tf_op jit(solution)/shard_map/jit(take_along_axis)/gather | solution.py:113
  199.7 0.6 fusion.78
  200.5 0.8 fusion.43
  201.5 4.1 %fusion.2 = f32[2,32,17,384]{3,1,2,0:T(8,128)} fusion(bf16[2,384,1024,1]{2,1,3,0:T(8,128)(2,1)} %bitcast.120, f32[32,1024]{1,0:T(8,128)S(1)} %fusion.44, f32[2,32,17]{1,2,0:T(8,128)S(1)} %copy.147), kind=kOutput, calls=%fused_computation.12 | convolution fusion | flops 857866240 | bytes 3379456 | tf_op jit(solution)/shard_map/escd,efd->escf/dot_general | solution.py:141
  205.6 0.5 fusion.1
  206.3 0.8 copy-done.2
  207.0 3.6 %fusion.17 = f32[2,32,17,1024]{3,1,2,0:T(8,128)S(1)} fusion(bf16[2,1024,384,1]{2,1,3,0:T(8,128)(2,1)S(1)} %bitcast.115, f32[2,32,17,384]{3,1,2,0:T(8,128)S(1)} %copy-done.7, f32[2,32,17,384]{3,1,2,0:T(8,128)} %fusion.2, f32[2,32,17,384]{3,1,2,0:T(8,128)} %copy-done.8), kind=kOutput, calls=%fused_computation.30 | convolution fusion | flops 859815936 | bytes 11042816 | tf_op jit(solution)/shard_map/escf,edf->escd/dot_general | solution.py:144
  210.6 1.4 add_convert_fusion
  212.1 0.2 pad_maximum_fusion
  212.3 3.8 %copy.154 = bf16[2,32,18,1024]{3,0,2,1:T(2,128)(2,1)} copy(bf16[2,32,18,1024]{3,1,2,0:T(8,128)(2,1)S(1)} %pad_maximum_fusion) | data formatting | bytes 4718592 | tf_op jit(solution)/shard_map/concatenate | solution.py:149
  216.2 9.6 %all-to-all-start.3 = ((bf16[2,32,18,1024]{3,0,2,1:T(2,128)(2,1)}), bf16[2,32,18,1024]{3,0,2,1:T(2,128)(2,1)S(1)}, u32[]{:S(2)}, u32[]{:S(2)}) async-start(bf16[2,32,18,1024]{3,0,2,1:T(2,128)(2,1)} %copy.154), calls=%async_computation.3 | async-start | bytes 4718592 | tf_op jit(solution)/shard_map/all_to_all | solution.py:150
  226.0 7.1 %gather_fusion.2 = s32[1024]{0:T(1024)S(1)} fusion(s32[128,64]{1,0:T(8,128)S(1)} %sub.51, s32[1024]{0:T(1024)S(1)} %reshape.176), kind=kCustom, calls=%fused_computation.2 | custom fusion | bytes 16384 | tf_op jit(solution)/shard_map/jit(take_along_axis)/gather | solution.py:69
  234.2 45.7 %all-to-all-done.3 = bf16[2,32,18,1024]{3,0,2,1:T(2,128)(2,1)S(1)} async-done(((bf16[2,32,18,1024]{3,0,2,1:T(2,128)(2,1)}), bf16[2,32,18,1024]{3,0,2,1:T(2,128)(2,1)S(1)}, u32[]{:S(2)}, u32[]{:S(2)}) %all-to-all-start.3) | async-done | bytes 2359328 | tf_op jit(solution)/shard_map/all_to_all | solution.py:150
  279.9 3.7 %copy.155 = bf16[32,2,1,18,1024]{4,1,0,3,2:T(2,128)(2,1)} copy(bf16[32,2,1,18,1024]{4,1,3,0,2:T(2,128)(2,1)S(1)} %bitcast.113) | data formatting | bytes 4718592 | tf_op jit(solution)/shard_map/all_to_all | solution.py:150
  283.6 5.0 %reshape.156 = bf16[64,18,1024]{2,0,1:T(8,128)(2,1)S(1)} reshape(bf16[32,2,1,18,1024]{4,1,0,3,2:T(2,128)(2,1)} %copy.155) | data formatting | bytes 4718592 | tf_op jit(solution)/shard_map/reshape | solution.py:151
  288.7 1.3 fusion.14
  290.0 0.1 reshape.158
  290.2 6.2 %gather_fusion = f32[1024]{0:T(1024)S(1)} fusion(f32[1088]{0:T(1024)S(1)} %reshape.158, s32[1024]{0:T(1024)S(1)} %broadcast_clamp_fusion), kind=kCustom, calls=%fused_computation | custom fusion | bytes 12288 | tf_op jit(solution)/shard_map/jit(_take)/gather | solution.py:155
  296.5 0.6 and_select_fusion
  (77 shorter events, 2.4 us)
Async XLA Ops:
  7.2 5.1 %copy-start.10 = (bf16[128,1024]{1,0:T(8,128)(2,1)S(1)}, bf16[128,1024]{1,0:T(8,128)(2,1)}, u32[]{:S(2)}) copy-start(bf16[128,1024]{1,0:T(8,128)(2,1)} %param.7) | copy-start | bytes 786436
  7.2 88.8 %all-gather.6.cloned.1.call-start = ((), (), s32[]{:S(2)}) async-start(), calls=%async_computation.5 | async-start | bytes 5013504 | tf_op jit(solution)/shard_map/all_gather | solution.py:52
  106.5 1.9 copy-start
  108.2 5.3 %copy-start.9 = (bf16[16,2,24,1024]{3,2,0,1:T(8,128)(2,1)}, bf16[16,2,24,1024]{3,2,0,1:T(8,128)(2,1)S(1)}, u32[]{:S(2)}) copy-start(bf16[16,2,24,1024]{3,2,0,1:T(8,128)(2,1)S(1)} %copy.165) | copy-start | bytes 4718596
  108.2 2.6 copy-start.1
  108.5 3.6 %copy-start.3 = (bf16[16,1,2,64,384]{4,3,0,2,1:T(8,128)(2,1)}, bf16[16,1,2,64,384]{4,3,0,2,1:T(8,128)(2,1)S(1)}, u32[]{:S(2)}) copy-start(bf16[16,1,2,64,384]{4,3,0,2,1:T(8,128)(2,1)S(1)} %copy.168) | copy-start | bytes 4718596
  112.1 1.4 copy-start.6
  113.5 2.8 copy-start.8
  116.3 32.3 %copy-start.13 = (s32[512]{0:T(512)S(1)}, s32[512]{0:T(512)}, u32[]{:S(2)}) copy-start(s32[512]{0:T(512)} %param.13) | copy-start | bytes 6148
  117.0 17.8 %all-to-all-start.1 = ((f32[32,1,1024]{2,1,0:T(1,128)}), f32[32,1,1024]{2,1,0:T(1,128)S(1)}, u32[]{:S(2)}, u32[]{:S(2)}) async-start(f32[32,1,1024]{2,1,0:T(1,128)} %div.31), calls=%async_computation.1 | async-start | bytes 262144 | tf_op jit(solution)/shard_map/all_to_all | solution.py:94
  125.6 67.0 %all-gather.4.cloned.1.call-start = ((), (), s32[]{:S(2)}) async-start(), calls=%async_computation.4 | async-start | bytes 1114112 | tf_op jit(solution)/shard_map/all_gather | solution.py:100
  195.0 5.5 %copy-start.11 = (bf16[512,1024]{1,0:T(8,128)(2,1)S(1)}, bf16[512,1024]{1,0:T(8,128)(2,1)}, u32[]{:S(2)}) copy-start(bf16[512,1024]{1,0:T(8,128)(2,1)} %all-gather.4.cloned.1.call-done) | copy-start | bytes 3145732
  201.4 4.2 %copy-start.5 = (bf16[2,32,17,1024]{3,1,2,0:T(8,128)(2,1)S(1)}, bf16[2,32,17,1024]{3,1,2,0:T(8,128)(2,1)}, u32[]{:S(2)}) copy-start(bf16[2,32,17,1024]{3,1,2,0:T(8,128)(2,1)} %get-tuple-element.32) | copy-start | bytes 6684676
  201.5 4.8 %copy-start.7 = (f32[2,32,17,384]{3,1,2,0:T(8,128)S(1)}, f32[2,32,17,384]{3,1,2,0:T(8,128)}, u32[]{:S(2)}) copy-start(f32[2,32,17,384]{3,1,2,0:T(8,128)} %copy-done.6) | copy-start | bytes 5013508
  205.6 1.4 copy-start.2
  207.0 3.6 %copy-start.4 = (bf16[16,1,2,64,384]{4,3,0,2,1:T(8,128)(2,1)S(1)}, bf16[16,1,2,64,384]{4,3,0,2,1:T(8,128)(2,1)}, u32[]{:S(2)}) copy-start(bf16[16,1,2,64,384]{4,3,0,2,1:T(8,128)(2,1)} %copy-done.3) | copy-start | bytes 4718596
  207.0 3.6 %copy-start.14 = (f32[2,32,17,384]{3,1,2,0:T(8,128)S(1)}, f32[2,32,17,384]{3,1,2,0:T(8,128)}, u32[]{:S(2)}) copy-start(f32[2,32,17,384]{3,1,2,0:T(8,128)} %fusion.2) | copy-start | bytes 5013508
  216.2 9.6 %copy-start.12 = (s32[128,8]{0,1:T(8,128)S(1)}, s32[128,8]{0,1:T(8,128)}, u32[]{:S(2)}) copy-start(s32[128,8]{0,1:T(8,128)} %param.8) | copy-start | bytes 12292
  216.2 63.7 %all-to-all-start.3 = ((bf16[2,32,18,1024]{3,0,2,1:T(2,128)(2,1)}), bf16[2,32,18,1024]{3,0,2,1:T(2,128)(2,1)S(1)}, u32[]{:S(2)}, u32[]{:S(2)}) async-start(bf16[2,32,18,1024]{3,0,2,1:T(2,128)(2,1)} %copy.154), calls=%async_computation.3 | async-start | bytes 4718592 | tf_op jit(solution)/shard_map/all_to_all | solution.py:150
Sparse Core Ops, SparseCore 0:
  10.1 51.9 all-gather.5
  148.7 43.8 all-gather.3

commit v3 on v2

--- a/solution.py
+++ b/solution.py
@@ -49,46 +49,38 @@
 
     ff_width = w_gate.shape[2]
     stacked = jnp.stack([w_gate, w_up, w_down.reshape(w_gate.shape)])
-    every = lax.all_gather(stacked, "dp", axis=0, tiled=False)
-    parts = every.shape[0]
-
-    def joined(k, slab, inner):
-        return jnp.swapaxes(every[:, k].reshape((parts, local_experts) + slab), 0, 1).reshape(
-            (local_experts, parts * slab[0]) + inner
-        )
-
-    gate_full = joined(0, w_gate.shape[1:], (ff_width,))
-    up_full = joined(1, w_gate.shape[1:], (ff_width,))
-    down_full = joined(2, w_down.shape[1:], (model_width,))
+    every = lax.all_gather(stacked, "dp", axis=2, tiled=True)
+    gate_full = every[0]
+    up_full = every[1]
+    down_full = every[2].reshape(local_experts, ff_width, model_width)
 
     expert_iota = jnp.arange(experts, dtype=jnp.int32)
     matches = expert_ids[:, :, None] == expert_iota
     chosen = jnp.sum(matches.astype(jnp.int32), axis=1, dtype=jnp.int32)
     chosen_gate = jnp.sum(jnp.where(matches, gate_values[:, :, None], 0.0), axis=1)
     before = jnp.cumsum(chosen, axis=0, dtype=jnp.int32) - chosen
-    slot_rank = jnp.take_along_axis(before, expert_ids, axis=1)
-    slot_row = (expert_ids * capacity + slot_rank).reshape(-1)
+    slot_rank = jnp.sum(jnp.where(matches, before[:, None, :], 0), axis=2, dtype=jnp.int32)
     slot_iota = jnp.arange(capacity, dtype=jnp.int32)
     onehot = (chosen.T[:, None, :] == 1) & (before.T[:, None, :] == slot_iota[None, :, None])
     placer = onehot.astype(bf16)
     slot_gate = jnp.sum(jnp.where(onehot, chosen_gate.T[:, None, :], 0.0), axis=2)
     outgoing = jnp.einsum("ect,td->ecd", placer, tokens, preferred_element_type=f32).astype(bf16)
     outgoing = jnp.concatenate([outgoing, pack_row(slot_gate, model_width)], axis=1)
-    outgoing = outgoing.reshape(experts, 1, capacity + 1, model_width)
+    outgoing = outgoing.reshape(group, local_experts, capacity + 1, model_width)
     placer_flat = placer.reshape(slot_total, tok_rows)
 
-    arrived = lax.all_to_all(outgoing, "expert", split_axis=0, concat_axis=1, tiled=True)
+    arrived = lax.all_to_all(outgoing, "expert", split_axis=0, concat_axis=0, tiled=True)
     rows_in = arrived[:, :, :capacity, :]
     gates = join3(arrived[:, :, capacity, :], capacity)
-    pre_gate = jnp.einsum("escd,edf->escf", rows_in, gate_full, preferred_element_type=f32)
-    pre_up = jnp.einsum("escd,edf->escf", rows_in, up_full, preferred_element_type=f32)
+    pre_gate = jnp.einsum("secd,edf->secf", rows_in, gate_full, preferred_element_type=f32)
+    pre_up = jnp.einsum("secd,edf->secf", rows_in, up_full, preferred_element_type=f32)
     activated, derivative = silu_parts(pre_gate)
     hidden = (activated * pre_up).astype(bf16)
-    expert_out = jnp.einsum("escf,efd->escd", hidden, down_full, preferred_element_type=f32).astype(
+    expert_out = jnp.einsum("secf,efd->secd", hidden, down_full, preferred_element_type=f32).astype(
         bf16
     )
     out_f32 = expert_out.astype(f32)
-    partial = jnp.sum(gates[..., None] * out_f32, axis=(0, 2))
+    partial = jnp.sum(gates[..., None] * out_f32, axis=(1, 2))
 
     token_mean = jnp.mean(tokens.astype(f32), axis=0)
     shares = lax.all_to_all(partial / tok_rows, "expert", split_axis=0, concat_axis=0, tiled=True)
@@ -97,7 +89,10 @@
     pooled = lax.all_to_all(copies, "expert", split_axis=0, concat_axis=0, tiled=True)
     inv_rms = lax.rsqrt(jnp.mean(pooled * pooled, axis=1) + 1e-06)
     embedding = (pooled * inv_rms[:, None]).astype(bf16)
-    gathered = lax.all_gather(embedding, "dp", axis=0, tiled=True)
+    blocks = lax.axis_size("dp")
+    spread = jnp.broadcast_to(embedding[None], (blocks, group, model_width))
+    gathered = lax.all_to_all(spread, "dp", split_axis=0, concat_axis=0, tiled=True)
+    gathered = gathered.reshape(blocks * group, model_width)
     batch_size = gathered.shape[0]
 
     scores = (
@@ -110,7 +105,8 @@
     batch_iota = jnp.arange(batch_size, dtype=jnp.int32)
     others = batch_iota[:, None] != batch_iota[None, :]
     log_total = jnp.log(jnp.sum(jnp.where(others, jnp.exp(scores), 0.0), axis=1))
-    partner_score = jnp.take_along_axis(scores, partner[:, None], axis=1)[:, 0]
+    partner_hit = batch_iota[None, :] == partner[:, None]
+    partner_score = jnp.sum(jnp.where(partner_hit, scores, 0.0), axis=1)
     contrast_loss = jnp.mean(log_total - partner_score)
 
     first = row_block * group
@@ -136,23 +132,24 @@
         - (inv_rms**3 * jnp.sum(pooled * embed_grad, axis=1) / model_width)[:, None] * pooled
     )
 
-    slot_dots = jnp.sum(out_f32 * seq_grad[None, :, None, :], axis=3)
-    out_grad = (gates[..., None] * seq_grad[None, :, None, :]).astype(bf16)
-    hidden_grad = jnp.einsum("escd,efd->escf", out_grad, down_full, preferred_element_type=f32)
+    slot_dots = jnp.sum(out_f32 * seq_grad[:, None, None, :], axis=3)
+    out_grad = (gates[..., None] * seq_grad[:, None, None, :]).astype(bf16)
+    hidden_grad = jnp.einsum("secd,efd->secf", out_grad, down_full, preferred_element_type=f32)
     gate_side = (hidden_grad * pre_up * derivative).astype(bf16)
     up_side = (hidden_grad * activated).astype(bf16)
-    route_here = jnp.einsum("escf,edf->escd", gate_side, gate_full, preferred_element_type=f32)
+    route_here = jnp.einsum("secf,edf->secd", gate_side, gate_full, preferred_element_type=f32)
     route_here = (
         route_here
-        + jnp.einsum("escf,edf->escd", up_side, up_full, preferred_element_type=f32)
+        + jnp.einsum("secf,edf->secd", up_side, up_full, preferred_element_type=f32)
     ).astype(bf16)
     route_here = jnp.concatenate([route_here, pack_row(slot_dots, model_width)], axis=2)
-    returned = lax.all_to_all(route_here, "expert", split_axis=1, concat_axis=0, tiled=True)
+    returned = lax.all_to_all(route_here, "expert", split_axis=0, concat_axis=0, tiled=True)
     returned = returned.reshape(experts, capacity + 1, model_width)
 
     route_rows = returned[:, :capacity, :].reshape(slot_total, model_width)
-    slot_grads = join3(returned[:, capacity, :], capacity).reshape(slot_total)
-    gate_grad = jnp.take(slot_grads, slot_row, axis=0).reshape(tok_rows, route_count)
+    slot_grads = join3(returned[:, capacity, :], capacity)
+    token_slot_grads = jnp.sum(jnp.where(onehot, slot_grads[:, :, None], 0.0), axis=1).T
+    gate_grad = jnp.sum(jnp.where(matches, token_slot_grads[:, None, :], 0.0), axis=2)
     route_sum = jnp.einsum("st,sd->td", placer_flat, route_rows, preferred_element_type=f32)
     own_grad = lax.dynamic_index_in_dim(seq_grad, me, axis=0, keepdims=False)
     token_grad = (own_grad[None, :] + route_sum).astype(bf16)

time: 307 us -> 275 us (0.90)
  local copies, waits for them, and re-layouts: 52.2 us -> 32.9 us
  blocking collectives: 92.6 us -> 77.9 us
  waiting for transfers between devices: 98.7 us -> 91 us
  starting transfers between devices: 18.3 us -> 24.9 us
    all_gather x2 -> x1, waiting for transfers between devices: 43.9 us -> 0.01 us  [on_device(): every = lax.all_gather(stacked, 'dp', axis=2, tiled=True)]
    all_to_all x1 -> x2, waiting for transfers between devices: 45.7 us -> 81.9 us  [the longest x1 54.1 us: on_device(): lax.all_to_all(route_here, 'expert', split_axis=0, concat_axis=0, tiled=T...]
    gather x9 -> x0, local copies, waits for them, and re-layouts: 18.2 us -> none  [the longest x5 7.39 us: on_device(): slot_rank = jnp.take_along_axis(before, expert_ids, axis=1)]
    all_to_all x1, blocking collectives: 79.9 us -> 65.2 us  [on_device(): lax.all_to_all(outgoing, 'expert', split_axis=0, concat_axis=0, tiled=True)]
    all_to_all x1 -> x2, starting transfers between devices: 9.61 us -> 18.2 us  [the longest x1 13.9 us: on_device(): lax.all_to_all(spread, 'dp', split_axis=0, concat_axis=0, tiled=True)]
    concatenate x0 -> x2, local copies, waits for them, and re-layouts: none -> 4.69 us  [on_device(): jnp.concatenate([outgoing, pack_row(slot_gate, model_width)], axis=1)]
    another operation x2 -> x1, local copies, waits for them, and re-layouts: 5.98 us -> 2.69 us  [on_device(): down_full = every[2].reshape(local_experts, ff_width, model_width)]
  transfers between devices with their start and end apart: 4 -> 4, of which waited for: 3 -> 3; matrix products, arithmetic and copies ran while one was open for 5% -> 6% of each run, Pallas kernels for 0% -> 0%
where the time goes in v3:
time: 275 us; the launch traced here: 274 us
  waiting for transfers between devices  91 us (33%)
  blocking collectives  77.9 us (28%)
  local copies, waits for them, and re-layouts  32.9 us (12%)
  starting transfers between devices  24.9 us (9%)
  matrix products  22.3 us (8%)
  between operations  16.2 us (6%)
  other arithmetic  8.68 us (3%)
    all_to_all x1, blocking collectives, on_device(): lax.all_to_all(outgoing, 'expert', split_axis=0, concat_axis=0, tiled=True)  65.2 us
    all_to_all x1, waiting for transfers between devices, on_device(): lax.all_to_all(route_here, 'expert', split_axis=0, concat_axis=0, tiled=T...  54.1 us
    all_to_all x1, waiting for transfers between devices, on_device(): lax.all_to_all(spread, 'dp', split_axis=0, concat_axis=0, tiled=True)  27.8 us
    all_to_all x1, starting transfers between devices, on_device(): lax.all_to_all(spread, 'dp', split_axis=0, concat_axis=0, tiled=True)  13.9 us
    all_to_all x1, blocking collectives, on_device(): lax.all_to_all(copies, 'expert', split_axis=0, concat_axis=0, tiled=True)  12.7 us
    all_to_all x1, waiting for transfers between devices, on_device(): lax.all_to_all(partial / tok_rows, 'expert', split_axis=0, concat_axis=0,...  9.07 us
    all_to_all x1, starting transfers between devices, on_device(): lax.all_to_all(partial / tok_rows, 'expert', split_axis=0, concat_axis=0,...  6.68 us
  transfers between devices with their start and end apart: 4, of which 3 were waited for; matrix products, arithmetic and copies ran while one was open for 6% of the time, Pallas kernels for 0%

profile of v3, /device:TPU:1, one launch (start us, length us, event | category | flops | bytes accessed | tf_op | source)
XLA Modules:
  0.0 273.9 jit_solution(5623929682555565454)
XLA Ops:
  7.2 1.1 stack_reshape.3
  8.3 1.7 pad_maximum_fusion.2
  10.0 0.7 convert_reduce_fusion.1
  10.8 0.2 reduce_window_sum.11
  11.1 0.8 select_reduce_fusion.5
  11.9 0.2 select_reduce_fusion.3
  12.4 2.2 convolution_convert_fusion.1
  14.5 4.6 %concatenate.19 = bf16[32,2,17,1024]{3,1,0,2:T(2,128)(2,1)S(1)} reshape(bf16[64,17,1024]{2,0,1:T(8,128)(2,1)} %convolution_convert_fusion.1) | data formatting | bytes 4456448 | tf_op jit(solution)/shard_map/concatenate | solution.py:68
  19.2 2.1 pad_maximum_fusion
  21.3 65.2 %all_to_all.30 = bf16[32,2,18,1024]{3,1,2,0:T(2,128)(2,1)S(1)} all-to-all(bf16[32,2,18,1024]{3,1,2,0:T(2,128)(2,1)S(1)} %pad_maximum_fusion), channel_id=1, replica_groups=mesh['dp'=16,'expert'=32] {'expert'}, dimensions={0} | all-to-all | bytes 4718592 | tf_op jit(solution)/shard_map/all_to_all | solution.py:72
  86.7 0.7 copy.100
  87.4 3.0 %slice.58 = bf16[32,2,17,1024]{3,1,2,0:T(2,128)(2,1)} slice(bf16[32,2,18,1024]{3,1,2,0:T(2,128)(2,1)S(1)} %all_to_all.30), slice={[0:32], [0:2], [0:17], [0:1024]} | slice | bytes 4456448 | tf_op jit(solution)/shard_map/slice | solution.py:73
  90.4 1.4 slice-done.4
  91.8 2.7 reshape.98
  94.5 3.6 %fusion.10 = f32[2,384,32,17]{1,2,3,0:T(8,128)S(1)} fusion(bf16[32,2,17,1024]{3,1,2,0:T(2,128)(2,1)} %slice.58, bf16[3,2,1024,384]{3,2,1,0:T(8,128)(2,1)} %all-gather.2.cloned.1.call-done), kind=kOutput, calls=%fused_computation.16 | convolution fusion | flops 855638016 | bytes 5472256 | tf_op jit(solution)/shard_map/secd,edf->secf/dot_general | solution.py:75
  98.1 0.4 copy-done
  98.5 1.3 fusion.8
  99.9 0.7 copy-done.1
  100.5 1.4 fusion
  102.0 0.7 div.31
  102.7 6.7 %all-to-all-start.1 = ((f32[32,1,1024]{2,1,0:T(1,128)}), f32[32,1,1024]{2,1,0:T(1,128)S(1)}, u32[]{:S(2)}, u32[]{:S(2)}) async-start(f32[32,1,1024]{2,1,0:T(1,128)} %div.31), calls=%async_computation.1 | async-start | bytes 262144 | tf_op jit(solution)/shard_map/all_to_all | solution.py:86
  109.5 9.1 %all-to-all-done.1 = f32[32,1,1024]{2,1,0:T(1,128)S(1)} async-done(((f32[32,1,1024]{2,1,0:T(1,128)}), f32[32,1,1024]{2,1,0:T(1,128)S(1)}, u32[]{:S(2)}, u32[]{:S(2)}) %all-to-all-start.1) | async-done | bytes 131104 | tf_op jit(solution)/shard_map/all_to_all | solution.py:86
  118.8 12.7 %all_to_all.31 = f32[32,1,1024]{2,1,0:T(1,128)S(1)} all-to-all(f32[32,1,1024]{2,1,0:T(1,128)S(1)} %broadcast_in_dim.56), channel_id=1, replica_groups=mesh['dp'=16,'expert'=32] {'expert'}, dimensions={0} | all-to-all | bytes 262144 | tf_op jit(solution)/shard_map/all_to_all | solution.py:89
  131.5 0.1 fusion.51
  131.7 1.2 broadcast_in_dim.57
  132.9 13.9 %all-to-all-start.3 = ((bf16[16,32,1024]{2,1,0:T(8,128)(2,1)}), bf16[16,32,1024]{2,1,0:T(8,128)(2,1)S(1)}, u32[]{:S(2)}, u32[]{:S(2)}) async-start(bf16[16,32,1024]{2,1,0:T(8,128)(2,1)} %broadcast_in_dim.57), calls=%async_computation.3 | async-start | bytes 2097152 | tf_op jit(solution)/shard_map/all_to_all | solution.py:94
  146.9 27.8 %all-to-all-done.3 = bf16[16,32,1024]{2,1,0:T(8,128)(2,1)S(1)} async-done(((bf16[16,32,1024]{2,1,0:T(8,128)(2,1)}), bf16[16,32,1024]{2,1,0:T(8,128)(2,1)S(1)}, u32[]{:S(2)}, u32[]{:S(2)}) %all-to-all-start.3) | async-done | bytes 1048608 | tf_op jit(solution)/shard_map/all_to_all | solution.py:94
  174.7 0.9 select_reduce_fusion.1
  175.6 0.7 fusion.84
  176.4 0.3 copy-done.6
  176.7 0.8 constant_dynamic-slice_fusion.1
  177.5 1.0 copy.114
  178.6 1.6 fusion.53
  180.3 4.1 %fusion.2 = f32[2,384,32,17]{1,2,3,0:T(8,128)} fusion(f32[32,1024]{1,0:T(8,128)S(1)} %fusion.54, f32[32,2,17]{0,2,1:T(8,128)} %copy.100, bf16[2,384,1024,1]{2,1,0,3:T(8,128)(2,1)} %reshape.98), kind=kOutput, calls=%fused_computation.8 | convolution fusion | flops 857866240 | bytes 3379456 | tf_op jit(solution)/shard_map/secd,efd->secf/dot_general | solution.py:137
  184.4 0.5 fusion.1
  185.1 4.5 %fusion.23 = f32[2,1024,32,17]{1,2,3,0:T(8,128)S(1)} fusion(bf16[3,2,1024,384]{3,2,1,0:T(8,128)(2,1)} %all-gather.2.cloned.1.call-done, f32[2,384,32,17]{1,2,3,0:T(8,128)} %fusion.2, f32[2,384,32,17]{1,2,3,0:T(8,128)} %copy-done.13, f32[2,384,32,17]{1,2,3,0:T(8,128)} %copy-done.10), kind=kOutput, calls=%fused_computation.39 | convolution fusion | flops 859815936 | bytes 11042816 | tf_op jit(solution)/shard_map/secf,edf->secd/dot_general | solution.py:140
  189.8 0.5 copy-done.12
  190.3 1.4 fusion.3
  191.7 0.2 pad_maximum_fusion.1
  191.9 3.8 %copy.105 = bf16[32,2,18,1024]{3,1,2,0:T(2,128)(2,1)} copy(bf16[32,2,18,1024]{3,0,2,1:T(8,128)(2,1)S(1)} %pad_maximum_fusion.1) | data formatting | bytes 4718592 | tf_op jit(solution)/shard_map/concatenate | solution.py:145
  195.8 4.3 %all-to-all-start.4 = ((bf16[32,2,18,1024]{3,1,2,0:T(2,128)(2,1)}), bf16[32,2,18,1024]{3,1,2,0:T(2,128)(2,1)S(1)}, u32[]{:S(2)}, u32[]{:S(2)}) async-start(bf16[32,2,18,1024]{3,1,2,0:T(2,128)(2,1)} %copy.105), calls=%async_computation.4 | async-start | bytes 4718592 | tf_op jit(solution)/shard_map/all_to_all | solution.py:146
  200.8 54.1 %all-to-all-done.4 = bf16[32,2,18,1024]{3,1,2,0:T(2,128)(2,1)S(1)} async-done(((bf16[32,2,18,1024]{3,1,2,0:T(2,128)(2,1)}), bf16[32,2,18,1024]{3,1,2,0:T(2,128)(2,1)S(1)}, u32[]{:S(2)}, u32[]{:S(2)}) %all-to-all-start.4) | async-done | bytes 2359328 | tf_op jit(solution)/shard_map/all_to_all | solution.py:146
  254.8 3.7 %copy.106 = bf16[32,2,18,1024]{3,1,0,2:T(2,128)(2,1)} copy(bf16[32,2,18,1024]{3,1,2,0:T(2,128)(2,1)S(1)} %all-to-all-done.4) | data formatting | bytes 4718592 | tf_op jit(solution)/shard_map/all_to_all | solution.py:146
  258.5 5.0 %reshape.94 = bf16[64,18,1024]{2,0,1:T(8,128)(2,1)S(1)} reshape(bf16[32,2,18,1024]{3,1,0,2:T(2,128)(2,1)} %copy.106) | data formatting | bytes 4718592 | tf_op jit(solution)/shard_map/reshape | solution.py:147
  263.6 1.3 fusion.30
  264.9 0.2 copy.115
  265.1 0.2 select_reduce_fusion.2
  265.3 0.6 select_reduce_fusion.4
  (68 shorter events, 1.6 us)
Async XLA Ops:
  7.2 5.2 %copy-start.2 = (bf16[128,1024]{1,0:T(8,128)(2,1)S(1)}, bf16[128,1024]{1,0:T(8,128)(2,1)}, u32[]{:S(2)}) copy-start(bf16[128,1024]{1,0:T(8,128)(2,1)} %param.7) | copy-start | bytes 786436
  7.2 83.2 %all-gather.2.cloned.1.call-start = ((), (), s32[]{:S(2)}) async-start(), calls=%async_computation.5 | async-start | bytes 5013504 | tf_op jit(solution)/shard_map/all_gather | solution.py:52
  11.1 1.2 copy-start.4
  90.4 1.4 slice-start.4
  91.8 6.3 %slice-start = ((s8[4718592]{0:T(1024)(128)(4,1)}), s8[524288]{0:T(1024)(128)(4,1)S(1)}, s32[]{:S(2)}) async-start(s8[4718592]{0:T(1024)(128)(4,1)} %bitcast.136), calls=%async_computation.6 | async-start | bytes 1048576
  94.5 3.6 %slice-start.1 = ((s8[4718592]{0:T(1024)(128)(4,1)}), s8[4194304]{0:T(1024)(128)(4,1)S(1)}, s32[]{:S(2)}) async-start(s8[4718592]{0:T(1024)(128)(4,1)} %bitcast.136), calls=%async_computation.7 | async-start | bytes 8388608
  94.5 4.0 %copy-start = (bf16[32,2,17,1024]{3,1,2,0:T(2,128)(2,1)S(1)}, bf16[32,2,17,1024]{3,1,2,0:T(2,128)(2,1)}, u32[]{:S(2)}) copy-start(bf16[32,2,17,1024]{3,1,2,0:T(2,128)(2,1)} %slice.58) | copy-start | bytes 6684676
  98.5 1.3 copy-start.10
  98.5 2.0 copy-start.1
  98.5 2.0 copy-start.8
  100.5 1.4 copy-start.13
  100.5 8.9 %copy-start.3 = (bf16[128,1024]{1,0:T(8,128)(2,1)S(1)}, bf16[128,1024]{1,0:T(8,128)(2,1)}, u32[]{:S(2)}) copy-start(bf16[128,1024]{1,0:T(8,128)(2,1)} %param.7) | copy-start | bytes 786436
  102.7 15.8 %all-to-all-start.1 = ((f32[32,1,1024]{2,1,0:T(1,128)}), f32[32,1,1024]{2,1,0:T(1,128)S(1)}, u32[]{:S(2)}, u32[]{:S(2)}) async-start(f32[32,1,1024]{2,1,0:T(1,128)} %div.31), calls=%async_computation.1 | async-start | bytes 262144 | tf_op jit(solution)/shard_map/all_to_all | solution.py:86
  109.4 37.3 %copy-start.9 = (s32[512]{0:T(512)S(1)}, s32[512]{0:T(512)}, u32[]{:S(2)}) copy-start(s32[512]{0:T(512)} %param.13) | copy-start | bytes 6148
  132.9 41.8 %all-to-all-start.3 = ((bf16[16,32,1024]{2,1,0:T(8,128)(2,1)}), bf16[16,32,1024]{2,1,0:T(8,128)(2,1)S(1)}, u32[]{:S(2)}, u32[]{:S(2)}) async-start(bf16[16,32,1024]{2,1,0:T(8,128)(2,1)} %broadcast_in_dim.57), calls=%async_computation.3 | async-start | bytes 2097152 | tf_op jit(solution)/shard_map/all_to_all | solution.py:94
  175.6 1.1 copy-start.6
  184.4 5.3 %slice-start.2 = ((s8[4718592]{0:T(1024)(128)(4,1)}), s8[524288]{0:T(1024)(128)(4,1)S(1)}, s32[]{:S(2)}) async-start(s8[4718592]{0:T(1024)(128)(4,1)} %bitcast.138), calls=%async_computation.8 | async-start | bytes 1048576
  185.1 4.6 %slice-start.3 = ((s8[4718592]{0:T(1024)(128)(4,1)}), s8[4194304]{0:T(1024)(128)(4,1)S(1)}, s32[]{:S(2)}) async-start(s8[4718592]{0:T(1024)(128)(4,1)} %bitcast.138), calls=%async_computation.9 | async-start | bytes 8388608
  185.1 4.7 %copy-start.11 = (f32[2,384,32,17]{1,2,3,0:T(8,128)S(1)}, f32[2,384,32,17]{1,2,3,0:T(8,128)}, u32[]{:S(2)}) copy-start(f32[2,384,32,17]{1,2,3,0:T(8,128)} %copy-done.10) | copy-start | bytes 5013508
  185.1 5.2 %copy-start.12 = (f32[2,384,32,17]{1,2,3,0:T(8,128)S(1)}, f32[2,384,32,17]{1,2,3,0:T(8,128)}, u32[]{:S(2)}) copy-start(f32[2,384,32,17]{1,2,3,0:T(8,128)} %fusion.2) | copy-start | bytes 5013508
  195.8 59.1 %all-to-all-start.4 = ((bf16[32,2,18,1024]{3,1,2,0:T(2,128)(2,1)}), bf16[32,2,18,1024]{3,1,2,0:T(2,128)(2,1)S(1)}, u32[]{:S(2)}, u32[]{:S(2)}) async-start(bf16[32,2,18,1024]{3,1,2,0:T(2,128)(2,1)} %copy.105), calls=%async_computation.4 | async-start | bytes 4718592 | tf_op jit(solution)/shard_map/all_to_all | solution.py:146
  258.5 5.1 %copy-start.5 = (s32[64,128]{1,0:T(8,128)S(1)}, s32[64,128]{1,0:T(8,128)}, u32[]{:S(2)}) copy-start(s32[64,128]{1,0:T(8,128)} %copy-done.4) | copy-start | bytes 98308
  263.6 1.7 copy-start.7
Sparse Core Ops, SparseCore 0:
  10.2 52.0 all-gather.1

commit v4 on v3

--- a/solution.py
+++ b/solution.py
@@ -32,8 +32,7 @@
 def pack_row(values, width):
     pieces = split3(values)
     pad = width - pieces.shape[-1]
-    pieces = jnp.pad(pieces, [(0, 0)] * (pieces.ndim - 1) + [(0, pad)])
-    return pieces[..., None, :]
+    return jnp.pad(pieces, [(0, 0)] * (pieces.ndim - 1) + [(0, pad)])
 
 
 def on_device(tokens, expert_ids, gate_values, w_gate, w_up, w_down, partner):
@@ -62,16 +61,15 @@
     slot_rank = jnp.sum(jnp.where(matches, before[:, None, :], 0), axis=2, dtype=jnp.int32)
     slot_iota = jnp.arange(capacity, dtype=jnp.int32)
     onehot = (chosen.T[:, None, :] == 1) & (before.T[:, None, :] == slot_iota[None, :, None])
-    placer = onehot.astype(bf16)
+    placer = jnp.pad(onehot.astype(bf16), ((0, 0), (0, 1), (0, 0)))
     slot_gate = jnp.sum(jnp.where(onehot, chosen_gate.T[:, None, :], 0.0), axis=2)
     outgoing = jnp.einsum("ect,td->ecd", placer, tokens, preferred_element_type=f32).astype(bf16)
-    outgoing = jnp.concatenate([outgoing, pack_row(slot_gate, model_width)], axis=1)
+    outgoing = outgoing.at[:, capacity, :].set(pack_row(slot_gate, model_width))
     outgoing = outgoing.reshape(group, local_experts, capacity + 1, model_width)
-    placer_flat = placer.reshape(slot_total, tok_rows)
 
     arrived = lax.all_to_all(outgoing, "expert", split_axis=0, concat_axis=0, tiled=True)
-    rows_in = arrived[:, :, :capacity, :]
-    gates = join3(arrived[:, :, capacity, :], capacity)
+    rows_in = arrived
+    gates = jnp.pad(join3(arrived[:, :, capacity, :], capacity), ((0, 0), (0, 0), (0, 1)))
     pre_gate = jnp.einsum("secd,edf->secf", rows_in, gate_full, preferred_element_type=f32)
     pre_up = jnp.einsum("secd,edf->secf", rows_in, up_full, preferred_element_type=f32)
     activated, derivative = silu_parts(pre_gate)
@@ -142,15 +140,14 @@
         route_here
         + jnp.einsum("secf,edf->secd", up_side, up_full, preferred_element_type=f32)
     ).astype(bf16)
-    route_here = jnp.concatenate([route_here, pack_row(slot_dots, model_width)], axis=2)
+    route_here = route_here.at[:, :, capacity, :].set(pack_row(slot_dots[:, :, :capacity], model_width))
     returned = lax.all_to_all(route_here, "expert", split_axis=0, concat_axis=0, tiled=True)
     returned = returned.reshape(experts, capacity + 1, model_width)
 
-    route_rows = returned[:, :capacity, :].reshape(slot_total, model_width)
     slot_grads = join3(returned[:, capacity, :], capacity)
     token_slot_grads = jnp.sum(jnp.where(onehot, slot_grads[:, :, None], 0.0), axis=1).T
     gate_grad = jnp.sum(jnp.where(matches, token_slot_grads[:, None, :], 0.0), axis=2)
-    route_sum = jnp.einsum("st,sd->td", placer_flat, route_rows, preferred_element_type=f32)
+    route_sum = jnp.einsum("ect,ecd->td", placer, returned, preferred_element_type=f32)
     own_grad = lax.dynamic_index_in_dim(seq_grad, me, axis=0, keepdims=False)
     token_grad = (own_grad[None, :] + route_sum).astype(bf16)
     return (contrast_loss, token_grad, gate_grad)

time: 275 us -> 276 us (level)
    concatenate x3 -> x0, local copies, waits for them, and re-layouts: 8.53 us -> none  [the longest x2 4.69 us: on_device(): jnp.concatenate([outgoing, pack_row(slot_gate, model_width)], axis=1)]
    reshape x0 -> x2, local copies, waits for them, and re-layouts: none -> 5.65 us  [on_device(): outgoing = outgoing.reshape(group, local_experts, capacity + 1, model_width)]
    scatter x0 -> x2, local copies, waits for them, and re-layouts: none -> 3.85 us  [the longest x1 3.84 us: on_device(): route_here.at[:, :, capacity, :]]
    slice x2 -> x0, local copies, waits for them, and re-layouts: 3.05 us -> none  [the longest x1 2.96 us: on_device(): rows_in = arrived[:, :, :capacity, :]]
  transfers between devices with their start and end apart: 4 -> 4, of which waited for: 3 -> 3; matrix products, arithmetic and copies ran while one was open for 6% -> 4% of each run, Pallas kernels for 0% -> 0%
where the time goes in v4:
time: 276 us; the launch traced here: 275 us
  waiting for transfers between devices  89.1 us (32%)
  blocking collectives  78 us (28%)
  local copies, waits for them, and re-layouts  35.6 us (13%)
  starting transfers between devices  25 us (9%)
  matrix products  23.1 us (8%)
  between operations  16.3 us (6%)
  other arithmetic  7.7 us (3%)
    all_to_all x1, blocking collectives, on_device(): lax.all_to_all(outgoing, 'expert', split_axis=0, concat_axis=0, tiled=True)  65.2 us
    all_to_all x1, waiting for transfers between devices, on_device(): lax.all_to_all(route_here, 'expert', split_axis=0, concat_axis=0, tiled=T...  53.4 us
    all_to_all x1, waiting for transfers between devices, on_device(): lax.all_to_all(spread, 'dp', split_axis=0, concat_axis=0, tiled=True)  26.8 us
    all_to_all x1, starting transfers between devices, on_device(): lax.all_to_all(spread, 'dp', split_axis=0, concat_axis=0, tiled=True)  13.8 us
    all_to_all x1, blocking collectives, on_device(): lax.all_to_all(copies, 'expert', split_axis=0, concat_axis=0, tiled=True)  12.7 us
    all_to_all x1, waiting for transfers between devices, on_device(): lax.all_to_all(partial / tok_rows, 'expert', split_axis=0, concat_axis=0,...  8.91 us
    all_to_all x1, starting transfers between devices, on_device(): lax.all_to_all(partial / tok_rows, 'expert', split_axis=0, concat_axis=0,...  6.86 us
    reshape x2, local copies, waits for them, and re-layouts, on_device(): outgoing = outgoing.reshape(group, local_experts, capacity + 1, model_width)  5.65 us
  transfers between devices with their start and end apart: 4, of which 3 were waited for; matrix products, arithmetic and copies ran while one was open for 4% of the time, Pallas kernels for 0%

profile of v4, /device:TPU:1, one launch (start us, length us, event | category | flops | bytes accessed | tf_op | source)
XLA Modules:
  0.0 274.7 jit_solution(7104770918527226808)
XLA Ops:
  7.2 1.1 stack_reshape.3
  8.3 1.7 pad_maximum_fusion
  10.0 0.7 convert_reduce_fusion.1
  10.9 0.2 reduce_window_sum.11
  11.1 0.8 select_reduce_fusion.5
  11.9 0.2 select_reduce_fusion.3
  12.4 0.7 copy-done.2
  13.1 0.8 convolution_convert_fusion.1
  13.9 2.4 reshape.158
  16.3 3.3 %copy.96 = bf16[32,2,18,1024]{3,1,2,0:T(2,128)(2,1)S(1)} copy(bf16[32,2,18,1024]{3,1,0,2:T(2,128)(2,1)} %reshape.158) | data formatting | bytes 4718592 | tf_op jit(solution)/shard_map/reshape | solution.py:68
  19.5 65.2 %all_to_all.30 = bf16[32,2,18,1024]{3,1,2,0:T(2,128)(2,1)S(1)} all-to-all(bf16[32,2,18,1024]{3,1,2,0:T(2,128)(2,1)S(1)} %copy.96), channel_id=1, replica_groups=mesh['dp'=16,'expert'=32] {'expert'}, dimensions={0} | all-to-all | bytes 4718592 | tf_op jit(solution)/shard_map/all_to_all | solution.py:70
  84.8 0.7 copy.97
  85.7 0.6 pad.26.clone
  86.3 2.7 slice.97
  89.1 4.3 %reshape.165 = bf16[2,384,1024,1]{2,1,0,3:T(8,128)(2,1)} reshape(bf16[1,2,1024,384]{3,2,1,0:T(8,128)(2,1)} %slice.97) | data formatting | bytes 3145728 | tf_op jit(solution)/shard_map/reshape;squeeze | solution.py:54
  93.3 2.9 %fusion.18 = f32[2,384,32,18]{1,2,3,0:T(8,128)S(1)} fusion(bf16[3,2,1024,384]{3,2,1,0:T(8,128)(2,1)} %all-gather.2.cloned.1.call-done, bf16[32,2,18,1024]{3,1,2,0:T(2,128)(2,1)S(1)} %all_to_all.30), kind=kOutput, calls=%fused_computation.32 | convolution fusion | flops 905969664 | bytes 5701632 | tf_op jit(solution)/shard_map/secd,edf->secf/dot_general | solution.py:73
  96.3 3.6 %fusion.19 = f32[2,384,32,18]{1,2,3,0:T(8,128)S(1)} fusion(bf16[3,2,1024,384]{3,2,1,0:T(8,128)(2,1)} %all-gather.2.cloned.1.call-done, bf16[32,2,18,1024]{3,1,2,0:T(2,128)(2,1)S(1)} %all_to_all.30), kind=kOutput, calls=%fused_computation.33 | convolution fusion | flops 905969664 | bytes 5701632 | tf_op jit(solution)/shard_map/secd,edf->secf/dot_general | solution.py:74
  99.9 1.5 fusion
  101.4 0.7 div.31
  102.2 6.9 %all-to-all-start.1 = ((f32[32,1,1024]{2,1,0:T(1,128)}), f32[32,1,1024]{2,1,0:T(1,128)S(1)}, u32[]{:S(2)}, u32[]{:S(2)}) async-start(f32[32,1,1024]{2,1,0:T(1,128)} %div.31), calls=%async_computation.1 | async-start | bytes 262144 | tf_op jit(solution)/shard_map/all_to_all | solution.py:84
  109.1 8.9 %all-to-all-done.1 = f32[32,1,1024]{2,1,0:T(1,128)S(1)} async-done(((f32[32,1,1024]{2,1,0:T(1,128)}), f32[32,1,1024]{2,1,0:T(1,128)S(1)}, u32[]{:S(2)}, u32[]{:S(2)}) %all-to-all-start.1) | async-done | bytes 131104 | tf_op jit(solution)/shard_map/all_to_all | solution.py:84
  118.2 12.7 %all_to_all.31 = f32[32,1,1024]{2,1,0:T(1,128)S(1)} all-to-all(f32[32,1,1024]{2,1,0:T(1,128)S(1)} %broadcast_in_dim.54), channel_id=1, replica_groups=mesh['dp'=16,'expert'=32] {'expert'}, dimensions={0} | all-to-all | bytes 262144 | tf_op jit(solution)/shard_map/all_to_all | solution.py:87
  131.2 1.1 broadcast_in_dim.55
  132.3 13.8 %all-to-all-start.3 = ((bf16[16,32,1024]{2,1,0:T(8,128)(2,1)}), bf16[16,32,1024]{2,1,0:T(8,128)(2,1)S(1)}, u32[]{:S(2)}, u32[]{:S(2)}) async-start(bf16[16,32,1024]{2,1,0:T(8,128)(2,1)} %broadcast_in_dim.55), calls=%async_computation.3 | async-start | bytes 2097152 | tf_op jit(solution)/shard_map/all_to_all | solution.py:92
  146.1 0.6 dynamic_slice.18
  146.7 0.5 iota_add_fusion
  147.3 26.8 %all-to-all-done.3 = bf16[16,32,1024]{2,1,0:T(8,128)(2,1)S(1)} async-done(((bf16[16,32,1024]{2,1,0:T(8,128)(2,1)}), bf16[16,32,1024]{2,1,0:T(8,128)(2,1)S(1)}, u32[]{:S(2)}, u32[]{:S(2)}) %all-to-all-start.3) | async-done | bytes 1048608 | tf_op jit(solution)/shard_map/all_to_all | solution.py:92
  174.1 0.9 select_reduce_fusion.1
  175.0 0.7 fusion.80
  175.7 0.6 dynamic_slice.17
  176.3 0.8 constant_dynamic-slice_fusion.1
  177.2 1.7 copy.110
  178.9 1.8 fusion.45
  180.6 0.7 broadcast_multiply_fusion.1
  181.5 2.8 %fusion.2 = f32[2,384,32,18]{1,2,3,0:T(8,128)} fusion(f32[32,1024]{1,0:T(8,128)S(1)} %fusion.46, f32[32,2,18]{0,2,1:T(8,128)S(1)} %copy-done.12, bf16[2,384,1024,1]{2,1,0,3:T(8,128)(2,1)S(1)} %copy-done.1), kind=kOutput, calls=%fused_computation.6 | convolution fusion | flops 908328960 | bytes 3478016 | tf_op jit(solution)/shard_map/secd,efd->secf/dot_general | solution.py:135
  184.2 0.5 fusion.1
  184.9 4.7 %fusion.17 = f32[2,1024,32,18]{1,2,3,0:T(8,128)S(1)} fusion(bf16[3,2,1024,384]{3,2,1,0:T(8,128)(2,1)} %all-gather.2.cloned.1.call-done, f32[2,384,32,18]{1,2,3,0:T(8,128)} %fusion.2, f32[2,384,32,18]{1,2,3,0:T(8,128)} %copy-done.18, f32[2,384,32,18]{1,2,3,0:T(8,128)} %copy-done.15), kind=kOutput, calls=%fused_computation.31 | convolution fusion | flops 910393344 | bytes 11599872 | tf_op jit(solution)/shard_map/secf,edf->secd/dot_general | solution.py:138
  189.6 2.9 %fusion.3 = bf16[32,2,18,1024]{3,0,2,1:T(8,128)(2,1)S(1)} fusion(f32[2,1024,32,18]{1,2,3,0:T(8,128)S(1)} %fusion.17, bf16[3,2,1024,384]{3,2,1,0:T(8,128)(2,1)} %all-gather.2.cloned.1.call-done, f32[2,384,32,18]{1,2,3,0:T(8,128)S(1)} %copy-done.17, f32[2,384,32,18]{1,2,3,0:T(8,128)S(1)} %copy-done.16), kind=kOutput, calls=%fused_computation.7 | convolution fusion | flops 910983168 | bytes 12189696 | tf_op jit(solution)/shard_map/secf,edf->secd/dot_general | solution.py:141
  192.6 3.8 %copy.103 = bf16[32,2,18,1024]{3,1,2,0:T(2,128)(2,1)} copy(bf16[32,2,18,1024]{3,0,2,1:T(8,128)(2,1)S(1)} %fusion.42) | data formatting | bytes 4718592 | tf_op jit(solution)/shard_map/scatter | solution.py:143
  196.5 4.3 %all-to-all-start.4 = ((bf16[32,2,18,1024]{3,1,2,0:T(2,128)(2,1)}), bf16[32,2,18,1024]{3,1,2,0:T(2,128)(2,1)S(1)}, u32[]{:S(2)}, u32[]{:S(2)}) async-start(bf16[32,2,18,1024]{3,1,2,0:T(2,128)(2,1)} %copy.103), calls=%async_computation.4 | async-start | bytes 4718592 | tf_op jit(solution)/shard_map/all_to_all | solution.py:144
  201.4 0.8 constant_dynamic-slice_fusion
  202.2 53.4 %all-to-all-done.4 = bf16[32,2,18,1024]{3,1,2,0:T(2,128)(2,1)S(1)} async-done(((bf16[32,2,18,1024]{3,1,2,0:T(2,128)(2,1)}), bf16[32,2,18,1024]{3,1,2,0:T(2,128)(2,1)S(1)}, u32[]{:S(2)}, u32[]{:S(2)}) %all-to-all-start.4) | async-done | bytes 2359328 | tf_op jit(solution)/shard_map/all_to_all | solution.py:144
  255.5 3.7 %copy.104 = bf16[32,2,18,1024]{3,1,0,2:T(2,128)(2,1)} copy(bf16[32,2,18,1024]{3,1,2,0:T(2,128)(2,1)S(1)} %all-to-all-done.4) | data formatting | bytes 4718592 | tf_op jit(solution)/shard_map/all_to_all | solution.py:144
  259.2 5.1 %reshape.161 = bf16[64,18,1024]{2,0,1:T(8,128)(2,1)S(1)} reshape(bf16[32,2,18,1024]{3,1,0,2:T(2,128)(2,1)} %copy.104) | data formatting | bytes 4718592 | tf_op jit(solution)/shard_map/reshape | solution.py:145
  264.4 1.3 fusion.21
  265.7 0.2 copy.112
  265.9 0.2 select_reduce_fusion.2
  266.1 0.6 select_reduce_fusion.4
  (66 shorter events, 1.5 us)
Async XLA Ops:
  7.2 5.9 %copy-start.4 = (bf16[128,1024]{1,0:T(8,128)(2,1)S(1)}, bf16[128,1024]{1,0:T(8,128)(2,1)}, u32[]{:S(2)}) copy-start(bf16[128,1024]{1,0:T(8,128)(2,1)} %param.11) | copy-start | bytes 786436
  7.2 79.1 %all-gather.2.cloned.1.call-start = ((), (), s32[]{:S(2)}) async-start(), calls=%async_computation.5 | async-start | bytes 5013504 | tf_op jit(solution)/shard_map/all_gather | solution.py:51
  11.1 1.2 copy-start.7
  12.4 0.7 copy-start.2
  96.2 3.6 %copy-start.15 = (f32[2,384,32,18]{1,2,3,0:T(8,128)}, f32[2,384,32,18]{1,2,3,0:T(8,128)S(1)}, u32[]{:S(2)}) copy-start(f32[2,384,32,18]{1,2,3,0:T(8,128)S(1)} %fusion.18) | copy-start | bytes 5308420
  96.3 3.6 %copy-start = (bf16[2,384,1024,1]{2,1,0,3:T(8,128)(2,1)S(1)}, bf16[2,384,1024,1]{2,1,0,3:T(8,128)(2,1)}, u32[]{:S(2)}) copy-start(bf16[2,384,1024,1]{2,1,0,3:T(8,128)(2,1)} %reshape.165) | copy-start | bytes 4718596
  96.3 3.6 %copy-start.11 = (f32[32,2,18]{0,2,1:T(8,128)S(1)}, f32[32,2,18]{0,2,1:T(8,128)}, u32[]{:S(2)}) copy-start(f32[32,2,18]{0,2,1:T(8,128)} %pad.26.clone) | copy-start | bytes 13828
  99.9 1.5 copy-start.18
  99.9 9.2 %copy-start.5 = (bf16[128,1024]{1,0:T(8,128)(2,1)S(1)}, bf16[128,1024]{1,0:T(8,128)(2,1)}, u32[]{:S(2)}) copy-start(bf16[128,1024]{1,0:T(8,128)(2,1)} %param.11) | copy-start | bytes 786436
  102.2 15.8 %all-to-all-start.1 = ((f32[32,1,1024]{2,1,0:T(1,128)}), f32[32,1,1024]{2,1,0:T(1,128)S(1)}, u32[]{:S(2)}, u32[]{:S(2)}) async-start(f32[32,1,1024]{2,1,0:T(1,128)} %div.31), calls=%async_computation.1 | async-start | bytes 262144 | tf_op jit(solution)/shard_map/all_to_all | solution.py:84
  130.9 15.2 %copy-start.13 = (s32[512]{0:T(512)S(1)}, s32[512]{0:T(512)}, u32[]{:S(2)}) copy-start(s32[512]{0:T(512)} %param.17) | copy-start | bytes 6148
  131.1 43.9 %copy-start.14 = (f32[32]{0:T(128)}, f32[32]{0:T(128)S(1)}, u32[]{:S(2)}) copy-start(f32[32]{0:T(128)S(1)} %fusion.43) | copy-start | bytes 388
  132.3 41.8 %all-to-all-start.3 = ((bf16[16,32,1024]{2,1,0:T(8,128)(2,1)}), bf16[16,32,1024]{2,1,0:T(8,128)(2,1)S(1)}, u32[]{:S(2)}, u32[]{:S(2)}) async-start(bf16[16,32,1024]{2,1,0:T(8,128)(2,1)} %broadcast_in_dim.55), calls=%async_computation.3 | async-start | bytes 2097152 | tf_op jit(solution)/shard_map/all_to_all | solution.py:92
  175.0 1.3 copy-start.9
  178.8 2.6 copy-start.1
  178.9 2.6 copy-start.12
  181.4 2.8 %copy-start.6 = (f32[32,1024]{1,0:T(8,128)}, f32[32,1024]{1,0:T(8,128)S(1)}, u32[]{:S(2)}) copy-start(f32[32,1024]{1,0:T(8,128)S(1)} %fusion.46) | copy-start | bytes 393220
  184.9 4.7 %copy-start.16 = (f32[2,384,32,18]{1,2,3,0:T(8,128)S(1)}, f32[2,384,32,18]{1,2,3,0:T(8,128)}, u32[]{:S(2)}) copy-start(f32[2,384,32,18]{1,2,3,0:T(8,128)} %copy-done.15) | copy-start | bytes 5308420
  184.9 4.7 %copy-start.17 = (f32[2,384,32,18]{1,2,3,0:T(8,128)S(1)}, f32[2,384,32,18]{1,2,3,0:T(8,128)}, u32[]{:S(2)}) copy-start(f32[2,384,32,18]{1,2,3,0:T(8,128)} %fusion.2) | copy-start | bytes 5308420
  196.5 59.1 %all-to-all-start.4 = ((bf16[32,2,18,1024]{3,1,2,0:T(2,128)(2,1)}), bf16[32,2,18,1024]{3,1,2,0:T(2,128)(2,1)S(1)}, u32[]{:S(2)}, u32[]{:S(2)}) async-start(bf16[32,2,18,1024]{3,1,2,0:T(2,128)(2,1)} %copy.103), calls=%async_computation.4 | async-start | bytes 4718592 | tf_op jit(solution)/shard_map/all_to_all | solution.py:144
  259.2 5.1 %copy-start.3 = (pred[64,17,128]{2,0,1:T(32,128)(4,1)S(1)}, pred[64,17,128]{2,0,1:T(32,128)(4,1)}, u32[]{:S(2)}) copy-start(pred[64,17,128]{2,0,1:T(32,128)(4,1)} %copy-done.2) | copy-start | bytes 417796
  264.3 1.5 copy-start.8
  264.3 1.7 copy-start.10
Sparse Core Ops, SparseCore 0:
  10.2 52.0 all-gather.1

commit v5 on v4

--- a/solution.py
+++ b/solution.py
@@ -63,18 +63,20 @@
     onehot = (chosen.T[:, None, :] == 1) & (before.T[:, None, :] == slot_iota[None, :, None])
     placer = jnp.pad(onehot.astype(bf16), ((0, 0), (0, 1), (0, 0)))
     slot_gate = jnp.sum(jnp.where(onehot, chosen_gate.T[:, None, :], 0.0), axis=2)
-    outgoing = jnp.einsum("ect,td->ecd", placer, tokens, preferred_element_type=f32).astype(bf16)
-    outgoing = outgoing.at[:, capacity, :].set(pack_row(slot_gate, model_width))
-    outgoing = outgoing.reshape(group, local_experts, capacity + 1, model_width)
+    placer = placer.reshape(group, local_experts, capacity + 1, tok_rows).transpose(0, 2, 1, 3)
+    outgoing = jnp.einsum("jcet,td->jced", placer, tokens, preferred_element_type=f32).astype(bf16)
+    gate_row = pack_row(slot_gate, model_width).reshape(group, local_experts, model_width)
+    outgoing = outgoing.at[:, capacity, :, :].set(gate_row)
 
     arrived = lax.all_to_all(outgoing, "expert", split_axis=0, concat_axis=0, tiled=True)
     rows_in = arrived
-    gates = jnp.pad(join3(arrived[:, :, capacity, :], capacity), ((0, 0), (0, 0), (0, 1)))
-    pre_gate = jnp.einsum("secd,edf->secf", rows_in, gate_full, preferred_element_type=f32)
-    pre_up = jnp.einsum("secd,edf->secf", rows_in, up_full, preferred_element_type=f32)
+    gates = jnp.swapaxes(join3(arrived[:, capacity, :, :], capacity), 1, 2)
+    gates = jnp.pad(gates, ((0, 0), (0, 1), (0, 0)))
+    pre_gate = jnp.einsum("sced,edf->scef", rows_in, gate_full, preferred_element_type=f32)
+    pre_up = jnp.einsum("sced,edf->scef", rows_in, up_full, preferred_element_type=f32)
     activated, derivative = silu_parts(pre_gate)
     hidden = (activated * pre_up).astype(bf16)
-    expert_out = jnp.einsum("secf,efd->secd", hidden, down_full, preferred_element_type=f32).astype(
+    expert_out = jnp.einsum("scef,efd->sced", hidden, down_full, preferred_element_type=f32).astype(
         bf16
     )
     out_f32 = expert_out.astype(f32)
@@ -132,22 +134,22 @@
 
     slot_dots = jnp.sum(out_f32 * seq_grad[:, None, None, :], axis=3)
     out_grad = (gates[..., None] * seq_grad[:, None, None, :]).astype(bf16)
-    hidden_grad = jnp.einsum("secd,efd->secf", out_grad, down_full, preferred_element_type=f32)
+    hidden_grad = jnp.einsum("sced,efd->scef", out_grad, down_full, preferred_element_type=f32)
     gate_side = (hidden_grad * pre_up * derivative).astype(bf16)
     up_side = (hidden_grad * activated).astype(bf16)
-    route_here = jnp.einsum("secf,edf->secd", gate_side, gate_full, preferred_element_type=f32)
+    route_here = jnp.einsum("scef,edf->sced", gate_side, gate_full, preferred_element_type=f32)
     route_here = (
         route_here
-        + jnp.einsum("secf,edf->secd", up_side, up_full, preferred_element_type=f32)
+        + jnp.einsum("scef,edf->sced", up_side, up_full, preferred_element_type=f32)
     ).astype(bf16)
-    route_here = route_here.at[:, :, capacity, :].set(pack_row(slot_dots[:, :, :capacity], model_width))
+    grad_row = pack_row(jnp.swapaxes(slot_dots[:, :capacity, :], 1, 2), model_width)
+    route_here = route_here.at[:, capacity, :, :].set(grad_row)
     returned = lax.all_to_all(route_here, "expert", split_axis=0, concat_axis=0, tiled=True)
-    returned = returned.reshape(experts, capacity + 1, model_width)
 
-    slot_grads = join3(returned[:, capacity, :], capacity)
+    slot_grads = join3(returned[:, capacity, :, :], capacity).reshape(experts, capacity)
     token_slot_grads = jnp.sum(jnp.where(onehot, slot_grads[:, :, None], 0.0), axis=1).T
     gate_grad = jnp.sum(jnp.where(matches, token_slot_grads[:, None, :], 0.0), axis=2)
-    route_sum = jnp.einsum("ect,ecd->td", placer, returned, preferred_element_type=f32)
+    route_sum = jnp.einsum("jcet,jced->td", placer, returned, preferred_element_type=f32)
     own_grad = lax.dynamic_index_in_dim(seq_grad, me, axis=0, keepdims=False)
     token_grad = (own_grad[None, :] + route_sum).astype(bf16)
     return (contrast_loss, token_grad, gate_grad)

time: 276 us -> 261 us (0.946)
  local copies, waits for them, and re-layouts: 35.6 us -> 23 us
    reshape x3 -> x0, local copies, waits for them, and re-layouts: 10.7 us -> none  [the longest x2 5.65 us: on_device(): outgoing = outgoing.reshape(group, local_experts, capacity + 1, model_width)]
    all_to_all x1, local copies, waits for them, and re-layouts: 3.71 us -> 0.71 us  [on_device(): lax.all_to_all(route_here, 'expert', split_axis=0, concat_axis=0, tiled=T...]
    scatter x2 -> x3, local copies, waits for them, and re-layouts: 3.85 us -> 6.3 us  [the longest x1 3.84 us: on_device(): route_here = route_here.at[:, capacity, :, :].set(grad_row)]
  transfers between devices with their start and end apart: 4 -> 4, of which waited for: 3 -> 3; matrix products, arithmetic and copies ran while one was open for 4% -> 3% of each run, Pallas kernels for 0% -> 0%
where the time goes in v5:
time: 261 us; the launch traced here: 260 us
  waiting for transfers between devices  89.5 us (34%)
  blocking collectives  77.9 us (30%)
  starting transfers between devices  24.7 us (9%)
  local copies, waits for them, and re-layouts  23 us (9%)
  matrix products  20.9 us (8%)
  between operations  16.3 us (6%)
  other arithmetic  8.14 us (3%)
    all_to_all x1, blocking collectives, on_device(): lax.all_to_all(outgoing, 'expert', split_axis=0, concat_axis=0, tiled=True)  65.2 us
    all_to_all x1, waiting for transfers between devices, on_device(): lax.all_to_all(route_here, 'expert', split_axis=0, concat_axis=0, tiled=T...  53.6 us
    all_to_all x1, waiting for transfers between devices, on_device(): lax.all_to_all(spread, 'dp', split_axis=0, concat_axis=0, tiled=True)  26.8 us
    all_to_all x1, starting transfers between devices, on_device(): lax.all_to_all(spread, 'dp', split_axis=0, concat_axis=0, tiled=True)  13.9 us
    all_to_all x1, blocking collectives, on_device(): lax.all_to_all(copies, 'expert', split_axis=0, concat_axis=0, tiled=True)  12.7 us
    all_to_all x1, waiting for transfers between devices, on_device(): lax.all_to_all(partial / tok_rows, 'expert', split_axis=0, concat_axis=0,...  9.09 us
    all_to_all x1, starting transfers between devices, on_device(): lax.all_to_all(partial / tok_rows, 'expert', split_axis=0, concat_axis=0,...  6.68 us
  transfers between devices with their start and end apart: 4, of which 3 were waited for; matrix products, arithmetic and copies ran while one was open for 3% of the time, Pallas kernels for 0%

profile of v5, /device:TPU:1, one launch (start us, length us, event | category | flops | bytes accessed | tf_op | source)
XLA Modules:
  0.0 260.3 jit_solution(15015142571759153449)
XLA Ops:
  7.2 1.1 stack_reshape.3
  8.3 1.7 pad_maximum_fusion
  10.0 0.7 convert_reduce_fusion.1
  10.9 0.2 reduce_window_sum.11
  11.1 0.8 select_reduce_fusion.5
  11.9 0.3 select_reduce_fusion.3
  12.5 0.2 fusion.28
  12.8 0.8 convolution_convert_fusion.1
  13.6 2.4 copy.124
  16.0 65.2 %all_to_all.30 = bf16[32,18,2,1024]{3,2,1,0:T(2,128)(2,1)S(1)} all-to-all(bf16[32,18,2,1024]{3,2,1,0:T(2,128)(2,1)S(1)} %copy.124), channel_id=1, replica_groups=mesh['dp'=16,'expert'=32] {'expert'}, dimensions={0} | all-to-all | bytes 4718592 | tf_op jit(solution)/shard_map/all_to_all | solution.py:71
  81.3 1.4 copy-done
  83.0 0.6 pad.23.clone
  83.6 1.4 slice-done.4
  85.0 2.8 %reshape.167 = bf16[2,384,1024,1]{2,1,0,3:T(8,128)(2,1)} reshape(bf16[1,2,1024,384]{3,2,1,0:T(8,128)(2,1)S(1)} %slice-done.4) | data formatting | bytes 3145728 | tf_op jit(solution)/shard_map/reshape;squeeze | solution.py:54
  87.8 3.8 %fusion.8 = f32[2,384,32,18]{1,2,3,0:T(8,128)S(1)} fusion(bf16[32,18,2,1024]{3,2,1,0:T(2,128)(2,1)} %copy-done, bf16[3,2,1024,384]{3,2,1,0:T(8,128)(2,1)} %all-gather.2.cloned.1.call-done), kind=kOutput, calls=%fused_computation.12 | convolution fusion | flops 905969664 | bytes 5701632 | tf_op jit(solution)/shard_map/sced,edf->scef/dot_general | solution.py:75
  91.6 0.3 copy-done.1
  91.9 1.6 fusion.6
  93.5 0.5 copy-done.2
  94.0 1.5 fusion
  95.5 0.7 div.31
  96.3 6.7 %all-to-all-start.1 = ((f32[32,1,1024]{2,1,0:T(1,128)}), f32[32,1,1024]{2,1,0:T(1,128)S(1)}, u32[]{:S(2)}, u32[]{:S(2)}) async-start(f32[32,1,1024]{2,1,0:T(1,128)} %div.31), calls=%async_computation.1 | async-start | bytes 262144 | tf_op jit(solution)/shard_map/all_to_all | solution.py:86
  103.0 9.1 %all-to-all-done.1 = f32[32,1,1024]{2,1,0:T(1,128)S(1)} async-done(((f32[32,1,1024]{2,1,0:T(1,128)}), f32[32,1,1024]{2,1,0:T(1,128)S(1)}, u32[]{:S(2)}, u32[]{:S(2)}) %all-to-all-start.1) | async-done | bytes 131104 | tf_op jit(solution)/shard_map/all_to_all | solution.py:86
  112.3 12.7 %all_to_all.31 = f32[32,1,1024]{2,1,0:T(1,128)S(1)} all-to-all(f32[32,1,1024]{2,1,0:T(1,128)S(1)} %broadcast_in_dim.56), channel_id=1, replica_groups=mesh['dp'=16,'expert'=32] {'expert'}, dimensions={0} | all-to-all | bytes 262144 | tf_op jit(solution)/shard_map/all_to_all | solution.py:89
  125.2 1.1 broadcast_in_dim.57
  126.3 13.9 %all-to-all-start.3 = ((bf16[16,32,1024]{2,1,0:T(8,128)(2,1)}), bf16[16,32,1024]{2,1,0:T(8,128)(2,1)S(1)}, u32[]{:S(2)}, u32[]{:S(2)}) async-start(bf16[16,32,1024]{2,1,0:T(8,128)(2,1)} %broadcast_in_dim.57), calls=%async_computation.3 | async-start | bytes 2097152 | tf_op jit(solution)/shard_map/all_to_all | solution.py:94
  140.2 0.6 dynamic_slice.18
  140.8 0.5 iota_add_fusion
  141.4 26.8 %all-to-all-done.3 = bf16[16,32,1024]{2,1,0:T(8,128)(2,1)S(1)} async-done(((bf16[16,32,1024]{2,1,0:T(8,128)(2,1)}), bf16[16,32,1024]{2,1,0:T(8,128)(2,1)S(1)}, u32[]{:S(2)}, u32[]{:S(2)}) %all-to-all-start.3) | async-done | bytes 1048608 | tf_op jit(solution)/shard_map/all_to_all | solution.py:94
  168.2 0.9 select_reduce_fusion.1
  169.1 0.7 fusion.74
  169.8 0.7 dynamic_slice.17
  170.4 0.8 constant_dynamic-slice_fusion.1
  171.3 1.7 copy.146
  173.0 1.8 fusion.42
  174.8 0.7 broadcast_multiply_fusion.1
  175.6 2.7 %fusion.2 = f32[2,384,32,18]{1,2,3,0:T(8,128)} fusion(f32[32,1024]{1,0:T(8,128)S(1)} %fusion.43, f32[32,18,2]{0,1,2:T(8,128)S(1)} %copy-done.14, bf16[2,384,1024,1]{2,1,0,3:T(8,128)(2,1)S(1)} %copy-done.3), kind=kOutput, calls=%fused_computation.6 | convolution fusion | flops 908328960 | bytes 3478016 | tf_op jit(solution)/shard_map/sced,efd->scef/dot_general | solution.py:137
  178.3 0.5 fusion.1
  179.0 4.7 %fusion.21 = f32[2,1024,32,18]{1,2,3,0:T(8,128)S(1)} fusion(bf16[3,2,1024,384]{3,2,1,0:T(8,128)(2,1)} %all-gather.2.cloned.1.call-done, f32[2,384,32,18]{1,2,3,0:T(8,128)} %fusion.2, f32[2,384,32,18]{1,2,3,0:T(8,128)} %copy-done.20, f32[2,384,32,18]{1,2,3,0:T(8,128)} %copy-done.17), kind=kOutput, calls=%fused_computation.35 | convolution fusion | flops 910393344 | bytes 11599872 | tf_op jit(solution)/shard_map/scef,edf->sced/dot_general | solution.py:140
  183.8 0.5 copy-done.19
  184.3 1.5 fusion.3
  185.9 3.8 %copy.130 = bf16[32,18,2,1024]{3,2,1,0:T(2,128)(2,1)} copy(bf16[32,18,2,1024]{3,0,1,2:T(8,128)(2,1)S(1)} %fusion.39) | data formatting | bytes 4718592 | tf_op jit(solution)/shard_map/scatter | solution.py:146
  189.7 4.1 %all-to-all-start.4 = ((bf16[32,18,2,1024]{3,2,1,0:T(2,128)(2,1)}), bf16[32,18,2,1024]{3,2,1,0:T(2,128)(2,1)S(1)}, u32[]{:S(2)}, u32[]{:S(2)}) async-start(bf16[32,18,2,1024]{3,2,1,0:T(2,128)(2,1)} %copy.130), calls=%async_computation.4 | async-start | bytes 4718592 | tf_op jit(solution)/shard_map/all_to_all | solution.py:147
  194.5 0.8 constant_dynamic-slice_fusion
  195.2 53.6 %all-to-all-done.4 = bf16[32,18,2,1024]{3,2,1,0:T(2,128)(2,1)S(1)} async-done(((bf16[32,18,2,1024]{3,2,1,0:T(2,128)(2,1)}), bf16[32,18,2,1024]{3,2,1,0:T(2,128)(2,1)S(1)}, u32[]{:S(2)}, u32[]{:S(2)}) %all-to-all-start.4) | async-done | bytes 2359328 | tf_op jit(solution)/shard_map/all_to_all | solution.py:147
  248.8 0.7 copy.140
  249.7 0.4 select_reduce_fusion.2
  250.1 0.6 select_reduce_fusion.4
  250.7 1.6 fusion.23
  (82 shorter events, 1.9 us)
Async XLA Ops:
  7.2 5.6 %copy-start.4 = (bf16[128,1024]{1,0:T(8,128)(2,1)S(1)}, bf16[128,1024]{1,0:T(8,128)(2,1)}, u32[]{:S(2)}) copy-start(bf16[128,1024]{1,0:T(8,128)(2,1)} %param.11) | copy-start | bytes 786436
  7.2 76.5 %all-gather.2.cloned.1.call-start = ((), (), s32[]{:S(2)}) async-start(), calls=%async_computation.5 | async-start | bytes 5013504 | tf_op jit(solution)/shard_map/all_gather | solution.py:51
  11.1 2.5 copy-start.9
  12.8 0.8 copy-start.6
  81.3 1.4 copy-start
  83.6 1.4 slice-start.4
  85.0 6.6 %slice-start = ((s8[4718592]{0:T(1024)(128)(4,1)}), s8[524288]{0:T(1024)(128)(4,1)S(1)}, s32[]{:S(2)}) async-start(s8[4718592]{0:T(1024)(128)(4,1)} %bitcast.154), calls=%async_computation.6 | async-start | bytes 1048576
  87.8 3.8 %slice-start.1 = ((s8[4718592]{0:T(1024)(128)(4,1)}), s8[4194304]{0:T(1024)(128)(4,1)S(1)}, s32[]{:S(2)}) async-start(s8[4718592]{0:T(1024)(128)(4,1)} %bitcast.154), calls=%async_computation.7 | async-start | bytes 8388608
  87.8 4.1 %copy-start.1 = (bf16[32,18,2,1024]{3,2,1,0:T(2,128)(2,1)S(1)}, bf16[32,18,2,1024]{3,2,1,0:T(2,128)(2,1)}, u32[]{:S(2)}) copy-start(bf16[32,18,2,1024]{3,2,1,0:T(2,128)(2,1)} %copy-done) | copy-start | bytes 7077892
  91.9 1.6 copy-start.17
  91.9 2.0 copy-start.2
  91.9 2.0 copy-start.13
  94.0 1.5 copy-start.20
  94.0 9.0 %copy-start.5 = (bf16[128,1024]{1,0:T(8,128)(2,1)S(1)}, bf16[128,1024]{1,0:T(8,128)(2,1)}, u32[]{:S(2)}) copy-start(bf16[128,1024]{1,0:T(8,128)(2,1)} %param.11) | copy-start | bytes 786436
  96.3 15.8 %all-to-all-start.1 = ((f32[32,1,1024]{2,1,0:T(1,128)}), f32[32,1,1024]{2,1,0:T(1,128)S(1)}, u32[]{:S(2)}, u32[]{:S(2)}) async-start(f32[32,1,1024]{2,1,0:T(1,128)} %div.31), calls=%async_computation.1 | async-start | bytes 262144 | tf_op jit(solution)/shard_map/all_to_all | solution.py:86
  125.0 15.2 %copy-start.15 = (s32[512]{0:T(512)S(1)}, s32[512]{0:T(512)}, u32[]{:S(2)}) copy-start(s32[512]{0:T(512)} %param.17) | copy-start | bytes 6148
  125.1 43.9 %copy-start.16 = (f32[32]{0:T(128)}, f32[32]{0:T(128)S(1)}, u32[]{:S(2)}) copy-start(f32[32]{0:T(128)S(1)} %fusion.40) | copy-start | bytes 388
  126.3 41.8 %all-to-all-start.3 = ((bf16[16,32,1024]{2,1,0:T(8,128)(2,1)}), bf16[16,32,1024]{2,1,0:T(8,128)(2,1)S(1)}, u32[]{:S(2)}, u32[]{:S(2)}) async-start(bf16[16,32,1024]{2,1,0:T(8,128)(2,1)} %broadcast_in_dim.57), calls=%async_computation.3 | async-start | bytes 2097152 | tf_op jit(solution)/shard_map/all_to_all | solution.py:94
  169.1 1.4 copy-start.11
  173.0 2.6 copy-start.3
  173.0 2.6 copy-start.14
  175.6 2.8 %copy-start.8 = (f32[32,1024]{1,0:T(8,128)}, f32[32,1024]{1,0:T(8,128)S(1)}, u32[]{:S(2)}) copy-start(f32[32,1024]{1,0:T(8,128)S(1)} %fusion.43) | copy-start | bytes 393220
  178.3 5.4 %slice-start.2 = ((s8[4718592]{0:T(1024)(128)(4,1)}), s8[524288]{0:T(1024)(128)(4,1)S(1)}, s32[]{:S(2)}) async-start(s8[4718592]{0:T(1024)(128)(4,1)} %bitcast.156), calls=%async_computation.8 | async-start | bytes 1048576
  179.0 4.8 %slice-start.3 = ((s8[4718592]{0:T(1024)(128)(4,1)}), s8[4194304]{0:T(1024)(128)(4,1)S(1)}, s32[]{:S(2)}) async-start(s8[4718592]{0:T(1024)(128)(4,1)} %bitcast.156), calls=%async_computation.9 | async-start | bytes 8388608
  179.0 4.8 %copy-start.18 = (f32[2,384,32,18]{1,2,3,0:T(8,128)S(1)}, f32[2,384,32,18]{1,2,3,0:T(8,128)}, u32[]{:S(2)}) copy-start(f32[2,384,32,18]{1,2,3,0:T(8,128)} %copy-done.17) | copy-start | bytes 5308420
  179.0 5.3 %copy-start.19 = (f32[2,384,32,18]{1,2,3,0:T(8,128)S(1)}, f32[2,384,32,18]{1,2,3,0:T(8,128)}, u32[]{:S(2)}) copy-start(f32[2,384,32,18]{1,2,3,0:T(8,128)} %fusion.2) | copy-start | bytes 5308420
  189.7 59.1 %all-to-all-start.4 = ((bf16[32,18,2,1024]{3,2,1,0:T(2,128)(2,1)}), bf16[32,18,2,1024]{3,2,1,0:T(2,128)(2,1)S(1)}, u32[]{:S(2)}, u32[]{:S(2)}) async-start(bf16[32,18,2,1024]{3,2,1,0:T(2,128)(2,1)} %copy.130), calls=%async_computation.4 | async-start | bytes 4718592 | tf_op jit(solution)/shard_map/all_to_all | solution.py:147
  195.2 54.4 %copy-start.10 = (s32[64,128]{1,0:T(8,128)S(1)}, s32[64,128]{1,0:T(8,128)}, u32[]{:S(2)}) copy-start(s32[64,128]{1,0:T(8,128)} %copy-done.9) | copy-start | bytes 98308
  195.2 54.8 %copy-start.12 = (s32[128,8]{0,1:T(8,128)S(1)}, s32[128,8]{0,1:T(8,128)}, u32[]{:S(2)}) copy-start(s32[128,8]{0,1:T(8,128)} %param.12) | copy-start | bytes 12292
  195.2 55.5 %copy-start.7 = (pred[64,18,128]{2,1,0:T(8,128)(4,1)S(1)}, pred[64,18,128]{2,1,0:T(8,128)(4,1)}, u32[]{:S(2)}) copy-start(pred[64,18,128]{2,1,0:T(8,128)(4,1)} %copy-done.6) | copy-start | bytes 442372
Sparse Core Ops, SparseCore 0:
  10.2 51.9 all-gather.1

commit v6 on v5

--- a/solution.py
+++ b/solution.py
@@ -33,6 +33,25 @@
     pieces = split3(values)
     pad = width - pieces.shape[-1]
     return jnp.pad(pieces, [(0, 0)] * (pieces.ndim - 1) + [(0, pad)])
+
+
+def butterfly_sum(x, axis, n):
+    step = 1
+    while step < n:
+        x = x + lax.ppermute(x, axis, [(j, j ^ step) for j in range(n)])
+        step *= 2
+    return x
+
+
+def butterfly_gather(x, axis, n):
+    me = lax.axis_index(axis)
+    step = 1
+    while step < n:
+        other = lax.ppermute(x, axis, [(j, j ^ step) for j in range(n)])
+        low = (me // step) % 2 == 0
+        x = jnp.where(low, jnp.concatenate([x, other]), jnp.concatenate([other, x]))
+        step *= 2
+    return x
 
 
 def on_device(tokens, expert_ids, gate_values, w_gate, w_up, w_down, partner):
@@ -83,16 +102,13 @@
     partial = jnp.sum(gates[..., None] * out_f32, axis=(1, 2))
 
     token_mean = jnp.mean(tokens.astype(f32), axis=0)
-    shares = lax.all_to_all(partial / tok_rows, "expert", split_axis=0, concat_axis=0, tiled=True)
-    own_pooled = token_mean + jnp.sum(shares, axis=0)
-    copies = jnp.broadcast_to(own_pooled[None, :], (group, model_width))
-    pooled = lax.all_to_all(copies, "expert", split_axis=0, concat_axis=0, tiled=True)
+    own_row = (jnp.arange(group, dtype=jnp.int32) == me)[:, None]
+    share = partial / tok_rows + jnp.where(own_row, token_mean[None, :], 0.0)
+    pooled = butterfly_sum(share, "expert", group)
     inv_rms = lax.rsqrt(jnp.mean(pooled * pooled, axis=1) + 1e-06)
     embedding = (pooled * inv_rms[:, None]).astype(bf16)
     blocks = lax.axis_size("dp")
-    spread = jnp.broadcast_to(embedding[None], (blocks, group, model_width))
-    gathered = lax.all_to_all(spread, "dp", split_axis=0, concat_axis=0, tiled=True)
-    gathered = gathered.reshape(blocks * group, model_width)
+    gathered = butterfly_gather(embedding, "dp", blocks)
     batch_size = gathered.shape[0]
 
     scores = (

time: 261 us -> 297 us (1.14)
  blocking collectives: 77.9 us -> 0 us
  waiting for transfers between devices: 89.5 us -> 161 us
  starting transfers between devices: 24.7 us -> 68 us
  local copies, waits for them, and re-layouts: 23 us -> 17.5 us
  matrix products: 20.9 us -> 24 us
    all_to_all x2 -> x0, blocking collectives: 77.9 us -> none  [the longest x1 65.2 us: on_device(): lax.all_to_all(outgoing, 'expert', split_axis=0, concat_axis=0, tiled=True)]
    ppermute x0 -> x9, waiting for transfers between devices: none -> 53.1 us  [the longest x4 38.2 us: butterfly_gather(): other = lax.ppermute(x, axis, [(j, j ^ step) for j in range(n)])]
    ppermute x0 -> x9, starting transfers between devices: none -> 52.2 us  [the longest x4 30 us: butterfly_gather(): other = lax.ppermute(x, axis, [(j, j ^ step) for j in range(n)])]
    all_to_all x2 -> x1, waiting for transfers between devices: 35.9 us -> 54.3 us  [on_device(): lax.all_to_all(outgoing, 'expert', split_axis=0, concat_axis=0, tiled=True)]
    all_to_all x2 -> x1, starting transfers between devices: 20.6 us -> 10.5 us  [on_device(): lax.all_to_all(outgoing, 'expert', split_axis=0, concat_axis=0, tiled=True)]
  transfers between devices with their start and end apart: 4 -> 12, of which waited for: 3 -> 11; matrix products, arithmetic and copies ran while one was open for 3% -> 3% of each run, Pallas kernels for 0% -> 0%
where the time goes in v6:
time: 297 us; the launch traced here: 295 us
  waiting for transfers between devices  161 us (54%)
  starting transfers between devices  68 us (23%)
  matrix products  24 us (8%)
  local copies, waits for them, and re-layouts  17.5 us (6%)
  between operations  16.4 us (6%)
  other arithmetic  8.07 us (3%)
    all_to_all x1, waiting for transfers between devices, on_device(): lax.all_to_all(outgoing, 'expert', split_axis=0, concat_axis=0, tiled=True)  54.3 us
    all_to_all x1, waiting for transfers between devices, on_device(): lax.all_to_all(route_here, 'expert', split_axis=0, concat_axis=0, tiled=T...  53.5 us
    ppermute x4, waiting for transfers between devices, butterfly_gather(): other = lax.ppermute(x, axis, [(j, j ^ step) for j in range(n)])  38.2 us
    ppermute x4, starting transfers between devices, butterfly_gather(): other = lax.ppermute(x, axis, [(j, j ^ step) for j in range(n)])  30 us
    ppermute x5, starting transfers between devices, butterfly_sum(): x = x + lax.ppermute(x, axis, [(j, j ^ step) for j in range(n)])  22.2 us
    ppermute x5, waiting for transfers between devices, butterfly_sum(): x = x + lax.ppermute(x, axis, [(j, j ^ step) for j in range(n)])  14.9 us
    all_to_all x1, starting transfers between devices, on_device(): lax.all_to_all(outgoing, 'expert', split_axis=0, concat_axis=0, tiled=True)  10.5 us
  transfers between devices with their start and end apart: 12, of which 11 were waited for; matrix products, arithmetic and copies ran while one was open for 3% of the time, Pallas kernels for 0%

profile of v6, /device:TPU:1, one launch (start us, length us, event | category | flops | bytes accessed | tf_op | source)
XLA Modules:
  0.0 295.0 jit_solution(1666874462940956011)
XLA Ops:
  7.2 1.1 stack_reshape.3
  8.3 1.7 pad_maximum_fusion
  10.0 0.7 convert_reduce_fusion.1
  11.1 0.8 select_reduce_fusion.5
  12.8 0.8 convolution_convert_fusion.1
  13.6 3.9 %copy.124 = bf16[32,18,2,1024]{3,2,1,0:T(2,128)(2,1)} copy(bf16[32,18,2,1024]{3,0,2,1:T(8,128)(2,1)S(1)} %copy_dynamic-update-slice_fusion) | data formatting | bytes 4718592 | tf_op jit(solution)/shard_map/scatter | solution.py:88
  17.4 10.5 %all-to-all-start = ((bf16[32,18,2,1024]{3,2,1,0:T(2,128)(2,1)}), bf16[32,18,2,1024]{3,2,1,0:T(2,128)(2,1)S(1)}, u32[]{:S(2)}, u32[]{:S(2)}) async-start(bf16[32,18,2,1024]{3,2,1,0:T(2,128)(2,1)} %copy.124), calls=%async_computation | async-start | bytes 4718592 | tf_op jit(solution)/shard_map/all_to_all | solution.py:90
  28.0 54.3 %all-to-all-done = bf16[32,18,2,1024]{3,2,1,0:T(2,128)(2,1)S(1)} async-done(((bf16[32,18,2,1024]{3,2,1,0:T(2,128)(2,1)}), bf16[32,18,2,1024]{3,2,1,0:T(2,128)(2,1)S(1)}, u32[]{:S(2)}, u32[]{:S(2)}) %all-to-all-start) | async-done | bytes 2359328 | tf_op jit(solution)/shard_map/all_to_all | solution.py:90
  82.7 1.1 copy-done
  83.8 1.4 slice-done.4
  85.2 2.7 reshape.129
  87.9 3.8 %fusion.8 = f32[2,384,32,18]{1,2,3,0:T(8,128)S(1)} fusion(bf16[32,18,2,1024]{3,2,1,0:T(2,128)(2,1)} %copy-done, bf16[3,2,1024,384]{3,2,1,0:T(8,128)(2,1)} %all-gather.2.cloned.1.call-done), kind=kOutput, calls=%fused_computation.12 | convolution fusion | flops 905969664 | bytes 5701632 | tf_op jit(solution)/shard_map/sced,edf->scef/dot_general | solution.py:94
  92.0 1.6 fusion.6
  93.6 0.5 copy-done.2
  94.1 1.5 fusion
  95.7 3.9 %collective-permute-start = (f32[32,1024]{1,0:T(8,128)S(1)}, f32[32,1024]{1,0:T(8,128)S(1)}, u32[]{:S(2)}, u32[]{:S(2)}) collective-permute-start(f32[32,1024]{1,0:T(8,128)S(1)} %select_add_fusion), channel_id=1, source_target_pairs={{0,1},{1,0},{2,3},{3,2},{4,5},{5,4},{6,7},{7,6},{8,9},{9,8},{10,11... | collective-permute-start | bytes 393224 | tf_op jit(solution)/shard_map/ppermute | solution.py:41
  99.6 2.3 collective-permute-done
  102.0 3.6 %collective-permute-start.1 = (f32[32,1024]{1,0:T(8,128)S(1)}, f32[32,1024]{1,0:T(8,128)S(1)}, u32[]{:S(2)}, u32[]{:S(2)}) collective-permute-start(f32[32,1024]{1,0:T(8,128)S(1)} %fusion.73), channel_id=1, source_target_pairs={{0,2},{1,3},{2,0},{3,1},{4,6},{5,7},{6,4},{7,5},{8,10},{9,11},{10,... | collective-permute-start | bytes 393224 | tf_op jit(solution)/shard_map/ppermute | solution.py:41
  105.6 4.4 %collective-permute-done.1 = f32[32,1024]{1,0:T(8,128)S(1)} collective-permute-done((f32[32,1024]{1,0:T(8,128)S(1)}, f32[32,1024]{1,0:T(8,128)S(1)}, u32[]{:S(2)}, u32[]{:S(2)}) %collective-permute-start.1) | collective-permute-done | bytes 131104 | tf_op jit(solution)/shard_map/ppermute | solution.py:41
  110.1 7.1 %collective-permute-start.2 = (f32[32,1024]{1,0:T(8,128)S(1)}, f32[32,1024]{1,0:T(8,128)S(1)}, u32[]{:S(2)}, u32[]{:S(2)}) collective-permute-start(f32[32,1024]{1,0:T(8,128)S(1)} %add.122), channel_id=1, source_target_pairs={{0,4},{1,5},{2,6},{3,7},{4,0},{5,1},{6,2},{7,3},{8,12},{9,13},{10,... | collective-permute-start | bytes 393224 | tf_op jit(solution)/shard_map/ppermute | solution.py:41
  117.2 2.5 collective-permute-done.2
  119.7 3.2 %collective-permute-start.3 = (f32[32,1024]{1,0:T(8,128)S(1)}, f32[32,1024]{1,0:T(8,128)S(1)}, u32[]{:S(2)}, u32[]{:S(2)}) collective-permute-start(f32[32,1024]{1,0:T(8,128)S(1)} %add.123), channel_id=1, source_target_pairs={{0,8},{1,9},{2,10},{3,11},{4,12},{5,13},{6,14},{7,15},{8,0},{9,1},... | collective-permute-start | bytes 393224 | tf_op jit(solution)/shard_map/ppermute | solution.py:41
  122.9 2.8 collective-permute-done.3
  125.7 4.5 %collective-permute-start.4 = (f32[32,1024]{1,0:T(8,128)S(1)}, f32[32,1024]{1,0:T(8,128)S(1)}, u32[]{:S(2)}, u32[]{:S(2)}) collective-permute-start(f32[32,1024]{1,0:T(8,128)S(1)} %add.124), channel_id=1, source_target_pairs={{0,16},{1,17},{2,18},{3,19},{4,20},{5,21},{6,22},{7,23},{8,24},{9,... | collective-permute-start | bytes 393224 | tf_op jit(solution)/shard_map/ppermute | solution.py:41
  130.2 2.8 collective-permute-done.4
  133.2 12.2 %collective-permute-start.5 = (bf16[32,1024]{1,0:T(8,128)(2,1)S(1)}, bf16[32,1024]{1,0:T(8,128)(2,1)S(1)}, u32[]{:S(2)}, u32[]{:S(2)}) collective-permute-start(bf16[32,1024]{1,0:T(8,128)(2,1)S(1)} %multiply_convert_fusion.2), channel_id=1, source_target_pairs={{0,32},{32,0},{64,96},{96,64},{128,160},{160,128},{192,224},{224,1... | collective-permute-start | bytes 196616 | tf_op jit(solution)/shard_map/ppermute | solution.py:50
  145.4 0.9 collective-permute-done.5
  146.3 4.0 %collective-permute-start.6 = (bf16[64,1024]{1,0:T(8,128)(2,1)S(1)}, bf16[64,1024]{1,0:T(8,128)(2,1)S(1)}, u32[]{:S(2)}, u32[]{:S(2)}) collective-permute-start(bf16[64,1024]{1,0:T(8,128)(2,1)S(1)} %maximum_select_fusion.5), channel_id=1, source_target_pairs={{0,64},{32,96},{64,0},{96,32},{128,192},{160,224},{192,128},{224,1... | collective-permute-start | bytes 393224 | tf_op jit(solution)/shard_map/ppermute | solution.py:50
  150.3 3.5 %collective-permute-done.6 = bf16[64,1024]{1,0:T(8,128)(2,1)S(1)} collective-permute-done((bf16[64,1024]{1,0:T(8,128)(2,1)S(1)}, bf16[64,1024]{1,0:T(8,128)(2,1)S(1)}, u32[]{:S(2)}, u32[]{:S(2)}) %collective-permute-start.6) | collective-permute-done | bytes 131104 | tf_op jit(solution)/shard_map/ppermute | solution.py:50
  153.9 5.0 %collective-permute-start.7 = (bf16[128,1024]{1,0:T(8,128)(2,1)S(1)}, bf16[128,1024]{1,0:T(8,128)(2,1)S(1)}, u32[]{:S(2)}, u32[]{:S(2)}) collective-permute-start(bf16[128,1024]{1,0:T(8,128)(2,1)S(1)} %maximum_select_fusion.2), channel_id=1, source_target_pairs={{0,128},{32,160},{64,192},{96,224},{128,0},{160,32},{192,64},{224,... | collective-permute-start | bytes 786440 | tf_op jit(solution)/shard_map/ppermute | solution.py:50
  159.0 11.5 %collective-permute-done.7 = bf16[128,1024]{1,0:T(8,128)(2,1)S(1)} collective-permute-done((bf16[128,1024]{1,0:T(8,128)(2,1)S(1)}, bf16[128,1024]{1,0:T(8,128)(2,1)S(1)}, u32[]{:S(2)}, u32[]{:S(2)}) %collective-permute-start.7) | collective-permute-done | bytes 262176 | tf_op jit(solution)/shard_map/ppermute | solution.py:50
  170.5 0.9 maximum_select_fusion.1
  171.4 8.8 %collective-permute-start.8 = (bf16[256,1024]{1,0:T(8,128)(2,1)}, bf16[256,1024]{1,0:T(8,128)(2,1)}, u32[]{:S(2)}, u32[]{:S(2)}) collective-permute-start(bf16[256,1024]{1,0:T(8,128)(2,1)} %maximum_select_fusion.1), channel_id=1, source_target_pairs={{0,256},{32,288},{64,320},{96,352},{128,384},{160,416},{192,448},{... | collective-permute-start | bytes 1572872 | tf_op jit(solution)/shard_map/ppermute | solution.py:50
  180.3 22.3 %collective-permute-done.8 = bf16[256,1024]{1,0:T(8,128)(2,1)} collective-permute-done((bf16[256,1024]{1,0:T(8,128)(2,1)}, bf16[256,1024]{1,0:T(8,128)(2,1)}, u32[]{:S(2)}, u32[]{:S(2)}) %collective-permute-start.8) | collective-permute-done | bytes 524320 | tf_op jit(solution)/shard_map/ppermute | solution.py:50
  202.6 3.3 %select_reduce_fusion.1 = (f32[512]{0:T(512)S(1)}, f32[512]{0:T(512)S(1)}, f32[512,512]{0,1:T(8,128)S(1)}) fusion(s32[512]{0:T(512)S(1)} %copy-done.7, bf16[256,1024]{1,0:T(8,128)(2,1)} %collective-permute-done.8, bf16[256,1024]{1,0:T(8,128)(2,1)} %maximum_select_fusion.1, pred[]{:T(512)S(6)} %eq.96), kind=kOutput, calls=%fused_computation.43 | convolution fusion | flops 543423488 | bytes 2103297 | tf_op jit(solution)/shard_map/dot_general | solution.py:117
  206.0 0.7 fusion.72
  207.2 2.5 multiply_reduce_fusion
  209.9 2.7 fusion.2
  212.6 0.5 fusion.1
  213.3 4.7 %fusion.21 = f32[2,1024,32,18]{1,2,3,0:T(8,128)S(1)} fusion(bf16[3,2,1024,384]{3,2,1,0:T(8,128)(2,1)} %all-gather.2.cloned.1.call-done, f32[2,384,32,18]{1,2,3,0:T(8,128)} %fusion.2, f32[2,384,32,18]{1,2,3,0:T(8,128)} %copy-done.11, f32[2,384,32,18]{1,2,3,0:T(8,128)} %copy-done.8), kind=kOutput, calls=%fused_computation.35 | convolution fusion | flops 910393344 | bytes 11599872 | tf_op jit(solution)/shard_map/scef,edf->sced/dot_general | solution.py:156
  218.1 0.5 copy-done.10
  218.6 1.5 fusion.3
  220.2 3.8 %copy.130 = bf16[32,18,2,1024]{3,2,1,0:T(2,128)(2,1)} copy(bf16[32,18,2,1024]{3,0,1,2:T(8,128)(2,1)S(1)} %fusion.40) | data formatting | bytes 4718592 | tf_op jit(solution)/shard_map/scatter | solution.py:162
  224.0 5.3 %all-to-all-start.1 = ((bf16[32,18,2,1024]{3,2,1,0:T(2,128)(2,1)}), bf16[32,18,2,1024]{3,2,1,0:T(2,128)(2,1)S(1)}, u32[]{:S(2)}, u32[]{:S(2)}) async-start(bf16[32,18,2,1024]{3,2,1,0:T(2,128)(2,1)} %copy.130), calls=%async_computation.1 | async-start | bytes 4718592 | tf_op jit(solution)/shard_map/all_to_all | solution.py:163
  230.0 53.5 %all-to-all-done.1 = bf16[32,18,2,1024]{3,2,1,0:T(2,128)(2,1)S(1)} async-done(((bf16[32,18,2,1024]{3,2,1,0:T(2,128)(2,1)}), bf16[32,18,2,1024]{3,2,1,0:T(2,128)(2,1)S(1)}, u32[]{:S(2)}, u32[]{:S(2)}) %all-to-all-start.1) | async-done | bytes 2359328 | tf_op jit(solution)/shard_map/all_to_all | solution.py:163
  283.5 0.7 copy.140
  284.8 0.6 select_reduce_fusion.4
  285.4 1.6 fusion.23
  (82 shorter events, 3.9 us)
Async XLA Ops:
  7.2 5.6 %copy-start.4 = (bf16[128,1024]{1,0:T(8,128)(2,1)S(1)}, bf16[128,1024]{1,0:T(8,128)(2,1)}, u32[]{:S(2)}) copy-start(bf16[128,1024]{1,0:T(8,128)(2,1)} %param.11) | copy-start | bytes 786436
  7.2 76.6 %all-gather.2.cloned.1.call-start = ((), (), s32[]{:S(2)}) async-start(), calls=%async_computation.2 | async-start | bytes 5013504 | tf_op jit(solution)/shard_map/all_gather | solution.py:70
  17.4 64.9 %all-to-all-start = ((bf16[32,18,2,1024]{3,2,1,0:T(2,128)(2,1)}), bf16[32,18,2,1024]{3,2,1,0:T(2,128)(2,1)S(1)}, u32[]{:S(2)}, u32[]{:S(2)}) async-start(bf16[32,18,2,1024]{3,2,1,0:T(2,128)(2,1)} %copy.124), calls=%async_computation | async-start | bytes 4718592 | tf_op jit(solution)/shard_map/all_to_all | solution.py:90
  82.3 1.4 copy-start
  83.8 1.4 slice-start.4
  85.2 6.5 %slice-start = ((s8[4718592]{0:T(1024)(128)(4,1)}), s8[524288]{0:T(1024)(128)(4,1)S(1)}, s32[]{:S(2)}) async-start(s8[4718592]{0:T(1024)(128)(4,1)} %bitcast.137), calls=%async_computation.3 | async-start | bytes 1048576
  87.9 3.8 %slice-start.1 = ((s8[4718592]{0:T(1024)(128)(4,1)}), s8[4194304]{0:T(1024)(128)(4,1)S(1)}, s32[]{:S(2)}) async-start(s8[4718592]{0:T(1024)(128)(4,1)} %bitcast.137), calls=%async_computation.4 | async-start | bytes 8388608
  87.9 4.1 %copy-start.1 = (bf16[32,18,2,1024]{3,2,1,0:T(2,128)(2,1)S(1)}, bf16[32,18,2,1024]{3,2,1,0:T(2,128)(2,1)}, u32[]{:S(2)}) copy-start(bf16[32,18,2,1024]{3,2,1,0:T(2,128)(2,1)} %copy-done) | copy-start | bytes 7077892
  92.0 1.6 copy-start.8
  92.0 2.0 copy-start.2
  94.1 1.5 copy-start.11
  95.7 84.6 %copy-start.7 = (s32[512]{0:T(512)S(1)}, s32[512]{0:T(512)}, u32[]{:S(2)}) copy-start(s32[512]{0:T(512)} %param.17) | copy-start | bytes 6148
  95.7 6.3 %collective-permute-start = (f32[32,1024]{1,0:T(8,128)S(1)}, f32[32,1024]{1,0:T(8,128)S(1)}, u32[]{:S(2)}, u32[]{:S(2)}) collective-permute-start(f32[32,1024]{1,0:T(8,128)S(1)} %select_add_fusion), channel_id=1, source_target_pairs={{0,1},{1,0},{2,3},{3,2},{4,5},{5,4},{6,7},{7,6},{8,9},{9,8},{10,11... | collective-permute-start | bytes 393224 | tf_op jit(solution)/shard_map/ppermute | solution.py:41
  102.0 8.0 %collective-permute-start.1 = (f32[32,1024]{1,0:T(8,128)S(1)}, f32[32,1024]{1,0:T(8,128)S(1)}, u32[]{:S(2)}, u32[]{:S(2)}) collective-permute-start(f32[32,1024]{1,0:T(8,128)S(1)} %fusion.73), channel_id=1, source_target_pairs={{0,2},{1,3},{2,0},{3,1},{4,6},{5,7},{6,4},{7,5},{8,10},{9,11},{10,... | collective-permute-start | bytes 393224 | tf_op jit(solution)/shard_map/ppermute | solution.py:41
  110.1 9.6 %collective-permute-start.2 = (f32[32,1024]{1,0:T(8,128)S(1)}, f32[32,1024]{1,0:T(8,128)S(1)}, u32[]{:S(2)}, u32[]{:S(2)}) collective-permute-start(f32[32,1024]{1,0:T(8,128)S(1)} %add.122), channel_id=1, source_target_pairs={{0,4},{1,5},{2,6},{3,7},{4,0},{5,1},{6,2},{7,3},{8,12},{9,13},{10,... | collective-permute-start | bytes 393224 | tf_op jit(solution)/shard_map/ppermute | solution.py:41
  119.7 6.0 %collective-permute-start.3 = (f32[32,1024]{1,0:T(8,128)S(1)}, f32[32,1024]{1,0:T(8,128)S(1)}, u32[]{:S(2)}, u32[]{:S(2)}) collective-permute-start(f32[32,1024]{1,0:T(8,128)S(1)} %add.123), channel_id=1, source_target_pairs={{0,8},{1,9},{2,10},{3,11},{4,12},{5,13},{6,14},{7,15},{8,0},{9,1},... | collective-permute-start | bytes 393224 | tf_op jit(solution)/shard_map/ppermute | solution.py:41
  125.7 7.3 %collective-permute-start.4 = (f32[32,1024]{1,0:T(8,128)S(1)}, f32[32,1024]{1,0:T(8,128)S(1)}, u32[]{:S(2)}, u32[]{:S(2)}) collective-permute-start(f32[32,1024]{1,0:T(8,128)S(1)} %add.124), channel_id=1, source_target_pairs={{0,16},{1,17},{2,18},{3,19},{4,20},{5,21},{6,22},{7,23},{8,24},{9,... | collective-permute-start | bytes 393224 | tf_op jit(solution)/shard_map/ppermute | solution.py:41
  133.2 13.1 %collective-permute-start.5 = (bf16[32,1024]{1,0:T(8,128)(2,1)S(1)}, bf16[32,1024]{1,0:T(8,128)(2,1)S(1)}, u32[]{:S(2)}, u32[]{:S(2)}) collective-permute-start(bf16[32,1024]{1,0:T(8,128)(2,1)S(1)} %multiply_convert_fusion.2), channel_id=1, source_target_pairs={{0,32},{32,0},{64,96},{96,64},{128,160},{160,128},{192,224},{224,1... | collective-permute-start | bytes 196616 | tf_op jit(solution)/shard_map/ppermute | solution.py:50
  146.3 7.6 %collective-permute-start.6 = (bf16[64,1024]{1,0:T(8,128)(2,1)S(1)}, bf16[64,1024]{1,0:T(8,128)(2,1)S(1)}, u32[]{:S(2)}, u32[]{:S(2)}) collective-permute-start(bf16[64,1024]{1,0:T(8,128)(2,1)S(1)} %maximum_select_fusion.5), channel_id=1, source_target_pairs={{0,64},{32,96},{64,0},{96,32},{128,192},{160,224},{192,128},{224,1... | collective-permute-start | bytes 393224 | tf_op jit(solution)/shard_map/ppermute | solution.py:50
  153.9 16.6 %collective-permute-start.7 = (bf16[128,1024]{1,0:T(8,128)(2,1)S(1)}, bf16[128,1024]{1,0:T(8,128)(2,1)S(1)}, u32[]{:S(2)}, u32[]{:S(2)}) collective-permute-start(bf16[128,1024]{1,0:T(8,128)(2,1)S(1)} %maximum_select_fusion.2), channel_id=1, source_target_pairs={{0,128},{32,160},{64,192},{96,224},{128,0},{160,32},{192,64},{224,... | collective-permute-start | bytes 786440 | tf_op jit(solution)/shard_map/ppermute | solution.py:50
  171.4 31.2 %collective-permute-start.8 = (bf16[256,1024]{1,0:T(8,128)(2,1)}, bf16[256,1024]{1,0:T(8,128)(2,1)}, u32[]{:S(2)}, u32[]{:S(2)}) collective-permute-start(bf16[256,1024]{1,0:T(8,128)(2,1)} %maximum_select_fusion.1), channel_id=1, source_target_pairs={{0,256},{32,288},{64,320},{96,352},{128,384},{160,416},{192,448},{... | collective-permute-start | bytes 1572872 | tf_op jit(solution)/shard_map/ppermute | solution.py:50
  206.0 1.0 copy-start.5
  207.2 2.7 copy-start.3
  212.6 5.4 %slice-start.2 = ((s8[4718592]{0:T(1024)(128)(4,1)}), s8[524288]{0:T(1024)(128)(4,1)S(1)}, s32[]{:S(2)}) async-start(s8[4718592]{0:T(1024)(128)(4,1)} %bitcast.139), calls=%async_computation.5 | async-start | bytes 1048576
  213.2 4.8 %slice-start.3 = ((s8[4718592]{0:T(1024)(128)(4,1)}), s8[4194304]{0:T(1024)(128)(4,1)S(1)}, s32[]{:S(2)}) async-start(s8[4718592]{0:T(1024)(128)(4,1)} %bitcast.139), calls=%async_computation.6 | async-start | bytes 8388608
  213.3 4.8 %copy-start.9 = (f32[2,384,32,18]{1,2,3,0:T(8,128)S(1)}, f32[2,384,32,18]{1,2,3,0:T(8,128)}, u32[]{:S(2)}) copy-start(f32[2,384,32,18]{1,2,3,0:T(8,128)} %copy-done.8) | copy-start | bytes 5308420
  213.3 5.3 %copy-start.10 = (f32[2,384,32,18]{1,2,3,0:T(8,128)S(1)}, f32[2,384,32,18]{1,2,3,0:T(8,128)}, u32[]{:S(2)}) copy-start(f32[2,384,32,18]{1,2,3,0:T(8,128)} %fusion.2) | copy-start | bytes 5308420
  224.0 59.5 %all-to-all-start.1 = ((bf16[32,18,2,1024]{3,2,1,0:T(2,128)(2,1)}), bf16[32,18,2,1024]{3,2,1,0:T(2,128)(2,1)S(1)}, u32[]{:S(2)}, u32[]{:S(2)}) async-start(bf16[32,18,2,1024]{3,2,1,0:T(2,128)(2,1)} %copy.130), calls=%async_computation.1 | async-start | bytes 4718592 | tf_op jit(solution)/shard_map/all_to_all | solution.py:163
  229.9 54.8 %copy-start.6 = (s32[128,8]{0,1:T(8,128)S(1)}, s32[128,8]{0,1:T(8,128)}, u32[]{:S(2)}) copy-start(s32[128,8]{0,1:T(8,128)} %param.12) | copy-start | bytes 12292
Sparse Core Ops, SparseCore 0:
  10.1 51.9 all-gather.1

commit v7 on v5

--- a/solution.py
+++ b/solution.py
@@ -85,14 +85,19 @@
     token_mean = jnp.mean(tokens.astype(f32), axis=0)
     shares = lax.all_to_all(partial / tok_rows, "expert", split_axis=0, concat_axis=0, tiled=True)
     own_pooled = token_mean + jnp.sum(shares, axis=0)
-    copies = jnp.broadcast_to(own_pooled[None, :], (group, model_width))
-    pooled = lax.all_to_all(copies, "expert", split_axis=0, concat_axis=0, tiled=True)
+    blocks = lax.axis_size("dp")
+    copies = jnp.broadcast_to(own_pooled[None, :], (blocks, model_width))
+    column = lax.all_to_all(copies, "dp", split_axis=0, concat_axis=0, tiled=True)
+    column_inv = lax.rsqrt(jnp.mean(column * column, axis=1) + 1e-06)
+    column_embed = (column * column_inv[:, None]).astype(bf16)
+    own_pieces = split3(own_pooled[None, :]).reshape(3, model_width)
+    payload = jnp.concatenate([column_embed, own_pieces], axis=0)
+    payload = jnp.broadcast_to(payload[None], (group,) + payload.shape)
+    received = lax.all_to_all(payload, "expert", split_axis=0, concat_axis=0, tiled=True)
+    gathered = jnp.swapaxes(received[:, :blocks, :], 0, 1).reshape(blocks * group, model_width)
+    pieces = received[:, blocks:, :].astype(f32)
+    pooled = pieces[:, 0, :] + (pieces[:, 1, :] + pieces[:, 2, :])
     inv_rms = lax.rsqrt(jnp.mean(pooled * pooled, axis=1) + 1e-06)
-    embedding = (pooled * inv_rms[:, None]).astype(bf16)
-    blocks = lax.axis_size("dp")
-    spread = jnp.broadcast_to(embedding[None], (blocks, group, model_width))
-    gathered = lax.all_to_all(spread, "dp", split_axis=0, concat_axis=0, tiled=True)
-    gathered = gathered.reshape(blocks * group, model_width)
     batch_size = gathered.shape[0]
 
     scores = (

time: 261 us -> 272 us (1.042)
  waiting for transfers between devices: 89.5 us -> 108 us
  blocking collectives: 77.9 us -> 65.2 us
  starting transfers between devices: 24.7 us -> 31.2 us
    all_to_all x1 -> x2, waiting for transfers between devices: 26.8 us -> 45.3 us  [the longest x1 37.6 us: on_device(): lax.all_to_all(payload, 'expert', split_axis=0, concat_axis=0, tiled=True)]
    all_to_all x1 -> x0, blocking collectives: 12.7 us -> none  [on_device(): lax.all_to_all(copies, 'expert', split_axis=0, concat_axis=0, tiled=True)]
    all_to_all x1, starting transfers between devices: 4.06 us -> 7.74 us  [on_device(): lax.all_to_all(route_here, 'expert', split_axis=0, concat_axis=0, tiled=T...]
    all_to_all x1 -> x2, starting transfers between devices: 13.9 us -> 16.7 us  [the longest x1 12.6 us: on_device(): lax.all_to_all(copies, 'dp', split_axis=0, concat_axis=0, tiled=True)]
  transfers between devices with their start and end apart: 4 -> 5, of which waited for: 3 -> 4; matrix products, arithmetic and copies ran while one was open for 3% -> 2% of each run, Pallas kernels for 0% -> 0%
where the time goes in v7:
time: 272 us; the launch traced here: 271 us
  waiting for transfers between devices  108 us (40%)
  blocking collectives  65.2 us (24%)
  starting transfers between devices  31.2 us (11%)
  matrix products  21.4 us (8%)
  local copies, waits for them, and re-layouts  21.2 us (8%)
  between operations  16.2 us (6%)
  other arithmetic  7.15 us (3%)
    all_to_all x1, blocking collectives, on_device(): lax.all_to_all(outgoing, 'expert', split_axis=0, concat_axis=0, tiled=True)  65.2 us
    all_to_all x1, waiting for transfers between devices, on_device(): lax.all_to_all(route_here, 'expert', split_axis=0, concat_axis=0, tiled=T...  53.7 us
    all_to_all x1, waiting for transfers between devices, on_device(): lax.all_to_all(payload, 'expert', split_axis=0, concat_axis=0, tiled=True)  37.6 us
    all_to_all x1, starting transfers between devices, on_device(): lax.all_to_all(copies, 'dp', split_axis=0, concat_axis=0, tiled=True)  12.6 us
    all_to_all x1, waiting for transfers between devices, on_device(): lax.all_to_all(partial / tok_rows, 'expert', split_axis=0, concat_axis=0,...  9.1 us
    all_to_all x1, starting transfers between devices, on_device(): lax.all_to_all(route_here, 'expert', split_axis=0, concat_axis=0, tiled=T...  7.74 us
    all_to_all x1, waiting for transfers between devices, on_device(): lax.all_to_all(copies, 'dp', split_axis=0, concat_axis=0, tiled=True)  7.73 us
    all_to_all x1, starting transfers between devices, on_device(): lax.all_to_all(partial / tok_rows, 'expert', split_axis=0, concat_axis=0,...  6.68 us
  transfers between devices with their start and end apart: 5, of which 4 were waited for; matrix products, arithmetic and copies ran while one was open for 2% of the time, Pallas kernels for 0%

profile of v7, /device:TPU:1, one launch (start us, length us, event | category | flops | bytes accessed | tf_op | source)
XLA Modules:
  0.0 270.6 jit_solution(9266120768780358609)
XLA Ops:
  7.2 1.1 stack_reshape.3
  8.3 1.7 pad_maximum_fusion
  10.0 0.7 convert_reduce_fusion.1
  10.8 0.2 reduce_window_sum.11
  11.1 0.8 select_reduce_fusion.5
  11.9 0.3 select_reduce_fusion.3
  12.5 0.2 fusion.28
  12.8 0.8 convolution_convert_fusion.1
  13.6 2.4 copy.133
  16.0 65.2 %all_to_all.30 = bf16[32,18,2,1024]{3,2,1,0:T(2,128)(2,1)S(1)} all-to-all(bf16[32,18,2,1024]{3,2,1,0:T(2,128)(2,1)S(1)} %copy.133), channel_id=1, replica_groups=mesh['dp'=16,'expert'=32] {'expert'}, dimensions={0} | all-to-all | bytes 4718592 | tf_op jit(solution)/shard_map/all_to_all | solution.py:71
  81.2 1.4 copy-done
  83.0 1.4 slice-done.4
  84.4 2.7 reshape.210
  87.1 3.8 %fusion.8 = f32[2,384,32,18]{1,2,3,0:T(8,128)S(1)} fusion(bf16[32,18,2,1024]{3,2,1,0:T(2,128)(2,1)} %copy-done, bf16[3,2,1024,384]{3,2,1,0:T(8,128)(2,1)} %all-gather.2.cloned.1.call-done), kind=kOutput, calls=%fused_computation.12 | convolution fusion | flops 905969664 | bytes 5701632 | tf_op jit(solution)/shard_map/sced,edf->scef/dot_general | solution.py:75
  90.9 0.3 copy-done.1
  91.2 1.6 fusion.6
  92.8 0.5 copy-done.3
  93.3 2.9 %fusion = (f32[32,1024]{1,0:T(8,128)S(1)}, bf16[2,1024,32,18]{1,2,3,0:T(8,128)(2,1)}) fusion(f32[32,18,2]{0,1,2:T(8,128)S(1)} %pad.23.clone, f32[2,384,32,18]{1,2,3,0:T(8,128)S(1)} %fusion.6, f32[2,384,32,18]{1,2,3,0:T(8,128)S(1)} %fusion.8, bf16[2,384,1024,1]{2,1,0,3:T(8,128)(2,1)S(1)} %copy-done.3), kind=kOutput, calls=%fused_computation.2 | convolution fusion | flops 913309696 | bytes 7606784 | tf_op jit(solution)/shard_map/scef,efd->sced/dot_general | solution.py:79
  96.2 0.7 div.34
  97.0 6.7 %all-to-all-start.1 = ((f32[32,1,1024]{2,1,0:T(1,128)}), f32[32,1,1024]{2,1,0:T(1,128)S(1)}, u32[]{:S(2)}, u32[]{:S(2)}) async-start(f32[32,1,1024]{2,1,0:T(1,128)} %div.34), calls=%async_computation.1 | async-start | bytes 262144 | tf_op jit(solution)/shard_map/all_to_all | solution.py:86
  103.7 9.1 %all-to-all-done.1 = f32[32,1,1024]{2,1,0:T(1,128)S(1)} async-done(((f32[32,1,1024]{2,1,0:T(1,128)}), f32[32,1,1024]{2,1,0:T(1,128)S(1)}, u32[]{:S(2)}, u32[]{:S(2)}) %all-to-all-start.1) | async-done | bytes 131104 | tf_op jit(solution)/shard_map/all_to_all | solution.py:86
  112.9 0.7 broadcast_in_dim.56
  113.6 12.6 %all-to-all-start.2 = ((f32[16,1,1024]{2,1,0:T(1,128)}), f32[16,1,1024]{2,1,0:T(1,128)S(1)}, u32[]{:S(2)}, u32[]{:S(2)}) async-start(f32[16,1,1024]{2,1,0:T(1,128)} %broadcast_in_dim.56), calls=%async_computation.2 | async-start | bytes 131072 | tf_op jit(solution)/shard_map/all_to_all | solution.py:90
  126.2 7.7 %all-to-all-done.2 = f32[16,1,1024]{2,1,0:T(1,128)S(1)} async-done(((f32[16,1,1024]{2,1,0:T(1,128)}), f32[16,1,1024]{2,1,0:T(1,128)S(1)}, u32[]{:S(2)}, u32[]{:S(2)}) %all-to-all-start.2) | async-done | bytes 65568 | tf_op jit(solution)/shard_map/all_to_all | solution.py:90
  134.0 0.1 fusion.42
  134.2 1.4 broadcast_in_dim.57
  135.6 4.1 %all-to-all-start.3 = ((bf16[32,19,1024]{2,1,0:T(8,128)(2,1)}), bf16[32,19,1024]{2,1,0:T(8,128)(2,1)S(1)}, u32[]{:S(2)}, u32[]{:S(2)}) async-start(bf16[32,19,1024]{2,1,0:T(8,128)(2,1)} %broadcast_in_dim.57), calls=%async_computation.3 | async-start | bytes 3145728 | tf_op jit(solution)/shard_map/all_to_all | solution.py:96
  139.8 37.6 %all-to-all-done.3 = bf16[32,19,1024]{2,1,0:T(8,128)(2,1)S(1)} async-done(((bf16[32,19,1024]{2,1,0:T(8,128)(2,1)}), bf16[32,19,1024]{2,1,0:T(8,128)(2,1)S(1)}, u32[]{:S(2)}, u32[]{:S(2)}) %all-to-all-start.3) | async-done | bytes 1245216 | tf_op jit(solution)/shard_map/all_to_all | solution.py:96
  177.5 0.6 copy.157
  178.3 0.9 select_reduce_fusion.1
  179.2 0.6 fusion.76
  179.8 0.6 dynamic_slice.17
  180.4 0.1 constant_dynamic-slice_fusion.1
  180.6 0.7 copy.158
  181.3 1.6 fusion.46
  182.9 0.1 multiply_reduce_fusion.1
  183.1 2.6 fusion.2
  185.8 0.5 fusion.1
  186.4 0.8 copy-done.10
  187.3 4.2 %fusion.21 = f32[2,1024,32,18]{1,2,3,0:T(8,128)S(1)} fusion(bf16[3,2,1024,384]{3,2,1,0:T(8,128)(2,1)} %all-gather.2.cloned.1.call-done, f32[2,384,32,18]{1,2,3,0:T(8,128)} %fusion.2, f32[2,384,32,18]{1,2,3,0:T(8,128)} %copy-done.12, f32[2,384,32,18]{1,2,3,0:T(8,128)S(1)} %copy-done.10), kind=kOutput, calls=%fused_computation.35 | convolution fusion | flops 910393344 | bytes 11599872 | tf_op jit(solution)/shard_map/scef,edf->sced/dot_general | solution.py:145
  191.6 1.5 fusion.3
  193.2 3.8 %copy.141 = bf16[32,18,2,1024]{3,2,1,0:T(2,128)(2,1)} copy(bf16[32,18,2,1024]{3,0,1,2:T(8,128)(2,1)S(1)} %fusion.39) | data formatting | bytes 4718592 | tf_op jit(solution)/shard_map/scatter | solution.py:151
  197.0 7.7 %all-to-all-start.4 = ((bf16[32,18,2,1024]{3,2,1,0:T(2,128)(2,1)}), bf16[32,18,2,1024]{3,2,1,0:T(2,128)(2,1)S(1)}, u32[]{:S(2)}, u32[]{:S(2)}) async-start(bf16[32,18,2,1024]{3,2,1,0:T(2,128)(2,1)} %copy.141), calls=%async_computation.4 | async-start | bytes 4718592 | tf_op jit(solution)/shard_map/all_to_all | solution.py:152
  205.4 53.7 %all-to-all-done.4 = bf16[32,18,2,1024]{3,2,1,0:T(2,128)(2,1)S(1)} async-done(((bf16[32,18,2,1024]{3,2,1,0:T(2,128)(2,1)}), bf16[32,18,2,1024]{3,2,1,0:T(2,128)(2,1)S(1)}, u32[]{:S(2)}, u32[]{:S(2)}) %all-to-all-start.4) | async-done | bytes 2359328 | tf_op jit(solution)/shard_map/all_to_all | solution.py:152
  259.1 0.7 copy.151
  260.0 0.4 select_reduce_fusion.2
  260.4 0.6 select_reduce_fusion.4
  261.0 1.6 fusion.23
  (76 shorter events, 2.1 us)
Async XLA Ops:
  7.2 5.6 %copy-start.5 = (bf16[128,1024]{1,0:T(8,128)(2,1)S(1)}, bf16[128,1024]{1,0:T(8,128)(2,1)}, u32[]{:S(2)}) copy-start(bf16[128,1024]{1,0:T(8,128)(2,1)} %param.11) | copy-start | bytes 786436
  7.2 75.8 %all-gather.2.cloned.1.call-start = ((), (), s32[]{:S(2)}) async-start(), calls=%async_computation.5 | async-start | bytes 5013504 | tf_op jit(solution)/shard_map/all_gather | solution.py:51
  81.2 1.4 copy-start
  83.0 1.4 slice-start.4
  84.4 6.5 %slice-start = ((s8[4718592]{0:T(1024)(128)(4,1)}), s8[524288]{0:T(1024)(128)(4,1)S(1)}, s32[]{:S(2)}) async-start(s8[4718592]{0:T(1024)(128)(4,1)} %bitcast.152), calls=%async_computation.6 | async-start | bytes 1048576
  87.1 3.8 %slice-start.1 = ((s8[4718592]{0:T(1024)(128)(4,1)}), s8[4194304]{0:T(1024)(128)(4,1)S(1)}, s32[]{:S(2)}) async-start(s8[4718592]{0:T(1024)(128)(4,1)} %bitcast.152), calls=%async_computation.7 | async-start | bytes 8388608
  87.1 4.1 %copy-start.1 = (bf16[32,18,2,1024]{3,2,1,0:T(2,128)(2,1)S(1)}, bf16[32,18,2,1024]{3,2,1,0:T(2,128)(2,1)}, u32[]{:S(2)}) copy-start(bf16[32,18,2,1024]{3,2,1,0:T(2,128)(2,1)} %copy-done) | copy-start | bytes 7077892
  91.2 1.6 copy-start.9
  91.2 2.0 copy-start.3
  93.3 2.9 %copy-start.12 = (f32[2,384,32,18]{1,2,3,0:T(8,128)}, f32[2,384,32,18]{1,2,3,0:T(8,128)S(1)}, u32[]{:S(2)}) copy-start(f32[2,384,32,18]{1,2,3,0:T(8,128)S(1)} %fusion.6) | copy-start | bytes 5308420
  97.0 15.8 %all-to-all-start.1 = ((f32[32,1,1024]{2,1,0:T(1,128)}), f32[32,1,1024]{2,1,0:T(1,128)S(1)}, u32[]{:S(2)}, u32[]{:S(2)}) async-start(f32[32,1,1024]{2,1,0:T(1,128)} %div.34), calls=%async_computation.1 | async-start | bytes 262144 | tf_op jit(solution)/shard_map/all_to_all | solution.py:86
  113.6 20.4 %all-to-all-start.2 = ((f32[16,1,1024]{2,1,0:T(1,128)}), f32[16,1,1024]{2,1,0:T(1,128)S(1)}, u32[]{:S(2)}, u32[]{:S(2)}) async-start(f32[16,1,1024]{2,1,0:T(1,128)} %broadcast_in_dim.56), calls=%async_computation.2 | async-start | bytes 131072 | tf_op jit(solution)/shard_map/all_to_all | solution.py:90
  135.6 4.1 %copy-start.8 = (s32[512]{0:T(512)S(1)}, s32[512]{0:T(512)}, u32[]{:S(2)}) copy-start(s32[512]{0:T(512)} %param.17) | copy-start | bytes 6148
  135.6 41.8 %all-to-all-start.3 = ((bf16[32,19,1024]{2,1,0:T(8,128)(2,1)}), bf16[32,19,1024]{2,1,0:T(8,128)(2,1)S(1)}, u32[]{:S(2)}, u32[]{:S(2)}) async-start(bf16[32,19,1024]{2,1,0:T(8,128)(2,1)} %broadcast_in_dim.57), calls=%async_computation.3 | async-start | bytes 3145728 | tf_op jit(solution)/shard_map/all_to_all | solution.py:96
  179.2 1.2 copy-start.6
  179.2 3.9 %copy-start.4 = (bf16[2,384,1024,1]{2,1,0,3:T(8,128)(2,1)S(1)}, bf16[2,384,1024,1]{2,1,0,3:T(8,128)(2,1)}, u32[]{:S(2)}) copy-start(bf16[2,384,1024,1]{2,1,0,3:T(8,128)(2,1)} %reshape.210) | copy-start | bytes 4718596
  183.1 2.7 copy-start.2
  185.8 1.5 copy-start.10
  185.8 5.7 %slice-start.2 = ((s8[4718592]{0:T(1024)(128)(4,1)}), s8[524288]{0:T(1024)(128)(4,1)S(1)}, s32[]{:S(2)}) async-start(s8[4718592]{0:T(1024)(128)(4,1)} %bitcast.154), calls=%async_computation.8 | async-start | bytes 1048576
  187.3 4.2 %slice-start.3 = ((s8[4718592]{0:T(1024)(128)(4,1)}), s8[4194304]{0:T(1024)(128)(4,1)S(1)}, s32[]{:S(2)}) async-start(s8[4718592]{0:T(1024)(128)(4,1)} %bitcast.154), calls=%async_computation.9 | async-start | bytes 8388608
  187.3 4.3 %copy-start.11 = (f32[2,384,32,18]{1,2,3,0:T(8,128)S(1)}, f32[2,384,32,18]{1,2,3,0:T(8,128)}, u32[]{:S(2)}) copy-start(f32[2,384,32,18]{1,2,3,0:T(8,128)} %fusion.2) | copy-start | bytes 5308420
  197.0 62.1 %all-to-all-start.4 = ((bf16[32,18,2,1024]{3,2,1,0:T(2,128)(2,1)}), bf16[32,18,2,1024]{3,2,1,0:T(2,128)(2,1)S(1)}, u32[]{:S(2)}, u32[]{:S(2)}) async-start(bf16[32,18,2,1024]{3,2,1,0:T(2,128)(2,1)} %copy.141), calls=%async_computation.4 | async-start | bytes 4718592 | tf_op jit(solution)/shard_map/all_to_all | solution.py:152
  205.4 55.0 %copy-start.7 = (s32[128,8]{0,1:T(8,128)S(1)}, s32[128,8]{0,1:T(8,128)}, u32[]{:S(2)}) copy-start(s32[128,8]{0,1:T(8,128)} %param.12) | copy-start | bytes 12292
Sparse Core Ops, SparseCore 0:
  10.1 52.0 all-gather.1

commit v8 on v5

--- a/solution.py
+++ b/solution.py
@@ -47,11 +47,10 @@
     row_block = lax.axis_index("dp")
 
     ff_width = w_gate.shape[2]
-    stacked = jnp.stack([w_gate, w_up, w_down.reshape(w_gate.shape)])
-    every = lax.all_gather(stacked, "dp", axis=2, tiled=True)
-    gate_full = every[0]
-    up_full = every[1]
-    down_full = every[2].reshape(local_experts, ff_width, model_width)
+    stacked = jnp.concatenate([w_gate, w_up, w_down.reshape(w_gate.shape)], axis=2)
+    every = lax.all_gather(stacked, "dp", axis=1, tiled=True)
+    gate_up_full = every[:, :, : 2 * ff_width]
+    down_full = every[:, :, 2 * ff_width :].reshape(local_experts, ff_width, model_width)
 
     expert_iota = jnp.arange(experts, dtype=jnp.int32)
     matches = expert_ids[:, :, None] == expert_iota
@@ -72,8 +71,9 @@
     rows_in = arrived
     gates = jnp.swapaxes(join3(arrived[:, capacity, :, :], capacity), 1, 2)
     gates = jnp.pad(gates, ((0, 0), (0, 1), (0, 0)))
-    pre_gate = jnp.einsum("sced,edf->scef", rows_in, gate_full, preferred_element_type=f32)
-    pre_up = jnp.einsum("sced,edf->scef", rows_in, up_full, preferred_element_type=f32)
+    pre_both = jnp.einsum("sced,edf->scef", rows_in, gate_up_full, preferred_element_type=f32)
+    pre_gate = pre_both[..., :ff_width]
+    pre_up = pre_both[..., ff_width:]
     activated, derivative = silu_parts(pre_gate)
     hidden = (activated * pre_up).astype(bf16)
     expert_out = jnp.einsum("scef,efd->sced", hidden, down_full, preferred_element_type=f32).astype(
@@ -137,10 +137,9 @@
     hidden_grad = jnp.einsum("sced,efd->scef", out_grad, down_full, preferred_element_type=f32)
     gate_side = (hidden_grad * pre_up * derivative).astype(bf16)
     up_side = (hidden_grad * activated).astype(bf16)
-    route_here = jnp.einsum("scef,edf->sced", gate_side, gate_full, preferred_element_type=f32)
-    route_here = (
-        route_here
-        + jnp.einsum("scef,edf->sced", up_side, up_full, preferred_element_type=f32)
+    both_sides = jnp.concatenate([gate_side, up_side], axis=3)
+    route_here = jnp.einsum(
+        "scef,edf->sced", both_sides, gate_up_full, preferred_element_type=f32
     ).astype(bf16)
     grad_row = pack_row(jnp.swapaxes(slot_dots[:, :capacity, :], 1, 2), model_width)
     route_here = route_here.at[:, capacity, :, :].set(grad_row)

time: 261 us -> 261 us (level)
    another operation x3 -> x1, local copies, waits for them, and re-layouts: 3.87 us -> 0.05 us  [the longest x1 2.76 us: on_device(): down_full = every[2].reshape(local_experts, ff_width, model_width)]
    reshape x0 -> x2, local copies, waits for them, and re-layouts: none -> 3.8 us  [the longest x1 2.74 us: on_device(): every[:, :, 2 * ff_width:].reshape(local_experts, ff_width, model_width)]
    dot_general x4 -> x2, matrix products: 11.6 us -> 9.24 us  [the longest x1 5.07 us: on_device(): jnp.einsum('sced,edf->scef', rows_in, gate_up_full, preferred_element_typ...]
where the time goes in v8:
time: 261 us; the launch traced here: 260 us
  waiting for transfers between devices  89.4 us (34%)
  blocking collectives  77.9 us (30%)
  starting transfers between devices  24.8 us (10%)
  local copies, waits for them, and re-layouts  22.1 us (8%)
  matrix products  21.7 us (8%)
  between operations  16.2 us (6%)
  other arithmetic  8.06 us (3%)
    all_to_all x1, blocking collectives, on_device(): lax.all_to_all(outgoing, 'expert', split_axis=0, concat_axis=0, tiled=True)  65.2 us
    all_to_all x1, waiting for transfers between devices, on_device(): lax.all_to_all(route_here, 'expert', split_axis=0, concat_axis=0, tiled=T...  53.5 us
    all_to_all x1, waiting for transfers between devices, on_device(): lax.all_to_all(spread, 'dp', split_axis=0, concat_axis=0, tiled=True)  26.8 us
    all_to_all x1, starting transfers between devices, on_device(): lax.all_to_all(spread, 'dp', split_axis=0, concat_axis=0, tiled=True)  13.9 us
    all_to_all x1, blocking collectives, on_device(): lax.all_to_all(copies, 'expert', split_axis=0, concat_axis=0, tiled=True)  12.7 us
    all_to_all x1, waiting for transfers between devices, on_device(): lax.all_to_all(partial / tok_rows, 'expert', split_axis=0, concat_axis=0,...  9.09 us
    all_to_all x1, starting transfers between devices, on_device(): lax.all_to_all(partial / tok_rows, 'expert', split_axis=0, concat_axis=0,...  6.81 us
    dot_general x1, matrix products, on_device(): jnp.einsum('sced,efd->scef', out_grad, down_full, preferred_element_type=...  5.33 us
  transfers between devices with their start and end apart: 4, of which 3 were waited for; matrix products, arithmetic and copies ran while one was open for 3% of the time, Pallas kernels for 0%

profile of v8, /device:TPU:1, one launch (start us, length us, event | category | flops | bytes accessed | tf_op | source)
XLA Modules:
  0.0 260.2 jit_solution(9211802910296661233)
XLA Ops:
  7.2 1.1 reshape.168
  8.3 1.7 pad_maximum_fusion
  10.0 0.7 convert_reduce_fusion.1
  10.8 0.2 reduce_window_sum.11
  11.1 0.8 select_reduce_fusion.5
  11.9 0.3 select_reduce_fusion.3
  12.3 0.1 copy.139
  12.5 0.2 fusion.22
  12.8 0.8 convolution_convert_fusion.1
  13.6 2.4 copy.117
  16.0 65.2 %all_to_all.30 = bf16[32,18,2,1024]{3,2,1,0:T(2,128)(2,1)S(1)} all-to-all(bf16[32,18,2,1024]{3,2,1,0:T(2,128)(2,1)S(1)} %copy.117), channel_id=1, replica_groups=mesh['dp'=16,'expert'=32] {'expert'}, dimensions={0} | all-to-all | bytes 4718592 | tf_op jit(solution)/shard_map/all_to_all | solution.py:70
  81.3 1.4 copy-done
  82.8 0.1 add_bitcast_fusion
  82.9 0.1 copy.140
  83.0 0.6 pad.23.clone
  83.6 1.4 slice-done
  85.0 2.7 %reshape.174 = bf16[2,384,1024,1]{2,1,0,3:T(8,128)(2,1)} reshape(bf16[2,1024,384]{2,1,0:T(8,128)(2,1)S(1)} %slice-done) | data formatting | bytes 3145728 | tf_op jit(solution)/shard_map/reshape | solution.py:53
  87.8 5.1 %fusion.8 = f32[32,18,2,768]{3,0,1,2:T(8,128)S(1)} fusion(bf16[32,18,2,1024]{3,2,1,0:T(2,128)(2,1)} %copy-done, bf16[2,1024,1152]{2,1,0:T(8,128)(2,1)} %all-gather.2.cloned.1.call-done), kind=kOutput, calls=%fused_computation.14 | convolution fusion | flops 1811939328 | bytes 9043968 | tf_op jit(solution)/shard_map/sced,edf->scef/dot_general | solution.py:74
  92.9 1.7 fusion
  94.6 0.7 div.31
  95.4 6.8 %all-to-all-start.1 = ((f32[32,1,1024]{2,1,0:T(1,128)}), f32[32,1,1024]{2,1,0:T(1,128)S(1)}, u32[]{:S(2)}, u32[]{:S(2)}) async-start(f32[32,1,1024]{2,1,0:T(1,128)} %div.31), calls=%async_computation.1 | async-start | bytes 262144 | tf_op jit(solution)/shard_map/all_to_all | solution.py:86
  102.3 9.1 %all-to-all-done.1 = f32[32,1,1024]{2,1,0:T(1,128)S(1)} async-done(((f32[32,1,1024]{2,1,0:T(1,128)}), f32[32,1,1024]{2,1,0:T(1,128)S(1)}, u32[]{:S(2)}, u32[]{:S(2)}) %all-to-all-start.1) | async-done | bytes 131104 | tf_op jit(solution)/shard_map/all_to_all | solution.py:86
  111.4 0.1 reduce_sum.131
  111.5 12.7 %all_to_all.31 = f32[32,1,1024]{2,1,0:T(1,128)S(1)} all-to-all(f32[32,1,1024]{2,1,0:T(1,128)S(1)} %broadcast_in_dim.56), channel_id=1, replica_groups=mesh['dp'=16,'expert'=32] {'expert'}, dimensions={0} | all-to-all | bytes 262144 | tf_op jit(solution)/shard_map/all_to_all | solution.py:89
  124.2 0.1 fusion.35
  124.5 1.1 broadcast_in_dim.57
  125.6 13.9 %all-to-all-start.3 = ((bf16[16,32,1024]{2,1,0:T(8,128)(2,1)}), bf16[16,32,1024]{2,1,0:T(8,128)(2,1)S(1)}, u32[]{:S(2)}, u32[]{:S(2)}) async-start(bf16[16,32,1024]{2,1,0:T(8,128)(2,1)} %broadcast_in_dim.57), calls=%async_computation.3 | async-start | bytes 2097152 | tf_op jit(solution)/shard_map/all_to_all | solution.py:94
  139.5 0.6 dynamic_slice.18
  140.1 0.5 iota_add_fusion
  140.6 26.8 %all-to-all-done.3 = bf16[16,32,1024]{2,1,0:T(8,128)(2,1)S(1)} async-done(((bf16[16,32,1024]{2,1,0:T(8,128)(2,1)}), bf16[16,32,1024]{2,1,0:T(8,128)(2,1)S(1)}, u32[]{:S(2)}, u32[]{:S(2)}) %all-to-all-start.3) | async-done | bytes 1048608 | tf_op jit(solution)/shard_map/all_to_all | solution.py:94
  167.4 1.5 select_reduce_fusion.1
  168.9 1.0 copy-done.9
  169.9 0.8 constant_dynamic-slice_fusion.1
  170.7 1.7 copy.137
  172.4 1.3 fusion.68
  173.8 1.7 fusion.37
  175.5 0.1 fusion.38
  175.6 5.3 %fusion.15 = (bf16[32,18,2,384]{3,0,1,2:T(8,128)(2,1)S(1)}, bf16[32,18,2,384]{3,0,1,2:T(8,128)(2,1)}) fusion(f32[32,18,2,768]{3,0,1,2:T(8,128)} %copy-done.13, f32[32,1024]{1,0:T(8,128)S(1)} %fusion.38, f32[32,18,2]{0,1,2:T(8,128)} %pad.23.clone, bf16[2,384,1024,1]{2,1,0,3:T(8,128)(2,1)} %reshape.174), kind=kOutput, calls=%fused_computation.22 | convolution fusion | flops 914079744 | bytes 7016960 | tf_op jit(solution)/shard_map/sced,efd->scef/dot_general | solution.py:137
  180.9 0.5 fusion.1
  181.6 4.2 %convert_bitcast_fusion = bf16[32,18,2,1024]{3,0,1,2:T(8,128)(2,1)S(1)} fusion(bf16[2,1024,1152]{2,1,0:T(8,128)(2,1)} %all-gather.2.cloned.1.call-done, bf16[32,18,2,384]{3,0,1,2:T(8,128)(2,1)} %get-tuple-element.30, bf16[32,18,2,384]{3,0,1,2:T(8,128)(2,1)S(1)} %get-tuple-element.29), kind=kOutput, calls=%fused_computation.10 | convolution fusion | flops 1816657920 | bytes 7274496 | tf_op jit(solution)/shard_map/scef,edf->sced/dot_general | solution.py:141
  185.9 3.8 %copy.122 = bf16[32,18,2,1024]{3,2,1,0:T(2,128)(2,1)} copy(bf16[32,18,2,1024]{3,0,1,2:T(8,128)(2,1)S(1)} %fusion.34) | data formatting | bytes 4718592 | tf_op jit(solution)/shard_map/scatter | solution.py:145
  189.7 4.1 %all-to-all-start.4 = ((bf16[32,18,2,1024]{3,2,1,0:T(2,128)(2,1)}), bf16[32,18,2,1024]{3,2,1,0:T(2,128)(2,1)S(1)}, u32[]{:S(2)}, u32[]{:S(2)}) async-start(bf16[32,18,2,1024]{3,2,1,0:T(2,128)(2,1)} %copy.122), calls=%async_computation.4 | async-start | bytes 4718592 | tf_op jit(solution)/shard_map/all_to_all | solution.py:146
  194.4 0.8 constant_dynamic-slice_fusion
  195.2 53.5 %all-to-all-done.4 = bf16[32,18,2,1024]{3,2,1,0:T(2,128)(2,1)S(1)} async-done(((bf16[32,18,2,1024]{3,2,1,0:T(2,128)(2,1)}), bf16[32,18,2,1024]{3,2,1,0:T(2,128)(2,1)S(1)}, u32[]{:S(2)}, u32[]{:S(2)}) %all-to-all-start.4) | async-done | bytes 2359328 | tf_op jit(solution)/shard_map/all_to_all | solution.py:146
  248.7 0.7 copy.131
  249.6 0.4 select_reduce_fusion.2
  250.0 0.6 select_reduce_fusion.4
  250.6 1.6 fusion.21
  (56 shorter events, 1.3 us)
Async XLA Ops:
  7.2 5.6 %copy-start.2 = (bf16[128,1024]{1,0:T(8,128)(2,1)S(1)}, bf16[128,1024]{1,0:T(8,128)(2,1)}, u32[]{:S(2)}) copy-start(bf16[128,1024]{1,0:T(8,128)(2,1)} %param.11) | copy-start | bytes 786436
  7.2 76.4 %all-gather.2.cloned.1.call-start = ((), (), s32[]{:S(2)}) async-start(), calls=%async_computation.5 | async-start | bytes 5013504 | tf_op jit(solution)/shard_map/all_gather | solution.py:51
  11.1 4.9 %copy-start.7 = (s32[64,128]{1,0:T(8,128)}, s32[64,128]{1,0:T(8,128)S(1)}, u32[]{:S(2)}) copy-start(s32[64,128]{1,0:T(8,128)S(1)} %copy.111) | copy-start | bytes 98308
  12.8 0.8 copy-start.4
  81.3 1.4 copy-start
  83.6 1.4 slice-start
  87.8 5.1 %copy-start.1 = (bf16[2,384,1024,1]{2,1,0,3:T(8,128)(2,1)S(1)}, bf16[2,384,1024,1]{2,1,0,3:T(8,128)(2,1)}, u32[]{:S(2)}) copy-start(bf16[2,384,1024,1]{2,1,0,3:T(8,128)(2,1)} %reshape.174) | copy-start | bytes 4718596
  87.8 5.1 %copy-start.11 = (f32[32,18,2]{0,1,2:T(8,128)S(1)}, f32[32,18,2]{0,1,2:T(8,128)}, u32[]{:S(2)}) copy-start(f32[32,18,2]{0,1,2:T(8,128)} %pad.23.clone) | copy-start | bytes 13828
  92.9 1.8 copy-start.13
  92.9 9.3 %copy-start.3 = (bf16[128,1024]{1,0:T(8,128)(2,1)S(1)}, bf16[128,1024]{1,0:T(8,128)(2,1)}, u32[]{:S(2)}) copy-start(bf16[128,1024]{1,0:T(8,128)(2,1)} %param.11) | copy-start | bytes 786436
  95.4 44.1 %copy-start.12 = (s32[512]{0:T(512)S(1)}, s32[512]{0:T(512)}, u32[]{:S(2)}) copy-start(s32[512]{0:T(512)} %param.17) | copy-start | bytes 6148
  95.4 16.0 %all-to-all-start.1 = ((f32[32,1,1024]{2,1,0:T(1,128)}), f32[32,1,1024]{2,1,0:T(1,128)S(1)}, u32[]{:S(2)}, u32[]{:S(2)}) async-start(f32[32,1,1024]{2,1,0:T(1,128)} %div.31), calls=%async_computation.1 | async-start | bytes 262144 | tf_op jit(solution)/shard_map/all_to_all | solution.py:86
  125.6 41.8 %all-to-all-start.3 = ((bf16[16,32,1024]{2,1,0:T(8,128)(2,1)}), bf16[16,32,1024]{2,1,0:T(8,128)(2,1)S(1)}, u32[]{:S(2)}, u32[]{:S(2)}) async-start(bf16[16,32,1024]{2,1,0:T(8,128)(2,1)} %broadcast_in_dim.57), calls=%async_computation.3 | async-start | bytes 2097152 | tf_op jit(solution)/shard_map/all_to_all | solution.py:94
  168.9 1.0 copy-start.9
  175.6 5.3 %copy-start.6 = (f32[32,1024]{1,0:T(8,128)}, f32[32,1024]{1,0:T(8,128)S(1)}, u32[]{:S(2)}) copy-start(f32[32,1024]{1,0:T(8,128)S(1)} %fusion.38) | copy-start | bytes 393220
  189.7 59.0 %all-to-all-start.4 = ((bf16[32,18,2,1024]{3,2,1,0:T(2,128)(2,1)}), bf16[32,18,2,1024]{3,2,1,0:T(2,128)(2,1)S(1)}, u32[]{:S(2)}, u32[]{:S(2)}) async-start(bf16[32,18,2,1024]{3,2,1,0:T(2,128)(2,1)} %copy.122), calls=%async_computation.4 | async-start | bytes 4718592 | tf_op jit(solution)/shard_map/all_to_all | solution.py:146
  195.2 54.4 %copy-start.8 = (s32[64,128]{1,0:T(8,128)S(1)}, s32[64,128]{1,0:T(8,128)}, u32[]{:S(2)}) copy-start(s32[64,128]{1,0:T(8,128)} %copy-done.7) | copy-start | bytes 98308
  195.2 54.8 %copy-start.10 = (s32[128,8]{0,1:T(8,128)S(1)}, s32[128,8]{0,1:T(8,128)}, u32[]{:S(2)}) copy-start(s32[128,8]{0,1:T(8,128)} %param.12) | copy-start | bytes 12292
  195.2 55.5 %copy-start.5 = (pred[64,18,128]{2,1,0:T(8,128)(4,1)S(1)}, pred[64,18,128]{2,1,0:T(8,128)(4,1)}, u32[]{:S(2)}) copy-start(pred[64,18,128]{2,1,0:T(8,128)(4,1)} %copy-done.4) | copy-start | bytes 442372
Sparse Core Ops, SparseCore 0:
  10.2 51.9 all-gather.1

commit v9 on v5

--- a/solution.py
+++ b/solution.py
@@ -33,6 +33,16 @@
     pieces = split3(values)
     pad = width - pieces.shape[-1]
     return jnp.pad(pieces, [(0, 0)] * (pieces.ndim - 1) + [(0, pad)])
+
+
+def gather_all(x, axis, n):
+    me = lax.axis_index(axis)
+    blocks = [x]
+    for k in range(1, n):
+        blocks.append(lax.ppermute(x, axis, [(p, (p - k) % n) for p in range(n)]))
+    held = jnp.stack(blocks)
+    doubled = jnp.concatenate([held, held])
+    return lax.dynamic_slice_in_dim(doubled, n - me, n, axis=0)
 
 
 def on_device(tokens, expert_ids, gate_values, w_gate, w_up, w_down, partner):
@@ -90,9 +100,7 @@
     inv_rms = lax.rsqrt(jnp.mean(pooled * pooled, axis=1) + 1e-06)
     embedding = (pooled * inv_rms[:, None]).astype(bf16)
     blocks = lax.axis_size("dp")
-    spread = jnp.broadcast_to(embedding[None], (blocks, group, model_width))
-    gathered = lax.all_to_all(spread, "dp", split_axis=0, concat_axis=0, tiled=True)
-    gathered = gathered.reshape(blocks * group, model_width)
+    gathered = gather_all(embedding, "dp", blocks).reshape(blocks * group, model_width)
     batch_size = gathered.shape[0]
 
     scores = (

time: 261 us -> 286 us (1.096)
  starting transfers between devices: 24.7 us -> 73.7 us
  waiting for transfers between devices: 89.5 us -> 74.5 us
  blocking collectives: 77.9 us -> 65.2 us
    ppermute x0 -> x15, starting transfers between devices: none -> 58.8 us  [gather_all(): blocks.append(lax.ppermute(x, axis, [(p, (p - k) % n) for p in range(n)]))]
    all_to_all x1, waiting for transfers between devices: 26.8 us -> 7.96 us  [on_device(): lax.all_to_all(copies, 'expert', split_axis=0, concat_axis=0, tiled=True)]
    all_to_all x1 -> x0, blocking collectives: 12.7 us -> none  [on_device(): lax.all_to_all(copies, 'expert', split_axis=0, concat_axis=0, tiled=True)]
    all_to_all x1, starting transfers between devices: 13.9 us -> 4.04 us  [on_device(): lax.all_to_all(copies, 'expert', split_axis=0, concat_axis=0, tiled=True)]
    ppermute x0 -> x15, waiting for transfers between devices: none -> 4.6 us  [gather_all(): blocks.append(lax.ppermute(x, axis, [(p, (p - k) % n) for p in range(n)]))]
    unnamed x54 -> x77, local copies, waits for them, and re-layouts: 4.82 us -> 6.06 us
  transfers between devices with their start and end apart: 4 -> 19, of which waited for: 3 -> 5; matrix products, arithmetic and copies ran while one was open for 3% -> 3% of each run, Pallas kernels for 0% -> 0%
where the time goes in v9:
time: 286 us; the launch traced here: 284 us
  waiting for transfers between devices  74.5 us (26%)
  starting transfers between devices  73.7 us (26%)
  blocking collectives  65.2 us (23%)
  local copies, waits for them, and re-layouts  23.3 us (8%)
  matrix products  22.8 us (8%)
  between operations  16.6 us (6%)
  other arithmetic  8.22 us (3%)
    all_to_all x1, blocking collectives, on_device(): lax.all_to_all(outgoing, 'expert', split_axis=0, concat_axis=0, tiled=True)  65.2 us
    ppermute x15, starting transfers between devices, gather_all(): blocks.append(lax.ppermute(x, axis, [(p, (p - k) % n) for p in range(n)]))  58.8 us
    all_to_all x1, waiting for transfers between devices, on_device(): lax.all_to_all(route_here, 'expert', split_axis=0, concat_axis=0, tiled=T...  52.9 us
    all_to_all x1, waiting for transfers between devices, on_device(): lax.all_to_all(partial / tok_rows, 'expert', split_axis=0, concat_axis=0,...  9.09 us
    all_to_all x1, waiting for transfers between devices, on_device(): lax.all_to_all(copies, 'expert', split_axis=0, concat_axis=0, tiled=True)  7.96 us
    all_to_all x1, starting transfers between devices, on_device(): lax.all_to_all(partial / tok_rows, 'expert', split_axis=0, concat_axis=0,...  6.68 us
    unnamed x77, local copies, waits for them, and re-layouts  6.06 us
  transfers between devices with their start and end apart: 19, of which 5 were waited for; matrix products, arithmetic and copies ran while one was open for 3% of the time, Pallas kernels for 0%

profile of v9, /device:TPU:1, one launch (start us, length us, event | category | flops | bytes accessed | tf_op | source)
XLA Modules:
  0.0 284.4 jit_solution(7074013800361802730)
XLA Ops:
  7.2 1.1 stack_reshape.3
  8.3 1.7 pad_maximum_fusion
  10.0 0.7 convert_reduce_fusion.1
  11.1 0.8 select_reduce_fusion.5
  12.8 0.8 convolution_convert_fusion.1
  13.6 2.4 copy.124
  16.0 65.2 %all_to_all.28 = bf16[32,18,2,1024]{3,2,1,0:T(2,128)(2,1)S(1)} all-to-all(bf16[32,18,2,1024]{3,2,1,0:T(2,128)(2,1)S(1)} %copy.124), channel_id=1, replica_groups=mesh['dp'=16,'expert'=32] {'expert'}, dimensions={0} | all-to-all | bytes 4718592 | tf_op jit(solution)/shard_map/all_to_all | solution.py:81
  81.3 1.4 copy-done
  83.6 1.4 slice-done.4
  85.0 2.7 reshape.181
  87.8 3.8 %fusion.8 = f32[2,384,32,18]{1,2,3,0:T(8,128)S(1)} fusion(bf16[32,18,2,1024]{3,2,1,0:T(2,128)(2,1)} %copy-done, bf16[3,2,1024,384]{3,2,1,0:T(8,128)(2,1)} %all-gather.2.cloned.1.call-done), kind=kOutput, calls=%fused_computation.12 | convolution fusion | flops 905969664 | bytes 5701632 | tf_op jit(solution)/shard_map/sced,edf->scef/dot_general | solution.py:85
  91.9 1.6 fusion.6
  93.9 1.5 fusion
  95.5 0.7 div.31
  96.2 6.7 %all-to-all-start.1 = ((f32[32,1,1024]{2,1,0:T(1,128)}), f32[32,1,1024]{2,1,0:T(1,128)S(1)}, u32[]{:S(2)}, u32[]{:S(2)}) async-start(f32[32,1,1024]{2,1,0:T(1,128)} %div.31), calls=%async_computation.1 | async-start | bytes 262144 | tf_op jit(solution)/shard_map/all_to_all | solution.py:96
  103.0 9.1 %all-to-all-done.1 = f32[32,1,1024]{2,1,0:T(1,128)S(1)} async-done(((f32[32,1,1024]{2,1,0:T(1,128)}), f32[32,1,1024]{2,1,0:T(1,128)S(1)}, u32[]{:S(2)}, u32[]{:S(2)}) %all-to-all-start.1) | async-done | bytes 131104 | tf_op jit(solution)/shard_map/all_to_all | solution.py:96
  112.9 4.0 %all-to-all-start.2 = ((f32[32,1,1024]{2,1,0:T(1,128)}), f32[32,1,1024]{2,1,0:T(1,128)S(1)}, u32[]{:S(2)}, u32[]{:S(2)}) async-start(f32[32,1,1024]{2,1,0:T(1,128)} %broadcast_in_dim.58), calls=%async_computation.2 | async-start | bytes 262144 | tf_op jit(solution)/shard_map/all_to_all | solution.py:99
  118.1 8.0 %all-to-all-done.2 = f32[32,1,1024]{2,1,0:T(1,128)S(1)} async-done(((f32[32,1,1024]{2,1,0:T(1,128)}), f32[32,1,1024]{2,1,0:T(1,128)S(1)}, u32[]{:S(2)}, u32[]{:S(2)}) %all-to-all-start.2) | async-done | bytes 131104 | tf_op jit(solution)/shard_map/all_to_all | solution.py:99
  126.3 3.5 %collective-permute-start = (bf16[32,1024]{1,0:T(8,128)(2,1)S(1)}, bf16[32,1024]{1,0:T(8,128)(2,1)S(1)}, u32[]{:S(2)}, u32[]{:S(2)}) collective-permute-start(bf16[32,1024]{1,0:T(8,128)(2,1)S(1)} %fusion.41), channel_id=1, source_target_pairs={{0,480},{32,0},{64,32},{96,64},{128,96},{160,128},{192,160},{224,1... | collective-permute-start | bytes 196616 | tf_op jit(solution)/shard_map/ppermute | solution.py:42
  129.8 10.7 %collective-permute-start.1 = (bf16[32,1024]{1,0:T(8,128)(2,1)S(1)}, bf16[32,1024]{1,0:T(8,128)(2,1)S(1)}, u32[]{:S(2)}, u32[]{:S(2)}) collective-permute-start(bf16[32,1024]{1,0:T(8,128)(2,1)S(1)} %fusion.41), channel_id=1, source_target_pairs={{0,448},{32,480},{64,0},{96,32},{128,64},{160,96},{192,128},{224,1... | collective-permute-start | bytes 196616 | tf_op jit(solution)/shard_map/ppermute | solution.py:42
  140.5 2.4 collective-permute-start.2
  142.9 2.2 collective-permute-start.3
  145.0 1.9 collective-permute-start.4
  147.1 7.7 %collective-permute-start.5 = (bf16[32,1024]{1,0:T(8,128)(2,1)S(1)}, bf16[32,1024]{1,0:T(8,128)(2,1)S(1)}, u32[]{:S(2)}, u32[]{:S(2)}) collective-permute-start(bf16[32,1024]{1,0:T(8,128)(2,1)S(1)} %fusion.41), channel_id=1, source_target_pairs={{0,320},{32,352},{64,384},{96,416},{128,448},{160,480},{192,0},{22... | collective-permute-start | bytes 196616 | tf_op jit(solution)/shard_map/ppermute | solution.py:42
  154.8 2.2 collective-permute-start.6
  157.0 7.2 %collective-permute-start.7 = (bf16[32,1024]{1,0:T(8,128)(2,1)S(1)}, bf16[32,1024]{1,0:T(8,128)(2,1)S(1)}, u32[]{:S(2)}, u32[]{:S(2)}) collective-permute-start(bf16[32,1024]{1,0:T(8,128)(2,1)S(1)} %fusion.41), channel_id=1, source_target_pairs={{0,256},{32,288},{64,320},{96,352},{128,384},{160,416},{192,448},{... | collective-permute-start | bytes 196616 | tf_op jit(solution)/shard_map/ppermute | solution.py:42
  164.2 2.3 collective-permute-start.8
  166.5 5.2 %collective-permute-start.9 = (bf16[32,1024]{1,0:T(8,128)(2,1)S(1)}, bf16[32,1024]{1,0:T(8,128)(2,1)S(1)}, u32[]{:S(2)}, u32[]{:S(2)}) collective-permute-start(bf16[32,1024]{1,0:T(8,128)(2,1)S(1)} %fusion.41), channel_id=1, source_target_pairs={{0,192},{32,224},{64,256},{96,288},{128,320},{160,352},{192,384},{... | collective-permute-start | bytes 196616 | tf_op jit(solution)/shard_map/ppermute | solution.py:42
  171.7 2.6 collective-permute-start.10
  174.3 4.6 %collective-permute-start.11 = (bf16[32,1024]{1,0:T(8,128)(2,1)S(1)}, bf16[32,1024]{1,0:T(8,128)(2,1)S(1)}, u32[]{:S(2)}, u32[]{:S(2)}) collective-permute-start(bf16[32,1024]{1,0:T(8,128)(2,1)S(1)} %fusion.41), channel_id=1, source_target_pairs={{0,128},{32,160},{64,192},{96,224},{128,256},{160,288},{192,320},{... | collective-permute-start | bytes 196616 | tf_op jit(solution)/shard_map/ppermute | solution.py:42
  178.9 2.7 collective-permute-start.12
  181.7 3.3 %collective-permute-start.13 = (bf16[32,1024]{1,0:T(8,128)(2,1)S(1)}, bf16[32,1024]{1,0:T(8,128)(2,1)S(1)}, u32[]{:S(2)}, u32[]{:S(2)}) collective-permute-start(bf16[32,1024]{1,0:T(8,128)(2,1)S(1)} %fusion.41), channel_id=1, source_target_pairs={{0,64},{32,96},{64,128},{96,160},{128,192},{160,224},{192,256},{22... | collective-permute-start | bytes 196616 | tf_op jit(solution)/shard_map/ppermute | solution.py:42
  185.6 3.1 %collective-permute-done.12 = bf16[32,1024]{1,0:T(8,128)(2,1)S(1)} collective-permute-done((bf16[32,1024]{1,0:T(8,128)(2,1)S(1)}, bf16[32,1024]{1,0:T(8,128)(2,1)S(1)}, u32[]{:S(2)}, u32[]{:S(2)}) %collective-permute-start.12) | collective-permute-done | bytes 65568 | tf_op jit(solution)/shard_map/ppermute | solution.py:42
  188.7 1.5 collective-permute-done.13
  190.6 1.5 select_reduce_fusion.1
  192.1 1.0 copy-done.10
  193.2 0.8 constant_dynamic-slice_fusion.1
  194.0 1.7 copy.147
  195.7 1.3 fusion.75
  197.1 1.7 fusion.42
  198.9 4.2 %fusion.2 = f32[2,384,32,18]{1,2,3,0:T(8,128)} fusion(f32[32,1024]{1,0:T(8,128)S(1)} %fusion.43, f32[32,18,2]{0,1,2:T(8,128)} %pad.23.clone, bf16[2,384,1024,1]{2,1,0,3:T(8,128)(2,1)} %reshape.181), kind=kOutput, calls=%fused_computation.6 | convolution fusion | flops 908328960 | bytes 3478016 | tf_op jit(solution)/shard_map/sced,efd->scef/dot_general | solution.py:145
  203.7 4.7 %fusion.21 = f32[2,1024,32,18]{1,2,3,0:T(8,128)S(1)} fusion(bf16[3,2,1024,384]{3,2,1,0:T(8,128)(2,1)} %all-gather.2.cloned.1.call-done, f32[2,384,32,18]{1,2,3,0:T(8,128)} %fusion.2, f32[2,384,32,18]{1,2,3,0:T(8,128)} %copy-done.17, f32[2,384,32,18]{1,2,3,0:T(8,128)} %copy-done.14), kind=kOutput, calls=%fused_computation.35 | convolution fusion | flops 910393344 | bytes 11599872 | tf_op jit(solution)/shard_map/scef,edf->sced/dot_general | solution.py:148
  209.0 1.5 fusion.3
  210.6 3.9 %copy.130 = bf16[32,18,2,1024]{3,2,1,0:T(2,128)(2,1)} copy(bf16[32,18,2,1024]{3,0,1,2:T(8,128)(2,1)S(1)} %fusion.39) | data formatting | bytes 4718592 | tf_op jit(solution)/shard_map/scatter | solution.py:154
  214.5 4.1 %all-to-all-start.3 = ((bf16[32,18,2,1024]{3,2,1,0:T(2,128)(2,1)}), bf16[32,18,2,1024]{3,2,1,0:T(2,128)(2,1)S(1)}, u32[]{:S(2)}, u32[]{:S(2)}) async-start(bf16[32,18,2,1024]{3,2,1,0:T(2,128)(2,1)} %copy.130), calls=%async_computation.3 | async-start | bytes 4718592 | tf_op jit(solution)/shard_map/all_to_all | solution.py:155
  219.2 0.8 constant_dynamic-slice_fusion
  220.0 52.9 %all-to-all-done.3 = bf16[32,18,2,1024]{3,2,1,0:T(2,128)(2,1)S(1)} async-done(((bf16[32,18,2,1024]{3,2,1,0:T(2,128)(2,1)}), bf16[32,18,2,1024]{3,2,1,0:T(2,128)(2,1)S(1)}, u32[]{:S(2)}, u32[]{:S(2)}) %all-to-all-start.3) | async-done | bytes 2359328 | tf_op jit(solution)/shard_map/all_to_all | solution.py:155
  274.8 1.6 fusion.23
  (137 shorter events, 9.6 us)
Async XLA Ops:
  7.2 5.6 %copy-start.3 = (bf16[128,1024]{1,0:T(8,128)(2,1)S(1)}, bf16[128,1024]{1,0:T(8,128)(2,1)}, u32[]{:S(2)}) copy-start(bf16[128,1024]{1,0:T(8,128)(2,1)} %param.11) | copy-start | bytes 786436
  7.2 76.5 %all-gather.2.cloned.1.call-start = ((), (), s32[]{:S(2)}) async-start(), calls=%async_computation.4 | async-start | bytes 5013504 | tf_op jit(solution)/shard_map/all_gather | solution.py:61
  11.1 2.5 copy-start.8
  12.8 0.8 copy-start.5
  81.3 1.4 copy-start
  83.6 1.4 slice-start.4
  85.0 6.5 %slice-start = ((s8[4718592]{0:T(1024)(128)(4,1)}), s8[524288]{0:T(1024)(128)(4,1)S(1)}, s32[]{:S(2)}) async-start(s8[4718592]{0:T(1024)(128)(4,1)} %bitcast.207), calls=%async_computation.5 | async-start | bytes 1048576
  87.7 3.8 %slice-start.1 = ((s8[4718592]{0:T(1024)(128)(4,1)}), s8[4194304]{0:T(1024)(128)(4,1)S(1)}, s32[]{:S(2)}) async-start(s8[4718592]{0:T(1024)(128)(4,1)} %bitcast.207), calls=%async_computation.6 | async-start | bytes 8388608
  87.8 4.1 %copy-start.1 = (bf16[32,18,2,1024]{3,2,1,0:T(2,128)(2,1)S(1)}, bf16[32,18,2,1024]{3,2,1,0:T(2,128)(2,1)}, u32[]{:S(2)}) copy-start(bf16[32,18,2,1024]{3,2,1,0:T(2,128)(2,1)} %copy-done) | copy-start | bytes 7077892
  91.9 1.6 copy-start.14
  91.9 2.0 copy-start.2
  91.9 2.0 copy-start.12
  93.9 1.5 copy-start.17
  93.9 9.0 %copy-start.4 = (bf16[128,1024]{1,0:T(8,128)(2,1)S(1)}, bf16[128,1024]{1,0:T(8,128)(2,1)}, u32[]{:S(2)}) copy-start(bf16[128,1024]{1,0:T(8,128)(2,1)} %param.11) | copy-start | bytes 786436
  93.9 23.0 %copy-start.13 = (s32[512]{0:T(512)S(1)}, s32[512]{0:T(512)}, u32[]{:S(2)}) copy-start(s32[512]{0:T(512)} %param.17) | copy-start | bytes 6148
  96.2 15.8 %all-to-all-start.1 = ((f32[32,1,1024]{2,1,0:T(1,128)}), f32[32,1,1024]{2,1,0:T(1,128)S(1)}, u32[]{:S(2)}, u32[]{:S(2)}) async-start(f32[32,1,1024]{2,1,0:T(1,128)} %div.31), calls=%async_computation.1 | async-start | bytes 262144 | tf_op jit(solution)/shard_map/all_to_all | solution.py:96
  112.9 13.2 %all-to-all-start.2 = ((f32[32,1,1024]{2,1,0:T(1,128)}), f32[32,1,1024]{2,1,0:T(1,128)S(1)}, u32[]{:S(2)}, u32[]{:S(2)}) async-start(f32[32,1,1024]{2,1,0:T(1,128)} %broadcast_in_dim.58), calls=%async_computation.2 | async-start | bytes 262144 | tf_op jit(solution)/shard_map/all_to_all | solution.py:99
  126.3 20.7 %collective-permute-start = (bf16[32,1024]{1,0:T(8,128)(2,1)S(1)}, bf16[32,1024]{1,0:T(8,128)(2,1)S(1)}, u32[]{:S(2)}, u32[]{:S(2)}) collective-permute-start(bf16[32,1024]{1,0:T(8,128)(2,1)S(1)} %fusion.41), channel_id=1, source_target_pairs={{0,480},{32,0},{64,32},{96,64},{128,96},{160,128},{192,160},{224,1... | collective-permute-start | bytes 196616 | tf_op jit(solution)/shard_map/ppermute | solution.py:42
  129.8 24.9 %collective-permute-start.1 = (bf16[32,1024]{1,0:T(8,128)(2,1)S(1)}, bf16[32,1024]{1,0:T(8,128)(2,1)S(1)}, u32[]{:S(2)}, u32[]{:S(2)}) collective-permute-start(bf16[32,1024]{1,0:T(8,128)(2,1)S(1)} %fusion.41), channel_id=1, source_target_pairs={{0,448},{32,480},{64,0},{96,32},{128,64},{160,96},{192,128},{224,1... | collective-permute-start | bytes 196616 | tf_op jit(solution)/shard_map/ppermute | solution.py:42
  140.5 16.5 %collective-permute-start.2 = (bf16[32,1024]{1,0:T(8,128)(2,1)S(1)}, bf16[32,1024]{1,0:T(8,128)(2,1)S(1)}, u32[]{:S(2)}, u32[]{:S(2)}) collective-permute-start(bf16[32,1024]{1,0:T(8,128)(2,1)S(1)} %fusion.41), channel_id=1, source_target_pairs={{0,416},{32,448},{64,480},{96,0},{128,32},{160,64},{192,96},{224,1... | collective-permute-start | bytes 196616 | tf_op jit(solution)/shard_map/ppermute | solution.py:42
  142.9 21.3 %collective-permute-start.3 = (bf16[32,1024]{1,0:T(8,128)(2,1)S(1)}, bf16[32,1024]{1,0:T(8,128)(2,1)S(1)}, u32[]{:S(2)}, u32[]{:S(2)}) collective-permute-start(bf16[32,1024]{1,0:T(8,128)(2,1)S(1)} %fusion.41), channel_id=1, source_target_pairs={{0,384},{32,416},{64,448},{96,480},{128,0},{160,32},{192,64},{224,... | collective-permute-start | bytes 196616 | tf_op jit(solution)/shard_map/ppermute | solution.py:42
  145.0 21.5 %collective-permute-start.4 = (bf16[32,1024]{1,0:T(8,128)(2,1)S(1)}, bf16[32,1024]{1,0:T(8,128)(2,1)S(1)}, u32[]{:S(2)}, u32[]{:S(2)}) collective-permute-start(bf16[32,1024]{1,0:T(8,128)(2,1)S(1)} %fusion.41), channel_id=1, source_target_pairs={{0,352},{32,384},{64,416},{96,448},{128,480},{160,0},{192,32},{224... | collective-permute-start | bytes 196616 | tf_op jit(solution)/shard_map/ppermute | solution.py:42
  147.1 24.6 %collective-permute-start.5 = (bf16[32,1024]{1,0:T(8,128)(2,1)S(1)}, bf16[32,1024]{1,0:T(8,128)(2,1)S(1)}, u32[]{:S(2)}, u32[]{:S(2)}) collective-permute-start(bf16[32,1024]{1,0:T(8,128)(2,1)S(1)} %fusion.41), channel_id=1, source_target_pairs={{0,320},{32,352},{64,384},{96,416},{128,448},{160,480},{192,0},{22... | collective-permute-start | bytes 196616 | tf_op jit(solution)/shard_map/ppermute | solution.py:42
  154.8 19.5 %collective-permute-start.6 = (bf16[32,1024]{1,0:T(8,128)(2,1)S(1)}, bf16[32,1024]{1,0:T(8,128)(2,1)S(1)}, u32[]{:S(2)}, u32[]{:S(2)}) collective-permute-start(bf16[32,1024]{1,0:T(8,128)(2,1)S(1)} %fusion.41), channel_id=1, source_target_pairs={{0,288},{32,320},{64,352},{96,384},{128,416},{160,448},{192,480},{... | collective-permute-start | bytes 196616 | tf_op jit(solution)/shard_map/ppermute | solution.py:42
  157.0 21.9 %collective-permute-start.7 = (bf16[32,1024]{1,0:T(8,128)(2,1)S(1)}, bf16[32,1024]{1,0:T(8,128)(2,1)S(1)}, u32[]{:S(2)}, u32[]{:S(2)}) collective-permute-start(bf16[32,1024]{1,0:T(8,128)(2,1)S(1)} %fusion.41), channel_id=1, source_target_pairs={{0,256},{32,288},{64,320},{96,352},{128,384},{160,416},{192,448},{... | collective-permute-start | bytes 196616 | tf_op jit(solution)/shard_map/ppermute | solution.py:42
  164.2 17.5 %collective-permute-start.8 = (bf16[32,1024]{1,0:T(8,128)(2,1)S(1)}, bf16[32,1024]{1,0:T(8,128)(2,1)S(1)}, u32[]{:S(2)}, u32[]{:S(2)}) collective-permute-start(bf16[32,1024]{1,0:T(8,128)(2,1)S(1)} %fusion.41), channel_id=1, source_target_pairs={{0,224},{32,256},{64,288},{96,320},{128,352},{160,384},{192,416},{... | collective-permute-start | bytes 196616 | tf_op jit(solution)/shard_map/ppermute | solution.py:42
  166.5 18.5 %collective-permute-start.9 = (bf16[32,1024]{1,0:T(8,128)(2,1)S(1)}, bf16[32,1024]{1,0:T(8,128)(2,1)S(1)}, u32[]{:S(2)}, u32[]{:S(2)}) collective-permute-start(bf16[32,1024]{1,0:T(8,128)(2,1)S(1)} %fusion.41), channel_id=1, source_target_pairs={{0,192},{32,224},{64,256},{96,288},{128,320},{160,352},{192,384},{... | collective-permute-start | bytes 196616 | tf_op jit(solution)/shard_map/ppermute | solution.py:42
  171.7 13.9 %collective-permute-start.10 = (bf16[32,1024]{1,0:T(8,128)(2,1)S(1)}, bf16[32,1024]{1,0:T(8,128)(2,1)S(1)}, u32[]{:S(2)}, u32[]{:S(2)}) collective-permute-start(bf16[32,1024]{1,0:T(8,128)(2,1)S(1)} %fusion.41), channel_id=1, source_target_pairs={{0,160},{32,192},{64,224},{96,256},{128,288},{160,320},{192,352},{... | collective-permute-start | bytes 196616 | tf_op jit(solution)/shard_map/ppermute | solution.py:42
  174.3 11.3 %collective-permute-start.11 = (bf16[32,1024]{1,0:T(8,128)(2,1)S(1)}, bf16[32,1024]{1,0:T(8,128)(2,1)S(1)}, u32[]{:S(2)}, u32[]{:S(2)}) collective-permute-start(bf16[32,1024]{1,0:T(8,128)(2,1)S(1)} %fusion.41), channel_id=1, source_target_pairs={{0,128},{32,160},{64,192},{96,224},{128,256},{160,288},{192,320},{... | collective-permute-start | bytes 196616 | tf_op jit(solution)/shard_map/ppermute | solution.py:42
  178.9 9.8 %collective-permute-start.12 = (bf16[32,1024]{1,0:T(8,128)(2,1)S(1)}, bf16[32,1024]{1,0:T(8,128)(2,1)S(1)}, u32[]{:S(2)}, u32[]{:S(2)}) collective-permute-start(bf16[32,1024]{1,0:T(8,128)(2,1)S(1)} %fusion.41), channel_id=1, source_target_pairs={{0,96},{32,128},{64,160},{96,192},{128,224},{160,256},{192,288},{2... | collective-permute-start | bytes 196616 | tf_op jit(solution)/shard_map/ppermute | solution.py:42
  181.7 8.5 %collective-permute-start.13 = (bf16[32,1024]{1,0:T(8,128)(2,1)S(1)}, bf16[32,1024]{1,0:T(8,128)(2,1)S(1)}, u32[]{:S(2)}, u32[]{:S(2)}) collective-permute-start(bf16[32,1024]{1,0:T(8,128)(2,1)S(1)} %fusion.41), channel_id=1, source_target_pairs={{0,64},{32,96},{64,128},{96,160},{128,192},{160,224},{192,256},{22... | collective-permute-start | bytes 196616 | tf_op jit(solution)/shard_map/ppermute | solution.py:42
  185.1 5.1 %collective-permute-start.14 = (bf16[32,1024]{1,0:T(8,128)(2,1)S(1)}, bf16[32,1024]{1,0:T(8,128)(2,1)S(1)}, u32[]{:S(2)}, u32[]{:S(2)}) collective-permute-start(bf16[32,1024]{1,0:T(8,128)(2,1)S(1)} %fusion.41), channel_id=1, source_target_pairs={{0,32},{32,64},{64,96},{96,128},{128,160},{160,192},{192,224},{224... | collective-permute-start | bytes 196616 | tf_op jit(solution)/shard_map/ppermute | solution.py:42
  192.1 1.1 copy-start.10
  198.9 4.2 %copy-start.7 = (f32[32,1024]{1,0:T(8,128)}, f32[32,1024]{1,0:T(8,128)S(1)}, u32[]{:S(2)}) copy-start(f32[32,1024]{1,0:T(8,128)S(1)} %fusion.43) | copy-start | bytes 393220
  203.1 5.4 %slice-start.2 = ((s8[4718592]{0:T(1024)(128)(4,1)}), s8[524288]{0:T(1024)(128)(4,1)S(1)}, s32[]{:S(2)}) async-start(s8[4718592]{0:T(1024)(128)(4,1)} %bitcast.209), calls=%async_computation.7 | async-start | bytes 1048576
  203.7 4.8 %slice-start.3 = ((s8[4718592]{0:T(1024)(128)(4,1)}), s8[4194304]{0:T(1024)(128)(4,1)S(1)}, s32[]{:S(2)}) async-start(s8[4718592]{0:T(1024)(128)(4,1)} %bitcast.209), calls=%async_computation.8 | async-start | bytes 8388608
  203.7 4.8 %copy-start.15 = (f32[2,384,32,18]{1,2,3,0:T(8,128)S(1)}, f32[2,384,32,18]{1,2,3,0:T(8,128)}, u32[]{:S(2)}) copy-start(f32[2,384,32,18]{1,2,3,0:T(8,128)} %copy-done.14) | copy-start | bytes 5308420
  203.7 5.3 %copy-start.16 = (f32[2,384,32,18]{1,2,3,0:T(8,128)S(1)}, f32[2,384,32,18]{1,2,3,0:T(8,128)}, u32[]{:S(2)}) copy-start(f32[2,384,32,18]{1,2,3,0:T(8,128)} %fusion.2) | copy-start | bytes 5308420
  214.5 58.4 %all-to-all-start.3 = ((bf16[32,18,2,1024]{3,2,1,0:T(2,128)(2,1)}), bf16[32,18,2,1024]{3,2,1,0:T(2,128)(2,1)S(1)}, u32[]{:S(2)}, u32[]{:S(2)}) async-start(bf16[32,18,2,1024]{3,2,1,0:T(2,128)(2,1)} %copy.130), calls=%async_computation.3 | async-start | bytes 4718592 | tf_op jit(solution)/shard_map/all_to_all | solution.py:155
  220.0 53.7 %copy-start.9 = (s32[64,128]{1,0:T(8,128)S(1)}, s32[64,128]{1,0:T(8,128)}, u32[]{:S(2)}) copy-start(s32[64,128]{1,0:T(8,128)} %copy-done.8) | copy-start | bytes 98308
  220.0 54.2 %copy-start.11 = (s32[128,8]{0,1:T(8,128)S(1)}, s32[128,8]{0,1:T(8,128)}, u32[]{:S(2)}) copy-start(s32[128,8]{0,1:T(8,128)} %param.12) | copy-start | bytes 12292
  220.0 54.8 %copy-start.6 = (pred[64,18,128]{2,1,0:T(8,128)(4,1)S(1)}, pred[64,18,128]{2,1,0:T(8,128)(4,1)}, u32[]{:S(2)}) copy-start(pred[64,18,128]{2,1,0:T(8,128)(4,1)} %copy-done.5) | copy-start | bytes 442372
Sparse Core Ops, SparseCore 0:
  10.2 51.9 all-gather.1

commit v10 on v5

--- a/solution.py
+++ b/solution.py
@@ -118,8 +118,7 @@
     row_weight = jnp.where(row_others, jnp.exp(row_scores - row_totals[:, None]), 0.0) - (
         batch_iota[None, :] == row_partner[:, None]
     ).astype(f32)
-    col_scores = lax.dynamic_slice_in_dim(scores, first, group, axis=1).T
-    col_weight = jnp.where(row_others, jnp.exp(col_scores - log_total[None, :]), 0.0) - (
+    col_weight = jnp.where(row_others, jnp.exp(row_scores - log_total[None, :]), 0.0) - (
         rows[:, None] == partner[None, :]
     ).astype(f32)
     embed_grad = (

time: 261 us -> 256 us (0.981)
  local copies, waits for them, and re-layouts: 23 us -> 19.8 us
where the time goes in v10:
time: 256 us
  waiting for transfers between devices  89.5 us (35%)
  blocking collectives  77.9 us (30%)
  starting transfers between devices  24.7 us (10%)
  matrix products  20 us (8%)
  local copies, waits for them, and re-layouts  19.8 us (8%)
  between operations  16.2 us (6%)
  other arithmetic  7.35 us (3%)
    all_to_all x1, blocking collectives, on_device(): lax.all_to_all(outgoing, 'expert', split_axis=0, concat_axis=0, tiled=True)  65.2 us
    all_to_all x1, waiting for transfers between devices, on_device(): lax.all_to_all(route_here, 'expert', split_axis=0, concat_axis=0, tiled=T...  53.5 us
    all_to_all x1, waiting for transfers between devices, on_device(): lax.all_to_all(spread, 'dp', split_axis=0, concat_axis=0, tiled=True)  26.8 us
    all_to_all x1, starting transfers between devices, on_device(): lax.all_to_all(spread, 'dp', split_axis=0, concat_axis=0, tiled=True)  13.9 us
    all_to_all x1, blocking collectives, on_device(): lax.all_to_all(copies, 'expert', split_axis=0, concat_axis=0, tiled=True)  12.7 us
    all_to_all x1, waiting for transfers between devices, on_device(): lax.all_to_all(partial / tok_rows, 'expert', split_axis=0, concat_axis=0,...  9.09 us
    all_to_all x1, starting transfers between devices, on_device(): lax.all_to_all(partial / tok_rows, 'expert', split_axis=0, concat_axis=0,...  6.68 us
  transfers between devices with their start and end apart: 4, of which 3 were waited for; matrix products, arithmetic and copies ran while one was open for 3% of the time, Pallas kernels for 0%

profile of v10, /device:TPU:1, one launch (start us, length us, event | category | flops | bytes accessed | tf_op | source)
XLA Modules:
  0.0 255.5 jit_solution(67616809001957813)
XLA Ops:
  7.2 1.1 stack_reshape.3
  8.3 1.7 pad_maximum_fusion
  10.0 0.7 convert_reduce_fusion.1
  10.9 0.2 reduce_window_sum.11
  11.1 0.8 select_reduce_fusion.5
  11.9 0.3 select_reduce_fusion.3
  12.3 0.1 copy.139
  12.5 0.2 fusion.28
  12.8 0.8 convolution_convert_fusion.1
  13.6 2.4 copy.117
  16.1 65.2 %all_to_all.30 = bf16[32,18,2,1024]{3,2,1,0:T(2,128)(2,1)S(1)} all-to-all(bf16[32,18,2,1024]{3,2,1,0:T(2,128)(2,1)S(1)} %copy.117), channel_id=1, replica_groups=mesh['dp'=16,'expert'=32] {'expert'}, dimensions={0} | all-to-all | bytes 4718592 | tf_op jit(solution)/shard_map/all_to_all | solution.py:71
  81.3 1.4 copy-done
  82.8 0.1 add_bitcast_fusion
  83.0 0.6 pad.23.clone
  83.6 1.4 slice-done.4
  85.0 2.8 %reshape.167 = bf16[2,384,1024,1]{2,1,0,3:T(8,128)(2,1)} reshape(bf16[1,2,1024,384]{3,2,1,0:T(8,128)(2,1)S(1)} %slice-done.4) | data formatting | bytes 3145728 | tf_op jit(solution)/shard_map/reshape;squeeze | solution.py:54
  87.8 3.8 %fusion.8 = f32[2,384,32,18]{1,2,3,0:T(8,128)S(1)} fusion(bf16[32,18,2,1024]{3,2,1,0:T(2,128)(2,1)} %copy-done, bf16[3,2,1024,384]{3,2,1,0:T(8,128)(2,1)} %all-gather.2.cloned.1.call-done), kind=kOutput, calls=%fused_computation.12 | convolution fusion | flops 905969664 | bytes 5701632 | tf_op jit(solution)/shard_map/sced,edf->scef/dot_general | solution.py:75
  91.6 0.3 copy-done.1
  91.9 1.6 fusion.6
  93.5 0.5 copy-done.2
  94.0 1.5 fusion
  95.5 0.7 div.31
  96.2 6.7 %all-to-all-start.1 = ((f32[32,1,1024]{2,1,0:T(1,128)}), f32[32,1,1024]{2,1,0:T(1,128)S(1)}, u32[]{:S(2)}, u32[]{:S(2)}) async-start(f32[32,1,1024]{2,1,0:T(1,128)} %div.31), calls=%async_computation.1 | async-start | bytes 262144 | tf_op jit(solution)/shard_map/all_to_all | solution.py:86
  103.0 9.1 %all-to-all-done.1 = f32[32,1,1024]{2,1,0:T(1,128)S(1)} async-done(((f32[32,1,1024]{2,1,0:T(1,128)}), f32[32,1,1024]{2,1,0:T(1,128)S(1)}, u32[]{:S(2)}, u32[]{:S(2)}) %all-to-all-start.1) | async-done | bytes 131104 | tf_op jit(solution)/shard_map/all_to_all | solution.py:86
  112.3 12.7 %all_to_all.31 = f32[32,1,1024]{2,1,0:T(1,128)S(1)} all-to-all(f32[32,1,1024]{2,1,0:T(1,128)S(1)} %broadcast_in_dim.56), channel_id=1, replica_groups=mesh['dp'=16,'expert'=32] {'expert'}, dimensions={0} | all-to-all | bytes 262144 | tf_op jit(solution)/shard_map/all_to_all | solution.py:89
  125.0 0.1 fusion.40
  125.2 1.1 broadcast_in_dim.57
  126.3 13.9 %all-to-all-start.3 = ((bf16[16,32,1024]{2,1,0:T(8,128)(2,1)}), bf16[16,32,1024]{2,1,0:T(8,128)(2,1)S(1)}, u32[]{:S(2)}, u32[]{:S(2)}) async-start(bf16[16,32,1024]{2,1,0:T(8,128)(2,1)} %broadcast_in_dim.57), calls=%async_computation.3 | async-start | bytes 2097152 | tf_op jit(solution)/shard_map/all_to_all | solution.py:94
  140.2 0.6 dynamic_slice.15
  140.8 0.5 iota_add_fusion
  141.3 26.8 %all-to-all-done.3 = bf16[16,32,1024]{2,1,0:T(8,128)(2,1)S(1)} async-done(((bf16[16,32,1024]{2,1,0:T(8,128)(2,1)}), bf16[16,32,1024]{2,1,0:T(8,128)(2,1)S(1)}, u32[]{:S(2)}, u32[]{:S(2)}) %all-to-all-start.3) | async-done | bytes 1048608 | tf_op jit(solution)/shard_map/all_to_all | solution.py:94
  168.1 1.0 select_reduce_fusion.1
  169.2 0.6 fusion.74
  169.9 0.8 fusion.42
  170.7 0.1 fusion.43
  170.8 2.8 %fusion.2 = f32[2,384,32,18]{1,2,3,0:T(8,128)} fusion(f32[32,1024]{1,0:T(8,128)S(1)} %fusion.43, f32[32,18,2]{0,1,2:T(8,128)S(1)} %copy-done.13, bf16[2,384,1024,1]{2,1,0,3:T(8,128)(2,1)S(1)} %copy-done.3), kind=kOutput, calls=%fused_computation.6 | convolution fusion | flops 908328960 | bytes 3478016 | tf_op jit(solution)/shard_map/sced,efd->scef/dot_general | solution.py:136
  173.6 0.5 fusion.1
  174.3 4.7 %fusion.21 = f32[2,1024,32,18]{1,2,3,0:T(8,128)S(1)} fusion(bf16[3,2,1024,384]{3,2,1,0:T(8,128)(2,1)} %all-gather.2.cloned.1.call-done, f32[2,384,32,18]{1,2,3,0:T(8,128)} %fusion.2, f32[2,384,32,18]{1,2,3,0:T(8,128)} %copy-done.20, f32[2,384,32,18]{1,2,3,0:T(8,128)} %copy-done.17), kind=kOutput, calls=%fused_computation.35 | convolution fusion | flops 910393344 | bytes 11599872 | tf_op jit(solution)/shard_map/scef,edf->sced/dot_general | solution.py:139
  179.0 0.5 copy-done.19
  179.6 1.5 fusion.3
  181.2 3.8 %copy.122 = bf16[32,18,2,1024]{3,2,1,0:T(2,128)(2,1)} copy(bf16[32,18,2,1024]{3,0,1,2:T(8,128)(2,1)S(1)} %fusion.39) | data formatting | bytes 4718592 | tf_op jit(solution)/shard_map/scatter | solution.py:145
  185.0 4.1 %all-to-all-start.4 = ((bf16[32,18,2,1024]{3,2,1,0:T(2,128)(2,1)}), bf16[32,18,2,1024]{3,2,1,0:T(2,128)(2,1)S(1)}, u32[]{:S(2)}, u32[]{:S(2)}) async-start(bf16[32,18,2,1024]{3,2,1,0:T(2,128)(2,1)} %copy.122), calls=%async_computation.4 | async-start | bytes 4718592 | tf_op jit(solution)/shard_map/all_to_all | solution.py:146
  189.7 0.8 constant_dynamic-slice_fusion
  190.5 53.5 %all-to-all-done.4 = bf16[32,18,2,1024]{3,2,1,0:T(2,128)(2,1)S(1)} async-done(((bf16[32,18,2,1024]{3,2,1,0:T(2,128)(2,1)}), bf16[32,18,2,1024]{3,2,1,0:T(2,128)(2,1)S(1)}, u32[]{:S(2)}, u32[]{:S(2)}) %all-to-all-start.4) | async-done | bytes 2359328 | tf_op jit(solution)/shard_map/all_to_all | solution.py:146
  244.1 0.7 copy.132
  244.9 0.4 select_reduce_fusion.2
  245.3 0.6 select_reduce_fusion.4
  246.0 1.6 fusion.23
  (80 shorter events, 1.5 us)
Async XLA Ops:
  7.2 5.6 %copy-start.4 = (bf16[128,1024]{1,0:T(8,128)(2,1)S(1)}, bf16[128,1024]{1,0:T(8,128)(2,1)}, u32[]{:S(2)}) copy-start(bf16[128,1024]{1,0:T(8,128)(2,1)} %param.11) | copy-start | bytes 786436
  7.2 76.5 %all-gather.2.cloned.1.call-start = ((), (), s32[]{:S(2)}) async-start(), calls=%async_computation.5 | async-start | bytes 5013504 | tf_op jit(solution)/shard_map/all_gather | solution.py:51
  11.1 2.5 copy-start.9
  12.8 0.8 copy-start.6
  81.3 1.4 copy-start
  83.6 1.4 slice-start.4
  85.0 6.6 %slice-start = ((s8[4718592]{0:T(1024)(128)(4,1)}), s8[524288]{0:T(1024)(128)(4,1)S(1)}, s32[]{:S(2)}) async-start(s8[4718592]{0:T(1024)(128)(4,1)} %bitcast.145), calls=%async_computation.6 | async-start | bytes 1048576
  87.8 3.8 %slice-start.1 = ((s8[4718592]{0:T(1024)(128)(4,1)}), s8[4194304]{0:T(1024)(128)(4,1)S(1)}, s32[]{:S(2)}) async-start(s8[4718592]{0:T(1024)(128)(4,1)} %bitcast.145), calls=%async_computation.7 | async-start | bytes 8388608
  87.8 4.1 %copy-start.1 = (bf16[32,18,2,1024]{3,2,1,0:T(2,128)(2,1)S(1)}, bf16[32,18,2,1024]{3,2,1,0:T(2,128)(2,1)}, u32[]{:S(2)}) copy-start(bf16[32,18,2,1024]{3,2,1,0:T(2,128)(2,1)} %copy-done) | copy-start | bytes 7077892
  91.9 1.6 copy-start.17
  91.9 2.0 copy-start.2
  91.9 2.0 copy-start.12
  94.0 1.5 copy-start.20
  94.0 9.0 %copy-start.5 = (bf16[128,1024]{1,0:T(8,128)(2,1)S(1)}, bf16[128,1024]{1,0:T(8,128)(2,1)}, u32[]{:S(2)}) copy-start(bf16[128,1024]{1,0:T(8,128)(2,1)} %param.11) | copy-start | bytes 786436
  96.2 15.8 %all-to-all-start.1 = ((f32[32,1,1024]{2,1,0:T(1,128)}), f32[32,1,1024]{2,1,0:T(1,128)S(1)}, u32[]{:S(2)}, u32[]{:S(2)}) async-start(f32[32,1,1024]{2,1,0:T(1,128)} %div.31), calls=%async_computation.1 | async-start | bytes 262144 | tf_op jit(solution)/shard_map/all_to_all | solution.py:86
  125.0 15.2 %copy-start.14 = (s32[512]{0:T(512)S(1)}, s32[512]{0:T(512)}, u32[]{:S(2)}) copy-start(s32[512]{0:T(512)} %param.17) | copy-start | bytes 6148
  126.3 41.8 %all-to-all-start.3 = ((bf16[16,32,1024]{2,1,0:T(8,128)(2,1)}), bf16[16,32,1024]{2,1,0:T(8,128)(2,1)S(1)}, u32[]{:S(2)}, u32[]{:S(2)}) async-start(bf16[16,32,1024]{2,1,0:T(8,128)(2,1)} %broadcast_in_dim.57), calls=%async_computation.3 | async-start | bytes 2097152 | tf_op jit(solution)/shard_map/all_to_all | solution.py:94
  168.1 1.7 copy-start.15
  168.1 1.7 copy-start.16
  169.2 1.6 copy-start.3
  169.2 1.6 copy-start.13
  170.8 2.8 %copy-start.8 = (f32[32,1024]{1,0:T(8,128)}, f32[32,1024]{1,0:T(8,128)S(1)}, u32[]{:S(2)}) copy-start(f32[32,1024]{1,0:T(8,128)S(1)} %fusion.43) | copy-start | bytes 393220
  173.6 5.4 %slice-start.2 = ((s8[4718592]{0:T(1024)(128)(4,1)}), s8[524288]{0:T(1024)(128)(4,1)S(1)}, s32[]{:S(2)}) async-start(s8[4718592]{0:T(1024)(128)(4,1)} %bitcast.147), calls=%async_computation.8 | async-start | bytes 1048576
  174.2 4.8 %slice-start.3 = ((s8[4718592]{0:T(1024)(128)(4,1)}), s8[4194304]{0:T(1024)(128)(4,1)S(1)}, s32[]{:S(2)}) async-start(s8[4718592]{0:T(1024)(128)(4,1)} %bitcast.147), calls=%async_computation.9 | async-start | bytes 8388608
  174.2 4.8 %copy-start.18 = (f32[2,384,32,18]{1,2,3,0:T(8,128)S(1)}, f32[2,384,32,18]{1,2,3,0:T(8,128)}, u32[]{:S(2)}) copy-start(f32[2,384,32,18]{1,2,3,0:T(8,128)} %copy-done.17) | copy-start | bytes 5308420
  174.2 5.3 %copy-start.19 = (f32[2,384,32,18]{1,2,3,0:T(8,128)S(1)}, f32[2,384,32,18]{1,2,3,0:T(8,128)}, u32[]{:S(2)}) copy-start(f32[2,384,32,18]{1,2,3,0:T(8,128)} %fusion.2) | copy-start | bytes 5308420
  185.0 59.1 %all-to-all-start.4 = ((bf16[32,18,2,1024]{3,2,1,0:T(2,128)(2,1)}), bf16[32,18,2,1024]{3,2,1,0:T(2,128)(2,1)S(1)}, u32[]{:S(2)}, u32[]{:S(2)}) async-start(bf16[32,18,2,1024]{3,2,1,0:T(2,128)(2,1)} %copy.122), calls=%async_computation.4 | async-start | bytes 4718592 | tf_op jit(solution)/shard_map/all_to_all | solution.py:146
  190.5 54.4 %copy-start.10 = (s32[64,128]{1,0:T(8,128)S(1)}, s32[64,128]{1,0:T(8,128)}, u32[]{:S(2)}) copy-start(s32[64,128]{1,0:T(8,128)} %copy-done.9) | copy-start | bytes 98308
  190.5 54.8 %copy-start.11 = (s32[128,8]{0,1:T(8,128)S(1)}, s32[128,8]{0,1:T(8,128)}, u32[]{:S(2)}) copy-start(s32[128,8]{0,1:T(8,128)} %param.12) | copy-start | bytes 12292
  190.5 55.5 %copy-start.7 = (pred[64,18,128]{2,1,0:T(8,128)(4,1)S(1)}, pred[64,18,128]{2,1,0:T(8,128)(4,1)}, u32[]{:S(2)}) copy-start(pred[64,18,128]{2,1,0:T(8,128)(4,1)} %copy-done.6) | copy-start | bytes 442372
Sparse Core Ops, SparseCore 0:
  10.2 51.9 all-gather.1

commit v11 on v10

--- a/solution.py
+++ b/solution.py
@@ -64,9 +64,16 @@
     placer = jnp.pad(onehot.astype(bf16), ((0, 0), (0, 1), (0, 0)))
     slot_gate = jnp.sum(jnp.where(onehot, chosen_gate.T[:, None, :], 0.0), axis=2)
     placer = placer.reshape(group, local_experts, capacity + 1, tok_rows).transpose(0, 2, 1, 3)
-    outgoing = jnp.einsum("jcet,td->jced", placer, tokens, preferred_element_type=f32).astype(bf16)
-    gate_row = pack_row(slot_gate, model_width).reshape(group, local_experts, model_width)
-    outgoing = outgoing.at[:, capacity, :, :].set(gate_row)
+    token_of = jnp.sum(jnp.where(onehot, jnp.arange(tok_rows, dtype=jnp.int32)[None, None, :], 0), axis=2)
+    token_of = jnp.where(jnp.any(onehot, axis=2), token_of, tok_rows)
+    source_row = jnp.concatenate(
+        [token_of, tok_rows + 1 + jnp.arange(experts, dtype=jnp.int32)[:, None]], axis=1
+    )
+    source_row = source_row.reshape(group, local_experts, capacity + 1).transpose(0, 2, 1)
+    sources = jnp.concatenate(
+        [tokens, jnp.zeros((1, model_width), bf16), pack_row(slot_gate, model_width)], axis=0
+    )
+    outgoing = jnp.take(sources, source_row, axis=0, mode="clip")
 
     arrived = lax.all_to_all(outgoing, "expert", split_axis=0, concat_axis=0, tiled=True)
     rows_in = arrived

time: 256 us -> 266 us (1.039)
  local copies, waits for them, and re-layouts: 19.8 us -> 27.1 us
  other arithmetic: 7.35 us -> 10.2 us
    gather x0 -> x2, local copies, waits for them, and re-layouts: none -> 9.88 us  [on_device(): outgoing = jnp.take(sources, source_row, axis=0, mode='clip')]
  transfers between devices with their start and end apart: 4 -> 4, of which waited for: 3 -> 3; matrix products, arithmetic and copies ran while one was open for 3% -> 7% of each run, Pallas kernels for 0% -> 0%
where the time goes in v11:
time: 266 us; the launch traced here: 265 us
  waiting for transfers between devices  89.2 us (34%)
  blocking collectives  78 us (29%)
  local copies, waits for them, and re-layouts  27.1 us (10%)
  starting transfers between devices  24.9 us (9%)
  matrix products  19.4 us (7%)
  between operations  16.2 us (6%)
  other arithmetic  10.2 us (4%)
    all_to_all x1, blocking collectives, on_device(): lax.all_to_all(outgoing, 'expert', split_axis=0, concat_axis=0, tiled=True)  65.2 us
    all_to_all x1, waiting for transfers between devices, on_device(): lax.all_to_all(route_here, 'expert', split_axis=0, concat_axis=0, tiled=T...  53.5 us
    all_to_all x1, waiting for transfers between devices, on_device(): lax.all_to_all(spread, 'dp', split_axis=0, concat_axis=0, tiled=True)  26.8 us
    all_to_all x1, starting transfers between devices, on_device(): lax.all_to_all(spread, 'dp', split_axis=0, concat_axis=0, tiled=True)  13.9 us
    all_to_all x1, blocking collectives, on_device(): lax.all_to_all(copies, 'expert', split_axis=0, concat_axis=0, tiled=True)  12.7 us
    gather x2, local copies, waits for them, and re-layouts, on_device(): outgoing = jnp.take(sources, source_row, axis=0, mode='clip')  9.88 us
    all_to_all x1, waiting for transfers between devices, on_device(): lax.all_to_all(partial / tok_rows, 'expert', split_axis=0, concat_axis=0,...  8.91 us
    all_to_all x1, starting transfers between devices, on_device(): lax.all_to_all(partial / tok_rows, 'expert', split_axis=0, concat_axis=0,...  6.86 us
  transfers between devices with their start and end apart: 4, of which 3 were waited for; matrix products, arithmetic and copies ran while one was open for 7% of the time, Pallas kernels for 0%

profile of v11, /device:TPU:1, one launch (start us, length us, event | category | flops | bytes accessed | tf_op | source)
XLA Modules:
  0.0 265.2 jit_solution(9175341634050634327)
XLA Ops:
  7.2 1.1 stack_reshape.3
  8.3 1.7 pad_maximum_fusion
  10.0 0.7 convert_reduce_fusion.1
  10.9 0.2 reduce_window_sum.11
  11.1 0.8 select_reduce_fusion.6
  11.9 0.3 select_reduce_fusion.4
  12.5 1.2 select_reduce_fusion.3
  13.6 1.7 fusion.38
  15.4 0.3 copy.117
  15.7 0.2 reshape.155
  16.0 0.1 fusion.41
  16.1 5.0 %gather_fusion = bf16[1152,1024]{1,0:T(8,128)(2,1)} fusion(bf16[193,1024]{1,0:T(8,128)(2,1)S(1)} %fusion.41, s32[2048]{0:T(1024)S(1)} %pad_clamp_fusion), kind=kCustom, calls=%fused_computation | custom fusion | bytes 4723200 | tf_op jit(solution)/shard_map/jit(_take)/gather | solution.py:76
  21.1 4.9 %reshape.154 = bf16[32,18,2,1024]{3,2,1,0:T(2,128)(2,1)S(1)} reshape(bf16[1152,1024]{1,0:T(8,128)(2,1)} %gather_fusion) | data formatting | bytes 4718592 | tf_op jit(solution)/shard_map/jit(_take)/gather | solution.py:76
  26.0 65.2 %all_to_all.30 = bf16[32,18,2,1024]{3,2,1,0:T(2,128)(2,1)S(1)} all-to-all(bf16[32,18,2,1024]{3,2,1,0:T(2,128)(2,1)S(1)} %reshape.154), channel_id=1, replica_groups=mesh['dp'=16,'expert'=32] {'expert'}, dimensions={0} | all-to-all | bytes 4718592 | tf_op jit(solution)/shard_map/all_to_all | solution.py:78
  91.2 1.4 copy-done
  93.0 0.6 pad.20.clone
  93.6 1.4 slice-done.4
  95.0 2.7 %reshape.165 = bf16[2,384,1024,1]{2,1,0,3:T(8,128)(2,1)} reshape(bf16[1,2,1024,384]{3,2,1,0:T(8,128)(2,1)S(1)} %slice-done.4) | data formatting | bytes 3145728 | tf_op jit(solution)/shard_map/reshape;squeeze | solution.py:54
  97.7 3.8 %fusion.10 = f32[2,384,32,18]{1,2,3,0:T(8,128)S(1)} fusion(bf16[32,18,2,1024]{3,2,1,0:T(2,128)(2,1)} %copy-done, bf16[3,2,1024,384]{3,2,1,0:T(8,128)(2,1)} %all-gather.2.cloned.1.call-done), kind=kOutput, calls=%fused_computation.15 | convolution fusion | flops 905969664 | bytes 5701632 | tf_op jit(solution)/shard_map/sced,edf->scef/dot_general | solution.py:82
  101.5 0.3 copy-done.1
  101.9 1.6 fusion.8
  103.4 0.5 copy-done.2
  103.9 1.5 fusion
  105.4 0.7 div.31
  106.2 6.9 %all-to-all-start.1 = ((f32[32,1,1024]{2,1,0:T(1,128)}), f32[32,1,1024]{2,1,0:T(1,128)S(1)}, u32[]{:S(2)}, u32[]{:S(2)}) async-start(f32[32,1,1024]{2,1,0:T(1,128)} %div.31), calls=%async_computation.1 | async-start | bytes 262144 | tf_op jit(solution)/shard_map/all_to_all | solution.py:93
  113.1 8.9 %all-to-all-done.1 = f32[32,1,1024]{2,1,0:T(1,128)S(1)} async-done(((f32[32,1,1024]{2,1,0:T(1,128)}), f32[32,1,1024]{2,1,0:T(1,128)S(1)}, u32[]{:S(2)}, u32[]{:S(2)}) %all-to-all-start.1) | async-done | bytes 131104 | tf_op jit(solution)/shard_map/all_to_all | solution.py:93
  122.2 12.7 %all_to_all.31 = f32[32,1,1024]{2,1,0:T(1,128)S(1)} all-to-all(f32[32,1,1024]{2,1,0:T(1,128)S(1)} %broadcast_in_dim.130), channel_id=1, replica_groups=mesh['dp'=16,'expert'=32] {'expert'}, dimensions={0} | all-to-all | bytes 262144 | tf_op jit(solution)/shard_map/all_to_all | solution.py:96
  135.0 0.1 fusion.49
  135.2 1.1 broadcast_in_dim.131
  136.3 13.9 %all-to-all-start.3 = ((bf16[16,32,1024]{2,1,0:T(8,128)(2,1)}), bf16[16,32,1024]{2,1,0:T(8,128)(2,1)S(1)}, u32[]{:S(2)}, u32[]{:S(2)}) async-start(bf16[16,32,1024]{2,1,0:T(8,128)(2,1)} %broadcast_in_dim.131), calls=%async_computation.3 | async-start | bytes 2097152 | tf_op jit(solution)/shard_map/all_to_all | solution.py:101
  150.2 0.6 dynamic_slice.15
  150.8 0.5 iota_add_fusion
  151.3 26.8 %all-to-all-done.3 = bf16[16,32,1024]{2,1,0:T(8,128)(2,1)S(1)} async-done(((bf16[16,32,1024]{2,1,0:T(8,128)(2,1)}), bf16[16,32,1024]{2,1,0:T(8,128)(2,1)S(1)}, u32[]{:S(2)}, u32[]{:S(2)}) %all-to-all-start.3) | async-done | bytes 1048608 | tf_op jit(solution)/shard_map/all_to_all | solution.py:101
  178.1 1.0 select_reduce_fusion.1
  179.2 0.6 fusion.83
  179.8 0.8 fusion.51
  180.8 2.8 %fusion.4 = f32[2,384,32,18]{1,2,3,0:T(8,128)} fusion(f32[32,1024]{1,0:T(8,128)S(1)} %fusion.52, f32[32,18,2]{0,1,2:T(8,128)S(1)} %copy-done.12, bf16[2,384,1024,1]{2,1,0,3:T(8,128)(2,1)S(1)} %copy-done.3), kind=kOutput, calls=%fused_computation.9 | convolution fusion | flops 908328960 | bytes 3478016 | tf_op jit(solution)/shard_map/sced,efd->scef/dot_general | solution.py:143
  183.6 0.5 fusion.1
  184.2 4.7 %fusion.23 = f32[2,1024,32,18]{1,2,3,0:T(8,128)S(1)} fusion(bf16[3,2,1024,384]{3,2,1,0:T(8,128)(2,1)} %all-gather.2.cloned.1.call-done, f32[2,384,32,18]{1,2,3,0:T(8,128)} %fusion.4, f32[2,384,32,18]{1,2,3,0:T(8,128)} %copy-done.19, f32[2,384,32,18]{1,2,3,0:T(8,128)} %copy-done.16), kind=kOutput, calls=%fused_computation.37 | convolution fusion | flops 910393344 | bytes 11599872 | tf_op jit(solution)/shard_map/scef,edf->sced/dot_general | solution.py:146
  189.0 0.5 copy-done.18
  189.5 1.5 fusion.5
  191.1 3.8 %copy.124 = bf16[32,18,2,1024]{3,2,1,0:T(2,128)(2,1)} copy(bf16[32,18,2,1024]{3,0,1,2:T(8,128)(2,1)S(1)} %fusion.48) | data formatting | bytes 4718592 | tf_op jit(solution)/shard_map/scatter | solution.py:152
  195.0 4.2 %all-to-all-start.4 = ((bf16[32,18,2,1024]{3,2,1,0:T(2,128)(2,1)}), bf16[32,18,2,1024]{3,2,1,0:T(2,128)(2,1)S(1)}, u32[]{:S(2)}, u32[]{:S(2)}) async-start(bf16[32,18,2,1024]{3,2,1,0:T(2,128)(2,1)} %copy.124), calls=%async_computation.4 | async-start | bytes 4718592 | tf_op jit(solution)/shard_map/all_to_all | solution.py:153
  199.9 0.8 constant_dynamic-slice_fusion
  200.7 53.5 %all-to-all-done.4 = bf16[32,18,2,1024]{3,2,1,0:T(2,128)(2,1)S(1)} async-done(((bf16[32,18,2,1024]{3,2,1,0:T(2,128)(2,1)}), bf16[32,18,2,1024]{3,2,1,0:T(2,128)(2,1)S(1)}, u32[]{:S(2)}, u32[]{:S(2)}) %all-to-all-start.4) | async-done | bytes 2359328 | tf_op jit(solution)/shard_map/all_to_all | solution.py:153
  254.4 0.4 select_reduce_fusion.2
  254.8 0.6 select_reduce_fusion.5
  255.5 1.7 fusion.30
  (85 shorter events, 2.0 us)
Async XLA Ops:
  7.2 8.8 %copy-start.4 = (bf16[128,1024]{1,0:T(8,128)(2,1)S(1)}, bf16[128,1024]{1,0:T(8,128)(2,1)}, u32[]{:S(2)}) copy-start(bf16[128,1024]{1,0:T(8,128)(2,1)} %param.9) | copy-start | bytes 786436
  7.2 86.4 %all-gather.2.cloned.1.call-start = ((), (), s32[]{:S(2)}) async-start(), calls=%async_computation.5 | async-start | bytes 5013504 | tf_op jit(solution)/shard_map/all_gather | solution.py:51
  11.1 4.2 %copy-start.6 = (s32[64,128]{1,0:T(8,128)}, s32[64,128]{1,0:T(8,128)S(1)}, u32[]{:S(2)}) copy-start(s32[64,128]{1,0:T(8,128)S(1)} %copy.113) | copy-start | bytes 98308
  91.2 1.4 copy-start
  93.6 1.4 slice-start.4
  95.0 6.5 %slice-start = ((s8[4718592]{0:T(1024)(128)(4,1)}), s8[524288]{0:T(1024)(128)(4,1)S(1)}, s32[]{:S(2)}) async-start(s8[4718592]{0:T(1024)(128)(4,1)} %bitcast.144), calls=%async_computation.6 | async-start | bytes 1048576
  97.7 3.8 %slice-start.1 = ((s8[4718592]{0:T(1024)(128)(4,1)}), s8[4194304]{0:T(1024)(128)(4,1)S(1)}, s32[]{:S(2)}) async-start(s8[4718592]{0:T(1024)(128)(4,1)} %bitcast.144), calls=%async_computation.7 | async-start | bytes 8388608
  97.7 4.1 %copy-start.1 = (bf16[32,18,2,1024]{3,2,1,0:T(2,128)(2,1)S(1)}, bf16[32,18,2,1024]{3,2,1,0:T(2,128)(2,1)}, u32[]{:S(2)}) copy-start(bf16[32,18,2,1024]{3,2,1,0:T(2,128)(2,1)} %copy-done) | copy-start | bytes 7077892
  101.9 1.6 copy-start.16
  101.9 2.0 copy-start.2
  101.9 2.0 copy-start.11
  103.9 1.5 copy-start.19
  103.9 9.1 %copy-start.5 = (bf16[128,1024]{1,0:T(8,128)(2,1)S(1)}, bf16[128,1024]{1,0:T(8,128)(2,1)}, u32[]{:S(2)}) copy-start(bf16[128,1024]{1,0:T(8,128)(2,1)} %param.9) | copy-start | bytes 786436
  106.2 15.8 %all-to-all-start.1 = ((f32[32,1,1024]{2,1,0:T(1,128)}), f32[32,1,1024]{2,1,0:T(1,128)S(1)}, u32[]{:S(2)}, u32[]{:S(2)}) async-start(f32[32,1,1024]{2,1,0:T(1,128)} %div.31), calls=%async_computation.1 | async-start | bytes 262144 | tf_op jit(solution)/shard_map/all_to_all | solution.py:93
  135.0 15.2 %copy-start.13 = (s32[512]{0:T(512)S(1)}, s32[512]{0:T(512)}, u32[]{:S(2)}) copy-start(s32[512]{0:T(512)} %param.15) | copy-start | bytes 6148
  136.3 41.8 %all-to-all-start.3 = ((bf16[16,32,1024]{2,1,0:T(8,128)(2,1)}), bf16[16,32,1024]{2,1,0:T(8,128)(2,1)S(1)}, u32[]{:S(2)}, u32[]{:S(2)}) async-start(bf16[16,32,1024]{2,1,0:T(8,128)(2,1)} %broadcast_in_dim.131), calls=%async_computation.3 | async-start | bytes 2097152 | tf_op jit(solution)/shard_map/all_to_all | solution.py:101
  178.1 1.7 copy-start.14
  178.1 1.7 copy-start.15
  179.1 1.6 copy-start.3
  179.1 1.6 copy-start.12
  180.8 2.8 %copy-start.9 = (f32[32,1024]{1,0:T(8,128)}, f32[32,1024]{1,0:T(8,128)S(1)}, u32[]{:S(2)}) copy-start(f32[32,1024]{1,0:T(8,128)S(1)} %fusion.52) | copy-start | bytes 393220
  183.6 5.4 %slice-start.2 = ((s8[4718592]{0:T(1024)(128)(4,1)}), s8[524288]{0:T(1024)(128)(4,1)S(1)}, s32[]{:S(2)}) async-start(s8[4718592]{0:T(1024)(128)(4,1)} %bitcast.146), calls=%async_computation.8 | async-start | bytes 1048576
  184.2 4.8 %slice-start.3 = ((s8[4718592]{0:T(1024)(128)(4,1)}), s8[4194304]{0:T(1024)(128)(4,1)S(1)}, s32[]{:S(2)}) async-start(s8[4718592]{0:T(1024)(128)(4,1)} %bitcast.146), calls=%async_computation.9 | async-start | bytes 8388608
  184.2 4.8 %copy-start.17 = (f32[2,384,32,18]{1,2,3,0:T(8,128)S(1)}, f32[2,384,32,18]{1,2,3,0:T(8,128)}, u32[]{:S(2)}) copy-start(f32[2,384,32,18]{1,2,3,0:T(8,128)} %copy-done.16) | copy-start | bytes 5308420
  184.2 5.3 %copy-start.18 = (f32[2,384,32,18]{1,2,3,0:T(8,128)S(1)}, f32[2,384,32,18]{1,2,3,0:T(8,128)}, u32[]{:S(2)}) copy-start(f32[2,384,32,18]{1,2,3,0:T(8,128)} %fusion.4) | copy-start | bytes 5308420
  195.0 4.2 %copy-start.8 = (pred[64,17,128]{2,1,0:T(8,128)(4,1)S(1)}, pred[64,17,128]{2,1,0:T(8,128)(4,1)}, u32[]{:S(2)}) copy-start(pred[64,17,128]{2,1,0:T(8,128)(4,1)} %get-tuple-element.17) | copy-start | bytes 417796
  195.0 59.4 %copy-start.7 = (s32[64,128]{1,0:T(8,128)S(1)}, s32[64,128]{1,0:T(8,128)}, u32[]{:S(2)}) copy-start(s32[64,128]{1,0:T(8,128)} %copy-done.6) | copy-start | bytes 98308
  195.0 59.8 %copy-start.10 = (s32[128,8]{0,1:T(8,128)S(1)}, s32[128,8]{0,1:T(8,128)}, u32[]{:S(2)}) copy-start(s32[128,8]{0,1:T(8,128)} %param.10) | copy-start | bytes 12292
  195.0 59.2 %all-to-all-start.4 = ((bf16[32,18,2,1024]{3,2,1,0:T(2,128)(2,1)}), bf16[32,18,2,1024]{3,2,1,0:T(2,128)(2,1)S(1)}, u32[]{:S(2)}, u32[]{:S(2)}) async-start(bf16[32,18,2,1024]{3,2,1,0:T(2,128)(2,1)} %copy.124), calls=%async_computation.4 | async-start | bytes 4718592 | tf_op jit(solution)/shard_map/all_to_all | solution.py:153
Sparse Core Ops, SparseCore 0:
  10.2 52.0 all-gather.1

commit v12 on v10

--- a/solution.py
+++ b/solution.py
@@ -44,11 +44,11 @@
     capacity = tok_rows * route_count // experts + max(1, tok_rows * route_count // (16 * experts))
     slot_total = experts * capacity
     me = lax.axis_index("expert")
-    row_block = lax.axis_index("dp")
+    row_block = lax.axis_index(("z", "core"))
 
     ff_width = w_gate.shape[2]
     stacked = jnp.stack([w_gate, w_up, w_down.reshape(w_gate.shape)])
-    every = lax.all_gather(stacked, "dp", axis=2, tiled=True)
+    every = lax.all_gather(stacked, ("z", "core"), axis=2, tiled=True)
     gate_full = every[0]
     up_full = every[1]
     down_full = every[2].reshape(local_experts, ff_width, model_width)
@@ -89,10 +89,14 @@
     pooled = lax.all_to_all(copies, "expert", split_axis=0, concat_axis=0, tiled=True)
     inv_rms = lax.rsqrt(jnp.mean(pooled * pooled, axis=1) + 1e-06)
     embedding = (pooled * inv_rms[:, None]).astype(bf16)
-    blocks = lax.axis_size("dp")
-    spread = jnp.broadcast_to(embedding[None], (blocks, group, model_width))
-    gathered = lax.all_to_all(spread, "dp", split_axis=0, concat_axis=0, tiled=True)
-    gathered = gathered.reshape(blocks * group, model_width)
+    chips = lax.axis_size("z")
+    cores = lax.axis_size("core")
+    spread = jnp.broadcast_to(embedding[None], (chips, group, model_width))
+    along_z = lax.all_to_all(spread, "z", split_axis=0, concat_axis=0, tiled=True)
+    pair = jnp.broadcast_to(along_z[None], (cores,) + along_z.shape)
+    both = lax.all_to_all(pair, "core", split_axis=0, concat_axis=0, tiled=True)
+    gathered = jnp.swapaxes(both, 0, 1).reshape(chips * cores * group, model_width)
+    blocks = chips * cores
     batch_size = gathered.shape[0]
 
     scores = (
@@ -155,19 +159,24 @@
 
 
 def solution(mesh):
+    chips_z = mesh.shape["dp"] // 2
+    split_mesh = jax.sharding.Mesh(
+        mesh.devices.reshape(chips_z, 2, mesh.shape["expert"]), ("z", "core", "expert")
+    )
+    rows = ("z", "core", "expert")
     placed = (
-        P(("dp", "expert"), None),
-        P(("dp", "expert"), None),
-        P(("dp", "expert"), None),
-        P("expert", "dp", None),
-        P("expert", "dp", None),
-        P("expert", "dp", None),
+        P(rows, None),
+        P(rows, None),
+        P(rows, None),
+        P("expert", ("z", "core"), None),
+        P("expert", ("z", "core"), None),
+        P("expert", ("z", "core"), None),
         P(),
     )
     return jax.shard_map(
         on_device,
-        mesh=mesh,
+        mesh=split_mesh,
         in_specs=placed,
-        out_specs=(P(), P(("dp", "expert"), None), P(("dp", "expert"), None)),
+        out_specs=(P(), P(rows, None), P(rows, None)),
         check_vma=False,
     )

time: 256 us -> 247 us (0.965)
  waiting for transfers between devices: 89.5 us -> 76.5 us
  blocking collectives: 77.9 us -> 86.8 us
  starting transfers between devices: 24.7 us -> 20.8 us
    all_to_all x1, waiting for transfers between devices: 26.8 us -> 13.7 us  [on_device(): lax.all_to_all(spread, 'z', split_axis=0, concat_axis=0, tiled=True)]
    all_to_all x0 -> x1, blocking collectives: none -> 8.9 us  [on_device(): both = lax.all_to_all(pair, 'core', split_axis=0, concat_axis=0, tiled=True)]
    all_to_all x1, starting transfers between devices: 13.9 us -> 10 us  [on_device(): lax.all_to_all(spread, 'z', split_axis=0, concat_axis=0, tiled=True)]
where the time goes in v12:
time: 247 us; the launch traced here: 245 us
  blocking collectives  86.8 us (35%)
  waiting for transfers between devices  76.5 us (31%)
  starting transfers between devices  20.8 us (8%)
  matrix products  20 us (8%)
  local copies, waits for them, and re-layouts  17.9 us (7%)
  between operations  16.2 us (7%)
  other arithmetic  6.83 us (3%)
    all_to_all x1, blocking collectives, on_device(): lax.all_to_all(outgoing, 'expert', split_axis=0, concat_axis=0, tiled=True)  65.2 us
    all_to_all x1, waiting for transfers between devices, on_device(): lax.all_to_all(route_here, 'expert', split_axis=0, concat_axis=0, tiled=T...  53.7 us
    all_to_all x1, waiting for transfers between devices, on_device(): lax.all_to_all(spread, 'z', split_axis=0, concat_axis=0, tiled=True)  13.7 us
    all_to_all x1, blocking collectives, on_device(): lax.all_to_all(copies, 'expert', split_axis=0, concat_axis=0, tiled=True)  12.7 us
    all_to_all x1, starting transfers between devices, on_device(): lax.all_to_all(spread, 'z', split_axis=0, concat_axis=0, tiled=True)  10 us
    all_to_all x1, waiting for transfers between devices, on_device(): lax.all_to_all(partial / tok_rows, 'expert', split_axis=0, concat_axis=0,...  9.1 us
    all_to_all x1, blocking collectives, on_device(): both = lax.all_to_all(pair, 'core', split_axis=0, concat_axis=0, tiled=True)  8.9 us
    all_to_all x1, starting transfers between devices, on_device(): lax.all_to_all(partial / tok_rows, 'expert', split_axis=0, concat_axis=0,...  6.67 us
  transfers between devices with their start and end apart: 4, of which 3 were waited for; matrix products, arithmetic and copies ran while one was open for 3% of the time, Pallas kernels for 0%

profile of v12, /device:TPU:1, one launch (start us, length us, event | category | flops | bytes accessed | tf_op | source)
XLA Modules:
  0.0 245.1 jit_solution(4186602295614392078)
XLA Ops:
  7.2 1.1 stack_reshape.3
  8.3 1.7 pad_maximum_fusion
  10.0 0.7 convert_reduce_fusion.1
  10.8 0.2 reduce_window_sum.11
  11.1 0.8 select_reduce_fusion.5
  11.9 0.3 select_reduce_fusion.3
  12.3 0.1 copy.145
  12.5 0.2 fusion.28
  12.8 0.8 convolution_convert_fusion.1
  13.6 2.4 copy.122
  16.0 65.2 %all_to_all.35 = bf16[32,18,2,1024]{3,2,1,0:T(2,128)(2,1)S(1)} all-to-all(bf16[32,18,2,1024]{3,2,1,0:T(2,128)(2,1)S(1)} %copy.122), channel_id=1, replica_groups=mesh['z'=8,'core'=2,'expert'=32] {'expert'}, dimensions={0} | all-to-all | bytes 4718592 | tf_op jit(solution)/shard_map/all_to_all | solution.py:71
  81.3 1.4 copy-done
  82.8 0.1 add_bitcast_fusion
  82.9 0.1 copy.146
  83.0 1.4 slice-done.4
  84.4 2.7 %reshape.168 = bf16[2,384,1024,1]{2,1,0,3:T(8,128)(2,1)} reshape(bf16[1,2,1024,384]{3,2,1,0:T(8,128)(2,1)S(1)} %slice-done.4) | data formatting | bytes 3145728 | tf_op jit(solution)/shard_map/reshape;squeeze | solution.py:54
  87.2 3.8 %fusion.8 = f32[2,384,32,18]{1,2,3,0:T(8,128)S(1)} fusion(bf16[32,18,2,1024]{3,2,1,0:T(2,128)(2,1)} %copy-done, bf16[3,2,1024,384]{3,2,1,0:T(8,128)(2,1)} %all-gather.2.cloned.1.call-done), kind=kOutput, calls=%fused_computation.12 | convolution fusion | flops 905969664 | bytes 5701632 | tf_op jit(solution)/shard_map/sced,edf->scef/dot_general | solution.py:75
  91.0 0.3 copy-done.1
  91.3 1.6 fusion.6
  92.9 0.5 copy-done.2
  93.4 1.5 fusion
  94.9 0.7 div.31
  95.6 6.7 %all-to-all-start.1 = ((f32[32,1,1024]{2,1,0:T(1,128)}), f32[32,1,1024]{2,1,0:T(1,128)S(1)}, u32[]{:S(2)}, u32[]{:S(2)}) async-start(f32[32,1,1024]{2,1,0:T(1,128)} %div.31), calls=%async_computation.1 | async-start | bytes 262144 | tf_op jit(solution)/shard_map/all_to_all | solution.py:86
  102.4 9.1 %all-to-all-done.1 = f32[32,1,1024]{2,1,0:T(1,128)S(1)} async-done(((f32[32,1,1024]{2,1,0:T(1,128)}), f32[32,1,1024]{2,1,0:T(1,128)S(1)}, u32[]{:S(2)}, u32[]{:S(2)}) %all-to-all-start.1) | async-done | bytes 131104 | tf_op jit(solution)/shard_map/all_to_all | solution.py:86
  111.4 0.1 reduce_sum.131
  111.6 12.7 %all_to_all.36 = f32[32,1,1024]{2,1,0:T(1,128)S(1)} all-to-all(f32[32,1,1024]{2,1,0:T(1,128)S(1)} %broadcast_in_dim.58), channel_id=1, replica_groups=mesh['z'=8,'core'=2,'expert'=32] {'expert'}, dimensions={0} | all-to-all | bytes 262144 | tf_op jit(solution)/shard_map/all_to_all | solution.py:89
  124.3 0.1 fusion.40
  124.6 0.9 broadcast_in_dim.59
  125.4 10.0 %all-to-all-start.3 = ((bf16[8,32,1024]{2,1,0:T(8,128)(2,1)}), bf16[8,32,1024]{2,1,0:T(8,128)(2,1)S(1)}, u32[]{:S(2)}, u32[]{:S(2)}) async-start(bf16[8,32,1024]{2,1,0:T(8,128)(2,1)} %broadcast_in_dim.59), calls=%async_computation.3 | async-start | bytes 1048576 | tf_op jit(solution)/shard_map/all_to_all | solution.py:95
  135.5 13.7 %all-to-all-done.3 = bf16[8,32,1024]{2,1,0:T(8,128)(2,1)S(1)} async-done(((bf16[8,32,1024]{2,1,0:T(8,128)(2,1)}), bf16[8,32,1024]{2,1,0:T(8,128)(2,1)S(1)}, u32[]{:S(2)}, u32[]{:S(2)}) %all-to-all-start.3) | async-done | bytes 524320 | tf_op jit(solution)/shard_map/all_to_all | solution.py:95
  149.2 0.1 broadcast_in_dim.60
  149.3 8.9 %all_to_all.37 = bf16[2,8,32,1024]{3,2,1,0:T(8,128)(2,1)S(1)} all-to-all(bf16[2,8,32,1024]{3,2,1,0:T(8,128)(2,1)S(1)} %broadcast_in_dim.60), channel_id=1, replica_groups=mesh['z'=8,'core'=2,'expert'=32] {'core'}, dimensions={0} | all-to-all | bytes 2097152 | tf_op jit(solution)/shard_map/all_to_all | solution.py:97
  158.3 1.0 select_reduce_fusion.1
  159.4 0.6 fusion.74
  160.1 0.8 fusion.42
  160.9 0.1 fusion.43
  161.0 2.8 %fusion.2 = f32[2,384,32,18]{1,2,3,0:T(8,128)} fusion(f32[32,1024]{1,0:T(8,128)S(1)} %fusion.43, f32[32,18,2]{0,1,2:T(8,128)S(1)} %pad.23.clone, bf16[2,384,1024,1]{2,1,0,3:T(8,128)(2,1)S(1)} %copy-done.3), kind=kOutput, calls=%fused_computation.6 | convolution fusion | flops 908328960 | bytes 3478016 | tf_op jit(solution)/shard_map/sced,efd->scef/dot_general | solution.py:140
  163.8 0.5 fusion.1
  164.4 4.7 %fusion.21 = f32[2,1024,32,18]{1,2,3,0:T(8,128)S(1)} fusion(bf16[3,2,1024,384]{3,2,1,0:T(8,128)(2,1)} %all-gather.2.cloned.1.call-done, f32[2,384,32,18]{1,2,3,0:T(8,128)} %fusion.2, f32[2,384,32,18]{1,2,3,0:T(8,128)} %copy-done.12, f32[2,384,32,18]{1,2,3,0:T(8,128)} %copy-done.9), kind=kOutput, calls=%fused_computation.35 | convolution fusion | flops 910393344 | bytes 11599872 | tf_op jit(solution)/shard_map/scef,edf->sced/dot_general | solution.py:143
  169.2 0.5 copy-done.11
  169.7 1.5 fusion.3
  171.3 3.8 %copy.128 = bf16[32,18,2,1024]{3,2,1,0:T(2,128)(2,1)} copy(bf16[32,18,2,1024]{3,0,1,2:T(8,128)(2,1)S(1)} %fusion.39) | data formatting | bytes 4718592 | tf_op jit(solution)/shard_map/scatter | solution.py:149
  175.2 4.1 %all-to-all-start.5 = ((bf16[32,18,2,1024]{3,2,1,0:T(2,128)(2,1)}), bf16[32,18,2,1024]{3,2,1,0:T(2,128)(2,1)S(1)}, u32[]{:S(2)}, u32[]{:S(2)}) async-start(bf16[32,18,2,1024]{3,2,1,0:T(2,128)(2,1)} %copy.128), calls=%async_computation.5 | async-start | bytes 4718592 | tf_op jit(solution)/shard_map/all_to_all | solution.py:150
  179.9 53.7 %all-to-all-done.5 = bf16[32,18,2,1024]{3,2,1,0:T(2,128)(2,1)S(1)} async-done(((bf16[32,18,2,1024]{3,2,1,0:T(2,128)(2,1)}), bf16[32,18,2,1024]{3,2,1,0:T(2,128)(2,1)S(1)}, u32[]{:S(2)}, u32[]{:S(2)}) %all-to-all-start.5) | async-done | bytes 2359328 | tf_op jit(solution)/shard_map/all_to_all | solution.py:150
  233.6 0.7 copy.138
  234.5 0.4 select_reduce_fusion.2
  234.9 0.6 select_reduce_fusion.4
  235.5 1.6 fusion.23
  (67 shorter events, 1.5 us)
Async XLA Ops:
  7.2 5.6 %copy-start.4 = (bf16[128,1024]{1,0:T(8,128)(2,1)S(1)}, bf16[128,1024]{1,0:T(8,128)(2,1)}, u32[]{:S(2)}) copy-start(bf16[128,1024]{1,0:T(8,128)(2,1)} %param.11) | copy-start | bytes 786436
  7.2 75.8 %all-gather.2.cloned.1.call-start = ((), (), s32[]{:S(2)}) async-start(), calls=%async_computation.6 | async-start | bytes 5013504 | tf_op jit(solution)/shard_map/all_gather | solution.py:51
  12.8 0.8 copy-start.5
  81.3 1.4 copy-start
  83.0 1.4 slice-start.4
  84.4 6.5 %slice-start = ((s8[4718592]{0:T(1024)(128)(4,1)}), s8[524288]{0:T(1024)(128)(4,1)S(1)}, s32[]{:S(2)}) async-start(s8[4718592]{0:T(1024)(128)(4,1)} %bitcast.147), calls=%async_computation.7 | async-start | bytes 1048576
  87.2 3.8 %slice-start.1 = ((s8[4718592]{0:T(1024)(128)(4,1)}), s8[4194304]{0:T(1024)(128)(4,1)S(1)}, s32[]{:S(2)}) async-start(s8[4718592]{0:T(1024)(128)(4,1)} %bitcast.147), calls=%async_computation.8 | async-start | bytes 8388608
  87.2 4.1 %copy-start.1 = (bf16[32,18,2,1024]{3,2,1,0:T(2,128)(2,1)S(1)}, bf16[32,18,2,1024]{3,2,1,0:T(2,128)(2,1)}, u32[]{:S(2)}) copy-start(bf16[32,18,2,1024]{3,2,1,0:T(2,128)(2,1)} %copy-done) | copy-start | bytes 7077892
  91.3 1.6 copy-start.9
  91.3 2.0 copy-start.2
  93.4 1.5 copy-start.12
  94.8 40.6 %copy-start.8 = (s32[512]{0:T(512)S(1)}, s32[512]{0:T(512)}, u32[]{:S(2)}) copy-start(s32[512]{0:T(512)} %param.17) | copy-start | bytes 6148
  95.6 15.8 %all-to-all-start.1 = ((f32[32,1,1024]{2,1,0:T(1,128)}), f32[32,1,1024]{2,1,0:T(1,128)S(1)}, u32[]{:S(2)}, u32[]{:S(2)}) async-start(f32[32,1,1024]{2,1,0:T(1,128)} %div.31), calls=%async_computation.1 | async-start | bytes 262144 | tf_op jit(solution)/shard_map/all_to_all | solution.py:86
  125.4 23.8 %all-to-all-start.3 = ((bf16[8,32,1024]{2,1,0:T(8,128)(2,1)}), bf16[8,32,1024]{2,1,0:T(8,128)(2,1)S(1)}, u32[]{:S(2)}, u32[]{:S(2)}) async-start(bf16[8,32,1024]{2,1,0:T(8,128)(2,1)} %broadcast_in_dim.59), calls=%async_computation.3 | async-start | bytes 1048576 | tf_op jit(solution)/shard_map/all_to_all | solution.py:95
  159.4 1.6 copy-start.3
  163.8 5.4 %slice-start.2 = ((s8[4718592]{0:T(1024)(128)(4,1)}), s8[524288]{0:T(1024)(128)(4,1)S(1)}, s32[]{:S(2)}) async-start(s8[4718592]{0:T(1024)(128)(4,1)} %bitcast.149), calls=%async_computation.9 | async-start | bytes 1048576
  164.4 4.8 %slice-start.3 = ((s8[4718592]{0:T(1024)(128)(4,1)}), s8[4194304]{0:T(1024)(128)(4,1)S(1)}, s32[]{:S(2)}) async-start(s8[4718592]{0:T(1024)(128)(4,1)} %bitcast.149), calls=%async_computation.10 | async-start | bytes 8388608
  164.4 4.8 %copy-start.10 = (f32[2,384,32,18]{1,2,3,0:T(8,128)S(1)}, f32[2,384,32,18]{1,2,3,0:T(8,128)}, u32[]{:S(2)}) copy-start(f32[2,384,32,18]{1,2,3,0:T(8,128)} %copy-done.9) | copy-start | bytes 5308420
  164.4 5.3 %copy-start.11 = (f32[2,384,32,18]{1,2,3,0:T(8,128)S(1)}, f32[2,384,32,18]{1,2,3,0:T(8,128)}, u32[]{:S(2)}) copy-start(f32[2,384,32,18]{1,2,3,0:T(8,128)} %fusion.2) | copy-start | bytes 5308420
  175.2 58.5 %all-to-all-start.5 = ((bf16[32,18,2,1024]{3,2,1,0:T(2,128)(2,1)}), bf16[32,18,2,1024]{3,2,1,0:T(2,128)(2,1)S(1)}, u32[]{:S(2)}, u32[]{:S(2)}) async-start(bf16[32,18,2,1024]{3,2,1,0:T(2,128)(2,1)} %copy.128), calls=%async_computation.5 | async-start | bytes 4718592 | tf_op jit(solution)/shard_map/all_to_all | solution.py:150
  179.9 55.0 %copy-start.7 = (s32[128,8]{0,1:T(8,128)S(1)}, s32[128,8]{0,1:T(8,128)}, u32[]{:S(2)}) copy-start(s32[128,8]{0,1:T(8,128)} %param.12) | copy-start | bytes 12292
  179.9 55.6 %copy-start.6 = (pred[64,18,128]{2,1,0:T(8,128)(4,1)S(1)}, pred[64,18,128]{2,1,0:T(8,128)(4,1)}, u32[]{:S(2)}) copy-start(pred[64,18,128]{2,1,0:T(8,128)(4,1)} %copy-done.5) | copy-start | bytes 442372
Sparse Core Ops, SparseCore 0:
  10.1 51.9 all-gather.1

commit v13 on v12

--- a/solution.py
+++ b/solution.py
@@ -93,8 +93,9 @@
     cores = lax.axis_size("core")
     spread = jnp.broadcast_to(embedding[None], (chips, group, model_width))
     along_z = lax.all_to_all(spread, "z", split_axis=0, concat_axis=0, tiled=True)
-    pair = jnp.broadcast_to(along_z[None], (cores,) + along_z.shape)
-    both = lax.all_to_all(pair, "core", split_axis=0, concat_axis=0, tiled=True)
+    sibling = lax.ppermute(along_z, "core", [(c, c ^ 1) for c in range(cores)])
+    low_core = lax.axis_index("core") == 0
+    both = jnp.where(low_core, jnp.stack([along_z, sibling]), jnp.stack([sibling, along_z]))
     gathered = jnp.swapaxes(both, 0, 1).reshape(chips * cores * group, model_width)
     blocks = chips * cores
     batch_size = gathered.shape[0]

time: 247 us -> 246 us (level)
  blocking collectives: 86.8 us -> 101 us
  waiting for transfers between devices: 76.5 us -> 64.4 us
  starting transfers between devices: 20.8 us -> 18.1 us
    all_to_all x1, blocking collectives: 8.9 us -> 22.8 us  [on_device(): lax.all_to_all(spread, 'z', split_axis=0, concat_axis=0, tiled=True)]
    all_to_all x1 -> x0, waiting for transfers between devices: 13.7 us -> none  [on_device(): lax.all_to_all(spread, 'z', split_axis=0, concat_axis=0, tiled=True)]
    all_to_all x1 -> x0, starting transfers between devices: 10 us -> none  [on_device(): lax.all_to_all(spread, 'z', split_axis=0, concat_axis=0, tiled=True)]
    ppermute x0 -> x1, starting transfers between devices: none -> 7.38 us  [on_device(): sibling = lax.ppermute(along_z, 'core', [(c, c ^ 1) for c in range(cores)])]
where the time goes in v13:
time: 246 us; the launch traced here: 245 us
  blocking collectives  101 us (41%)
  waiting for transfers between devices  64.4 us (26%)
  matrix products  20 us (8%)
  starting transfers between devices  18.1 us (7%)
  local copies, waits for them, and re-layouts  16.9 us (7%)
  between operations  16.2 us (7%)
  other arithmetic  8.16 us (3%)
    all_to_all x1, blocking collectives, on_device(): lax.all_to_all(outgoing, 'expert', split_axis=0, concat_axis=0, tiled=True)  65.2 us
    all_to_all x1, waiting for transfers between devices, on_device(): lax.all_to_all(route_here, 'expert', split_axis=0, concat_axis=0, tiled=T...  53.7 us
    all_to_all x1, blocking collectives, on_device(): lax.all_to_all(spread, 'z', split_axis=0, concat_axis=0, tiled=True)  22.8 us
    all_to_all x1, blocking collectives, on_device(): lax.all_to_all(copies, 'expert', split_axis=0, concat_axis=0, tiled=True)  12.7 us
    all_to_all x1, waiting for transfers between devices, on_device(): lax.all_to_all(partial / tok_rows, 'expert', split_axis=0, concat_axis=0,...  9.1 us
    ppermute x1, starting transfers between devices, on_device(): sibling = lax.ppermute(along_z, 'core', [(c, c ^ 1) for c in range(cores)])  7.38 us
    all_to_all x1, starting transfers between devices, on_device(): lax.all_to_all(partial / tok_rows, 'expert', split_axis=0, concat_axis=0,...  6.67 us
  transfers between devices with their start and end apart: 4, of which 3 were waited for; matrix products, arithmetic and copies ran while one was open for 3% of the time, Pallas kernels for 0%

profile of v13, /device:TPU:1, one launch (start us, length us, event | category | flops | bytes accessed | tf_op | source)
XLA Modules:
  0.0 244.6 jit_solution(14859158713221094206)
XLA Ops:
  7.2 1.1 stack_reshape.3
  8.3 1.7 pad_maximum_fusion
  10.0 0.7 convert_reduce_fusion.1
  10.8 0.2 reduce_window_sum.11
  11.1 0.8 select_reduce_fusion.5
  11.9 0.3 select_reduce_fusion.3
  12.3 0.1 copy.139
  12.5 0.2 fusion.28
  12.8 0.8 convolution_convert_fusion.1
  13.6 2.4 copy.117
  16.0 65.2 %all_to_all.30 = bf16[32,18,2,1024]{3,2,1,0:T(2,128)(2,1)S(1)} all-to-all(bf16[32,18,2,1024]{3,2,1,0:T(2,128)(2,1)S(1)} %copy.117), channel_id=1, replica_groups=mesh['z'=8,'core'=2,'expert'=32] {'expert'}, dimensions={0} | all-to-all | bytes 4718592 | tf_op jit(solution)/shard_map/all_to_all | solution.py:71
  81.3 1.4 copy-done
  82.7 0.1 slice_bitcast_fusion.7
  82.8 0.1 add_bitcast_fusion
  82.9 0.1 copy.140
  83.0 1.4 slice-done.4
  84.4 2.7 %reshape.167 = bf16[2,384,1024,1]{2,1,0,3:T(8,128)(2,1)} reshape(bf16[1,2,1024,384]{3,2,1,0:T(8,128)(2,1)S(1)} %slice-done.4) | data formatting | bytes 3145728 | tf_op jit(solution)/shard_map/reshape;squeeze | solution.py:54
  87.2 3.8 %fusion.8 = f32[2,384,32,18]{1,2,3,0:T(8,128)S(1)} fusion(bf16[32,18,2,1024]{3,2,1,0:T(2,128)(2,1)} %copy-done, bf16[3,2,1024,384]{3,2,1,0:T(8,128)(2,1)} %all-gather.2.cloned.1.call-done), kind=kOutput, calls=%fused_computation.12 | convolution fusion | flops 905969664 | bytes 5701632 | tf_op jit(solution)/shard_map/sced,edf->scef/dot_general | solution.py:75
  91.0 0.3 copy-done.1
  91.3 1.6 fusion.6
  92.9 0.5 copy-done.2
  93.4 1.5 fusion
  94.9 0.7 div.31
  95.6 6.7 %all-to-all-start.1 = ((f32[32,1,1024]{2,1,0:T(1,128)}), f32[32,1,1024]{2,1,0:T(1,128)S(1)}, u32[]{:S(2)}, u32[]{:S(2)}) async-start(f32[32,1,1024]{2,1,0:T(1,128)} %div.31), calls=%async_computation.1 | async-start | bytes 262144 | tf_op jit(solution)/shard_map/all_to_all | solution.py:86
  102.4 9.1 %all-to-all-done.1 = f32[32,1,1024]{2,1,0:T(1,128)S(1)} async-done(((f32[32,1,1024]{2,1,0:T(1,128)}), f32[32,1,1024]{2,1,0:T(1,128)S(1)}, u32[]{:S(2)}, u32[]{:S(2)}) %all-to-all-start.1) | async-done | bytes 131104 | tf_op jit(solution)/shard_map/all_to_all | solution.py:86
  111.4 0.1 reduce_sum.131
  111.6 12.7 %all_to_all.31 = f32[32,1,1024]{2,1,0:T(1,128)S(1)} all-to-all(f32[32,1,1024]{2,1,0:T(1,128)S(1)} %broadcast_in_dim.56), channel_id=1, replica_groups=mesh['z'=8,'core'=2,'expert'=32] {'expert'}, dimensions={0} | all-to-all | bytes 262144 | tf_op jit(solution)/shard_map/all_to_all | solution.py:89
  124.3 0.1 fusion.40
  124.6 22.8 %all_to_all.32 = bf16[8,32,1024]{2,1,0:T(8,128)(2,1)S(1)} all-to-all(bf16[8,32,1024]{2,1,0:T(8,128)(2,1)S(1)} %broadcast_in_dim.57), channel_id=1, replica_groups=mesh['z'=8,'core'=2,'expert'=32] {'z'}, dimensions={0} | all-to-all | bytes 1048576 | tf_op jit(solution)/shard_map/all_to_all | solution.py:95
  147.4 7.4 %collective-permute-start = (bf16[8,32,1024]{2,1,0:T(8,128)(2,1)S(1)}, bf16[8,32,1024]{2,1,0:T(8,128)(2,1)}, u32[]{:S(2)}, u32[]{:S(2)}) collective-permute-start(bf16[8,32,1024]{2,1,0:T(8,128)(2,1)S(1)} %all_to_all.32), channel_id=1, source_target_pairs={{0,32},{32,0},{1,33},{33,1},{2,34},{34,2},{3,35},{35,3},{4,36},{36... | collective-permute-start | bytes 1572872 | tf_op jit(solution)/shard_map/ppermute | solution.py:96
  154.9 1.5 collective-permute-done
  156.5 1.3 maximum_select_fusion
  157.8 1.0 select_reduce_fusion.1
  158.8 0.6 fusion.74
  159.5 0.8 fusion.42
  160.3 0.1 fusion.43
  160.4 2.8 %fusion.2 = f32[2,384,32,18]{1,2,3,0:T(8,128)} fusion(f32[32,1024]{1,0:T(8,128)S(1)} %fusion.43, f32[32,18,2]{0,1,2:T(8,128)S(1)} %pad.23.clone, bf16[2,384,1024,1]{2,1,0,3:T(8,128)(2,1)S(1)} %copy-done.3), kind=kOutput, calls=%fused_computation.6 | convolution fusion | flops 908328960 | bytes 3478016 | tf_op jit(solution)/shard_map/sced,efd->scef/dot_general | solution.py:141
  163.2 0.5 fusion.1
  163.9 4.7 %fusion.21 = f32[2,1024,32,18]{1,2,3,0:T(8,128)S(1)} fusion(bf16[3,2,1024,384]{3,2,1,0:T(8,128)(2,1)} %all-gather.2.cloned.1.call-done, f32[2,384,32,18]{1,2,3,0:T(8,128)} %fusion.2, f32[2,384,32,18]{1,2,3,0:T(8,128)} %copy-done.12, f32[2,384,32,18]{1,2,3,0:T(8,128)} %copy-done.9), kind=kOutput, calls=%fused_computation.35 | convolution fusion | flops 910393344 | bytes 11599872 | tf_op jit(solution)/shard_map/scef,edf->sced/dot_general | solution.py:144
  168.7 0.5 copy-done.11
  169.2 1.5 fusion.3
  170.8 3.8 %copy.122 = bf16[32,18,2,1024]{3,2,1,0:T(2,128)(2,1)} copy(bf16[32,18,2,1024]{3,0,1,2:T(8,128)(2,1)S(1)} %fusion.39) | data formatting | bytes 4718592 | tf_op jit(solution)/shard_map/scatter | solution.py:150
  174.6 4.1 %all-to-all-start.4 = ((bf16[32,18,2,1024]{3,2,1,0:T(2,128)(2,1)}), bf16[32,18,2,1024]{3,2,1,0:T(2,128)(2,1)S(1)}, u32[]{:S(2)}, u32[]{:S(2)}) async-start(bf16[32,18,2,1024]{3,2,1,0:T(2,128)(2,1)} %copy.122), calls=%async_computation.4 | async-start | bytes 4718592 | tf_op jit(solution)/shard_map/all_to_all | solution.py:151
  179.4 53.7 %all-to-all-done.4 = bf16[32,18,2,1024]{3,2,1,0:T(2,128)(2,1)S(1)} async-done(((bf16[32,18,2,1024]{3,2,1,0:T(2,128)(2,1)}), bf16[32,18,2,1024]{3,2,1,0:T(2,128)(2,1)S(1)}, u32[]{:S(2)}, u32[]{:S(2)}) %all-to-all-start.4) | async-done | bytes 2359328 | tf_op jit(solution)/shard_map/all_to_all | solution.py:151
  233.1 0.7 copy.132
  233.9 0.4 select_reduce_fusion.2
  234.3 0.6 select_reduce_fusion.4
  235.0 1.6 fusion.23
  (66 shorter events, 1.4 us)
Async XLA Ops:
  7.2 5.6 %copy-start.4 = (bf16[128,1024]{1,0:T(8,128)(2,1)S(1)}, bf16[128,1024]{1,0:T(8,128)(2,1)}, u32[]{:S(2)}) copy-start(bf16[128,1024]{1,0:T(8,128)(2,1)} %param.11) | copy-start | bytes 786436
  7.2 75.8 %all-gather.2.cloned.1.call-start = ((), (), s32[]{:S(2)}) async-start(), calls=%async_computation.5 | async-start | bytes 5013504 | tf_op jit(solution)/shard_map/all_gather | solution.py:51
  12.8 0.8 copy-start.5
  81.3 1.4 copy-start
  83.0 1.4 slice-start.4
  84.4 6.5 %slice-start = ((s8[4718592]{0:T(1024)(128)(4,1)}), s8[524288]{0:T(1024)(128)(4,1)S(1)}, s32[]{:S(2)}) async-start(s8[4718592]{0:T(1024)(128)(4,1)} %bitcast.149), calls=%async_computation.6 | async-start | bytes 1048576
  87.2 3.8 %slice-start.1 = ((s8[4718592]{0:T(1024)(128)(4,1)}), s8[4194304]{0:T(1024)(128)(4,1)S(1)}, s32[]{:S(2)}) async-start(s8[4718592]{0:T(1024)(128)(4,1)} %bitcast.149), calls=%async_computation.7 | async-start | bytes 8388608
  87.2 4.1 %copy-start.1 = (bf16[32,18,2,1024]{3,2,1,0:T(2,128)(2,1)S(1)}, bf16[32,18,2,1024]{3,2,1,0:T(2,128)(2,1)}, u32[]{:S(2)}) copy-start(bf16[32,18,2,1024]{3,2,1,0:T(2,128)(2,1)} %copy-done) | copy-start | bytes 7077892
  91.3 1.6 copy-start.9
  91.3 2.0 copy-start.2
  93.4 1.5 copy-start.12
  94.8 60.0 %copy-start.8 = (s32[512]{0:T(512)S(1)}, s32[512]{0:T(512)}, u32[]{:S(2)}) copy-start(s32[512]{0:T(512)} %param.17) | copy-start | bytes 6148
  95.6 15.8 %all-to-all-start.1 = ((f32[32,1,1024]{2,1,0:T(1,128)}), f32[32,1,1024]{2,1,0:T(1,128)S(1)}, u32[]{:S(2)}, u32[]{:S(2)}) async-start(f32[32,1,1024]{2,1,0:T(1,128)} %div.31), calls=%async_computation.1 | async-start | bytes 262144 | tf_op jit(solution)/shard_map/all_to_all | solution.py:86
  147.4 9.0 %collective-permute-start = (bf16[8,32,1024]{2,1,0:T(8,128)(2,1)S(1)}, bf16[8,32,1024]{2,1,0:T(8,128)(2,1)}, u32[]{:S(2)}, u32[]{:S(2)}) collective-permute-start(bf16[8,32,1024]{2,1,0:T(8,128)(2,1)S(1)} %all_to_all.32), channel_id=1, source_target_pairs={{0,32},{32,0},{1,33},{33,1},{2,34},{34,2},{3,35},{35,3},{4,36},{36... | collective-permute-start | bytes 1572872 | tf_op jit(solution)/shard_map/ppermute | solution.py:96
  158.8 1.6 copy-start.3
  163.2 5.4 %slice-start.2 = ((s8[4718592]{0:T(1024)(128)(4,1)}), s8[524288]{0:T(1024)(128)(4,1)S(1)}, s32[]{:S(2)}) async-start(s8[4718592]{0:T(1024)(128)(4,1)} %bitcast.151), calls=%async_computation.8 | async-start | bytes 1048576
  163.8 4.8 %slice-start.3 = ((s8[4718592]{0:T(1024)(128)(4,1)}), s8[4194304]{0:T(1024)(128)(4,1)S(1)}, s32[]{:S(2)}) async-start(s8[4718592]{0:T(1024)(128)(4,1)} %bitcast.151), calls=%async_computation.9 | async-start | bytes 8388608
  163.9 4.8 %copy-start.10 = (f32[2,384,32,18]{1,2,3,0:T(8,128)S(1)}, f32[2,384,32,18]{1,2,3,0:T(8,128)}, u32[]{:S(2)}) copy-start(f32[2,384,32,18]{1,2,3,0:T(8,128)} %copy-done.9) | copy-start | bytes 5308420
  163.9 5.3 %copy-start.11 = (f32[2,384,32,18]{1,2,3,0:T(8,128)S(1)}, f32[2,384,32,18]{1,2,3,0:T(8,128)}, u32[]{:S(2)}) copy-start(f32[2,384,32,18]{1,2,3,0:T(8,128)} %fusion.2) | copy-start | bytes 5308420
  174.6 58.5 %all-to-all-start.4 = ((bf16[32,18,2,1024]{3,2,1,0:T(2,128)(2,1)}), bf16[32,18,2,1024]{3,2,1,0:T(2,128)(2,1)S(1)}, u32[]{:S(2)}, u32[]{:S(2)}) async-start(bf16[32,18,2,1024]{3,2,1,0:T(2,128)(2,1)} %copy.122), calls=%async_computation.4 | async-start | bytes 4718592 | tf_op jit(solution)/shard_map/all_to_all | solution.py:151
  179.3 55.0 %copy-start.7 = (s32[128,8]{0,1:T(8,128)S(1)}, s32[128,8]{0,1:T(8,128)}, u32[]{:S(2)}) copy-start(s32[128,8]{0,1:T(8,128)} %param.12) | copy-start | bytes 12292
  179.4 55.6 %copy-start.6 = (pred[64,18,128]{2,1,0:T(8,128)(4,1)S(1)}, pred[64,18,128]{2,1,0:T(8,128)(4,1)}, u32[]{:S(2)}) copy-start(pred[64,18,128]{2,1,0:T(8,128)(4,1)} %copy-done.5) | copy-start | bytes 442372
Sparse Core Ops, SparseCore 0:
  10.1 51.9 all-gather.1
